TPU v7x, 32 devices: a whole 2x2x4 slice. The times are simulated.
32 devices in a mesh: chain: 2 (over x), ops: 8 (over z, y), sector: 2 (over core).
Axes of the slice: x: 2, y: 2, z: 4, core: 2. Of those that a mesh axis runs over, the one named last changes fastest.
Arguments:
- psi: bfloat16 [2, 8, 384, 384], P('chain', 'sector'), may hold values from -90 to 90
- left_ops: bfloat16 [2, 96, 8, 384, 384], P('chain', 'ops', 'sector'), may hold values from -1 to 2
- right_ops: bfloat16 [2, 96, 8, 384, 384], P('chain', 'ops', 'sector'), may hold values from -1 to 1
- basis: bfloat16 [2, 8, 384, 384], P('chain', 'sector'), may hold values from -0.3125 to 0.3125
- block_dims: int32 [2, 8], P('chain', 'sector'), may hold values from 64 to 384, as said below
Outputs:
- residual: float32 [2, 8, 384, 384], P('chain', 'sector', 'ops')
- thetas: float32 [2, 3], P('chain')
Inputs may be any that keep to these rules, and one draw needn't show every extreme that they name: `block_dims`: each is a multiple of 64; every section has a sector of exactly 384.
All inputs are finite; a program needn't handle non-finite values.
Results may differ from a plain program's by a relative error of at most 0.009.
Values may be sent and summed in bfloat16 or wider, within the bound.
No kernel may reach another device: no remote copies, remote signals or barrier semaphores. Data moves between devices by JAX's collectives and lax.ppermute only.
A program may use at most 128 MiB of HBM per device.

v0:
```python
import jax
import jax.numpy as jnp
from jax import lax
from jax.sharding import PartitionSpec as P

SECTORS = 8
ITERS = 3


def from_behind(block, axis, distance):
    devices = range(lax.axis_size(axis))
    route = [((i - distance) % len(devices), i) for i in devices]
    return lax.ppermute(block, axis, route)


def live_mask(block_dims, block_size):
    index_rows = jnp.arange(block_size, dtype=jnp.int32)
    limits = block_dims[:, :, None, None]
    inside = (index_rows[None, None, :, None] < limits) & (index_rows[None, None, None, :] < limits)
    return inside.astype(jnp.float32)


def quotient(vector_rows, sigma_rows):
    correlation, norm_sum = lax.psum(
        (jnp.sum(vector_rows * sigma_rows), jnp.sum(vector_rows * vector_rows)), ("ops", "sector")
    )
    rayleigh = correlation / norm_sum
    leftover = sigma_rows - rayleigh * vector_rows
    spread = lax.psum(jnp.sum(leftover * leftover), ("ops", "sector"))
    return (rayleigh, spread)


def on_device(psi, left_ops, right_ops, basis, block_dims):
    block_size = psi.shape[2]
    live = live_mask(block_dims, block_size)
    half_env = jnp.einsum(
        "ckqab,cqbd->ckqad", left_ops, basis, preferred_element_type=jnp.float32
    ).astype(jnp.bfloat16)
    boundary_ops = jnp.einsum(
        "cqba,ckqbd->ckqad", basis, half_env, preferred_element_type=jnp.float32
    ).astype(jnp.bfloat16)
    shifted = from_behind(boundary_ops, "chain", 1)
    vector = jnp.where(live > 0, psi, jnp.zeros_like(psi))
    entry_count = float(SECTORS * block_size * block_size)
    share_rows = block_size // lax.axis_size("ops")
    row_start = lax.axis_index("ops") * share_rows
    live_rows = lax.dynamic_slice_in_dim(live, row_start, share_rows, 2)
    residual = jnp.zeros(live_rows.shape, jnp.float32)
    quotients = []
    for iteration in range(ITERS):
        products = jnp.einsum(
            "ckqab,cqbd->ckqad", shifted, vector, preferred_element_type=jnp.float32
        ).astype(jnp.bfloat16)
        partial_sigma = jnp.einsum(
            "ckqad,ckqed->cqae", products, right_ops, preferred_element_type=jnp.float32
        )
        sigma_full = lax.psum(partial_sigma, "ops") * live
        sigma_rows = lax.dynamic_slice_in_dim(sigma_full, row_start, share_rows, 2)
        vector_rows = lax.dynamic_slice_in_dim(vector, row_start, share_rows, 2).astype(jnp.float32)
        rayleigh, spread = quotient(vector_rows, sigma_rows)
        quotients.append(rayleigh)
        if iteration + 1 < ITERS:
            residue = sigma_full - rayleigh * vector.astype(jnp.float32)
            vector = (residue * lax.rsqrt(spread / entry_count + 1e-06)).astype(jnp.bfloat16)
        else:
            residual = sigma_rows - rayleigh * vector_rows
    thetas = jnp.stack(quotients).reshape(1, ITERS)
    return (residual, thetas)


def solution(mesh):
    in_specs = (
        P("chain", "sector", None, None),
        P("chain", "ops", "sector", None, None),
        P("chain", "ops", "sector", None, None),
        P("chain", "sector", None, None),
        P("chain", "sector"),
    )
    out_specs = (P("chain", "sector", "ops", None), P("chain", None))
    return jax.shard_map(
        on_device, mesh=mesh, in_specs=in_specs, out_specs=out_specs, check_vma=False
    )
```

profile of v0, /device:TPU:0, one launch (start us, length us, event | category | flops | bytes accessed | tf_op | source)
XLA Modules:
  0.0 908.4 jit_solution(11232983917351738065)
XLA Ops:
  7.2 0.0 copy-start
  7.2 0.0 copy-start.7
  7.2 0.0 copy-start.4
  7.2 0.0 all-reduce.7.cloned.1.call-start
  7.2 1.2 copy-done
  8.4 21.1 %convert_bitcast_fusion = bf16[1,12,4,384,384]{3,4,1,2,0:T(8,128)(2,1)} fusion(bf16[1,4,384,384]{3,2,1,0:T(8,128)(2,1)S(1)} %copy-done, bf16[1,12,4,384,384]{4,3,2,1,0:T(8,128)(2,1)} %param.6), kind=kOutput, calls=%fused_computation.19 | convolution fusion | flops 10885791744 | bytes 29491200 | tf_op jit(solution)/shard_map/cqba,ckqbd->ckqad/dot_general | solution.py:39
  29.5 2.9 collective-permute-start
  32.4 0.0 copy-done.7
  32.4 0.1 iota_compare_fusion
  32.5 0.0 copy-done.4
  32.5 0.5 fusion.43
  33.0 303.8 %collective-permute-done = bf16[1,12,4,384,384]{3,4,1,2,0:T(8,128)(2,1)} collective-permute-done((bf16[1,12,4,384,384]{3,4,1,2,0:T(8,128)(2,1)}, bf16[1,12,4,384,384]{3,4,1,2,0:T(8,128)(2,1)}, u32[]{:S(2)}, u32[]{:S(2)}) %collective-permute-start) | collective-permute-done | bytes 14155808 | tf_op jit(solution)/shard_map/ppermute | solution.py:13
  336.8 20.1 %fusion.44 = f32[1,4,384,384]{3,2,1,0:T(8,128)} fusion(bf16[1,12,4,384,384]{3,4,1,2,0:T(8,128)(2,1)} %collective-permute-done, bf16[1,4,384,384]{3,2,1,0:T(8,128)(2,1)S(1)} %fusion.43, bf16[1,12,4,384,384]{4,3,2,1,0:T(8,128)(2,1)} %param.7), kind=kOutput, calls=%fused_computation.30 | convolution fusion | flops 10878713856 | bytes 31850496 | tf_op jit(solution)/shard_map/ckqad,ckqed->cqae/dot_general | solution.py:54
  356.9 0.0 all-reduce.7.cloned.1.call-update
  357.0 0.0 all-reduce.9.cloned.1.call-start
  357.0 110.3 %all-reduce.7.cloned.1.call-done = f32[1,4,384,384]{3,2,1,0:T(8,128)} async-done(((f32[1,4,384,384]{3,2,1,0:T(8,128)}), f32[1,4,384,384]{3,2,1,0:T(8,128)}) %all-reduce.7.cloned.1.call-update) | async-done | bytes 2359312 | tf_op jit(solution)/shard_map/psum | solution.py:57
  467.4 0.0 copy-start.2
  467.4 2.1 and_select_fusion.1
  469.5 0.0 copy-start.5
  469.5 1.4 copy-done.5
  470.9 0.7 fusion.74
  471.6 32.1 %all-reduce.2 = (f32[]{:T(128)}, f32[]{:T(128)}) all-reduce(f32[]{:T(128)} %get-tuple-element.7, f32[]{:T(128)} %get-tuple-element.6), channel_id=1, replica_groups=mesh['chain'=2,'ops'=8,'sector'=2] {'ops','sector'}, use_global_device_ids=true, to_apply=%region_2.3 | all-reduce | flops 2 | bytes 16 | tf_op jit(solution)/shard_map/psum | solution.py:24
  505.0 1.7 fusion.77
  506.7 30.3 %psum.80 = f32[]{:T(128)} all-reduce(f32[]{:T(128)} %fusion.77), channel_id=1, replica_groups=mesh['chain'=2,'ops'=8,'sector'=2] {'ops','sector'}, use_global_device_ids=true, to_apply=%region_6.7 | all-reduce | flops 1 | bytes 8 | tf_op jit(solution)/shard_map/psum | solution.py:29
  537.6 0.0 copy-done.2
  537.7 2.1 multiply_convert_fusion.1
  539.7 20.1 %fusion.51 = f32[1,4,384,384]{3,2,1,0:T(8,128)} fusion(bf16[1,12,4,384,384]{3,4,1,2,0:T(8,128)(2,1)} %collective-permute-done, bf16[1,4,384,384]{3,2,1,0:T(8,128)(2,1)S(1)} %multiply_convert_fusion.1, bf16[1,12,4,384,384]{4,3,2,1,0:T(8,128)(2,1)} %param.7), kind=kOutput, calls=%fused_computation.31 | convolution fusion | flops 10878713856 | bytes 31850496 | tf_op jit(solution)/shard_map/ckqad,ckqed->cqae/dot_general | solution.py:54
  559.9 0.0 all-reduce.9.cloned.1.call-update
  559.9 0.0 all-reduce.11.cloned.1.call-start
  559.9 106.1 %all-reduce.9.cloned.1.call-done = f32[1,4,384,384]{3,2,1,0:T(8,128)} async-done(((f32[1,4,384,384]{3,2,1,0:T(8,128)}), f32[1,4,384,384]{3,2,1,0:T(8,128)}) %all-reduce.9.cloned.1.call-update) | async-done | bytes 2359312 | tf_op jit(solution)/shard_map/psum | solution.py:57
  666.0 0.0 copy-start.3
  666.0 2.1 and_select_fusion
  668.1 0.0 copy-start.6
  668.1 1.4 copy-done.6
  669.6 0.7 fusion.79
  670.3 32.1 %all-reduce.1 = (f32[]{:T(128)}, f32[]{:T(128)}) all-reduce(f32[]{:T(128)} %get-tuple-element.5, f32[]{:T(128)} %get-tuple-element.4), channel_id=1, replica_groups=mesh['chain'=2,'ops'=8,'sector'=2] {'ops','sector'}, use_global_device_ids=true, to_apply=%region_9.10 | all-reduce | flops 2 | bytes 16 | tf_op jit(solution)/shard_map/psum | solution.py:24
  703.7 1.7 fusion.82
  705.3 30.1 %psum.84 = f32[]{:T(128)} all-reduce(f32[]{:T(128)} %fusion.82), channel_id=1, replica_groups=mesh['chain'=2,'ops'=8,'sector'=2] {'ops','sector'}, use_global_device_ids=true, to_apply=%region_13.14 | all-reduce | flops 1 | bytes 8 | tf_op jit(solution)/shard_map/psum | solution.py:29
  736.1 0.0 copy-done.3
  736.1 1.7 multiply_convert_fusion
  737.8 0.0 copy-start.1
  737.8 20.3 %fusion.58 = f32[1,4,384,384]{3,2,1,0:T(8,128)} fusion(bf16[1,12,4,384,384]{3,4,1,2,0:T(8,128)(2,1)} %collective-permute-done, bf16[1,4,384,384]{3,2,1,0:T(8,128)(2,1)} %multiply_convert_fusion, bf16[1,12,4,384,384]{4,3,2,1,0:T(8,128)(2,1)} %param.7), kind=kOutput, calls=%fused_computation.32 | convolution fusion | flops 10878713856 | bytes 31850496 | tf_op jit(solution)/shard_map/ckqad,ckqed->cqae/dot_general | solution.py:54
  758.1 0.0 all-reduce.11.cloned.1.call-update
  758.1 0.3 broadcast_and_fusion
  758.5 105.7 %all-reduce.11.cloned.1.call-done = f32[1,4,384,384]{3,2,1,0:T(8,128)} async-done(((f32[1,4,384,384]{3,2,1,0:T(8,128)}), f32[1,4,384,384]{3,2,1,0:T(8,128)}) %all-reduce.11.cloned.1.call-update) | async-done | bytes 2359312 | tf_op jit(solution)/shard_map/psum | solution.py:57
  864.2 1.8 fusion.84
  866.0 32.2 %all-reduce = (f32[]{:T(128)}, f32[]{:T(128)}) all-reduce(f32[]{:T(128)} %get-tuple-element.3, f32[]{:T(128)} %get-tuple-element.2), channel_id=1, replica_groups=mesh['chain'=2,'ops'=8,'sector'=2] {'ops','sector'}, use_global_device_ids=true, to_apply=%region_16.17 | all-reduce | flops 2 | bytes 16 | tf_op jit(solution)/shard_map/psum | solution.py:24
  899.5 0.6 maximum_bitcast_fusion
  900.1 1.8 fusion.85
  901.9 0.0 copy-done.1
Async XLA Ops:
  7.2 1.3 copy-start
  7.2 25.3 %copy-start.7 = (s32[1,4]{1,0:T(1,128)S(1)}, s32[1,4]{1,0:T(1,128)}, u32[]{:S(2)}) copy-start(s32[1,4]{1,0:T(1,128)} %param.9) | copy-start | bytes 52
  7.2 25.3 %copy-start.4 = (bf16[1,4,384,384]{3,2,1,0:T(8,128)(2,1)S(1)}, bf16[1,4,384,384]{3,2,1,0:T(8,128)(2,1)}, u32[]{:S(2)}) copy-start(bf16[1,4,384,384]{3,2,1,0:T(8,128)(2,1)} %param.5) | copy-start | bytes 3538948
  7.2 460.2 %all-reduce.7.cloned.1.call-start = ((), (), s32[]{:S(2)}) async-start(), calls=%async_computation | async-start | bytes 4718592 | tf_op jit(solution)/shard_map/psum | solution.py:57
  29.5 307.3 %collective-permute-start = (bf16[1,12,4,384,384]{3,4,1,2,0:T(8,128)(2,1)}, bf16[1,12,4,384,384]{3,4,1,2,0:T(8,128)(2,1)}, u32[]{:S(2)}, u32[]{:S(2)}) collective-permute-start(bf16[1,12,4,384,384]{3,4,1,2,0:T(8,128)(2,1)} %convert_bitcast_fusion), channel_id=1, source_target_pairs={{16,0},{0,16},{17,1},{1,17},{18,2},{2,18},{19,3},{3,19},{20,4},{4,... | collective-permute-start | bytes 42467336 | tf_op jit(solution)/shard_map/ppermute | solution.py:13
  357.0 309.0 %all-reduce.9.cloned.1.call-start = ((), (), s32[]{:S(2)}) async-start(), calls=%async_computation.1 | async-start | bytes 4718592 | tf_op jit(solution)/shard_map/psum | solution.py:57
  467.4 70.3 %copy-start.2 = (f32[1,4,384,384]{3,2,1,0:T(8,128)S(1)}, f32[1,4,384,384]{3,2,1,0:T(8,128)}, u32[]{:S(2)}) copy-start(f32[1,4,384,384]{3,2,1,0:T(8,128)} %all-reduce.7.cloned.1.call-done) | copy-start | bytes 7077892
  469.5 1.4 copy-start.5
  559.9 304.3 %all-reduce.11.cloned.1.call-start = ((), (), s32[]{:S(2)}) async-start(), calls=%async_computation.2 | async-start | bytes 4718592 | tf_op jit(solution)/shard_map/psum | solution.py:57
  666.0 70.1 %copy-start.3 = (f32[1,4,384,384]{3,2,1,0:T(8,128)S(1)}, f32[1,4,384,384]{3,2,1,0:T(8,128)}, u32[]{:S(2)}) copy-start(f32[1,4,384,384]{3,2,1,0:T(8,128)} %all-reduce.9.cloned.1.call-done) | copy-start | bytes 7077892
  668.1 1.4 copy-start.6
  737.8 164.1 %copy-start.1 = (bf16[1,4,384,384]{3,2,1,0:T(8,128)(2,1)S(1)}, bf16[1,4,384,384]{3,2,1,0:T(8,128)(2,1)}, u32[]{:S(2)}) copy-start(bf16[1,4,384,384]{3,2,1,0:T(8,128)(2,1)} %param.8) | copy-start | bytes 3538948
Sparse Core Ops, SparseCore 0:
  357.1 110.2 all-reduce.6
  560.0 105.9 all-reduce.8
  758.3 105.8 all-reduce.10
where the time goes:
time: 909 us; the launch traced here: 908 us
  waiting for transfers between devices  626 us (69%)
  blocking collectives  157 us (17%)
  matrix products  81.7 us (9%)
  between operations  19.3 us (2%)
  other arithmetic  17.8 us (2%)
    psum x3, waiting for transfers between devices, on_device(): sigma_full = lax.psum(partial_sigma, 'ops') * live  322 us
    ppermute x1, waiting for transfers between devices, from_behind(): return lax.ppermute(block, axis, route)  304 us
    psum x3, blocking collectives, quotient(): lax.psum((jnp.sum(vector_rows * sigma_rows), jnp.sum(vector_rows * vector...  96.3 us
    dot_general x3, matrix products, on_device(): jnp.einsum('ckqad,ckqed->cqae', products, right_ops, preferred_element_ty...  60.6 us
    psum x2, blocking collectives, quotient(): spread = lax.psum(jnp.sum(leftover * leftover), ('ops', 'sector'))  60.4 us
    dot_general x1, matrix products, on_device(): jnp.einsum('cqba,ckqbd->ckqad', basis, half_env, preferred_element_type=j...  21.1 us
  transfers between devices with their start and end apart: 4, of which 4 were waited for; matrix products, arithmetic and copies ran while one was open for 0% of the time, Pallas kernels for 0%

commit v1 on v0

--- a/solution.py
+++ b/solution.py
@@ -20,14 +20,26 @@
     return inside.astype(jnp.float32)
 
 
-def quotient(vector_rows, sigma_rows):
-    correlation, norm_sum = lax.psum(
-        (jnp.sum(vector_rows * sigma_rows), jnp.sum(vector_rows * vector_rows)), ("ops", "sector")
-    )
-    rayleigh = correlation / norm_sum
-    leftover = sigma_rows - rayleigh * vector_rows
-    spread = lax.psum(jnp.sum(leftover * leftover), ("ops", "sector"))
-    return (rayleigh, spread)
+def gather_sector(values):
+    count = lax.axis_size("sector")
+    slots = jnp.zeros((count, values.shape[0]), jnp.float32)
+    slots = slots.at[lax.axis_index("sector")].set(values)
+    return lax.psum(slots, "sector")
+
+
+def quotient(vector_wide, sigma_full):
+    norm_part = jnp.sum(vector_wide * vector_wide)
+    corr_part = jnp.sum(vector_wide * sigma_full)
+    local_theta = jnp.where(norm_part > 0, corr_part / jnp.where(norm_part > 0, norm_part, 1.0), 0.0)
+    local_rest = sigma_full - local_theta * vector_wide
+    rest_part = jnp.sum(local_rest * local_rest)
+    cross_part = jnp.sum(vector_wide * local_rest)
+    table = gather_sector(jnp.stack([norm_part, corr_part, rest_part, cross_part, local_theta]))
+    norms, corrs, rests, crosses, thetas = (table[:, i] for i in range(5))
+    rayleigh = jnp.sum(corrs) / jnp.sum(norms)
+    shift = thetas - rayleigh
+    spread = jnp.sum(rests + 2.0 * shift * crosses + shift * shift * norms)
+    return rayleigh, spread
 
 
 def on_device(psi, left_ops, right_ops, basis, block_dims):
@@ -44,8 +56,7 @@
     entry_count = float(SECTORS * block_size * block_size)
     share_rows = block_size // lax.axis_size("ops")
     row_start = lax.axis_index("ops") * share_rows
-    live_rows = lax.dynamic_slice_in_dim(live, row_start, share_rows, 2)
-    residual = jnp.zeros(live_rows.shape, jnp.float32)
+    residual = None
     quotients = []
     for iteration in range(ITERS):
         products = jnp.einsum(
@@ -55,15 +66,14 @@
             "ckqad,ckqed->cqae", products, right_ops, preferred_element_type=jnp.float32
         )
         sigma_full = lax.psum(partial_sigma, "ops") * live
-        sigma_rows = lax.dynamic_slice_in_dim(sigma_full, row_start, share_rows, 2)
-        vector_rows = lax.dynamic_slice_in_dim(vector, row_start, share_rows, 2).astype(jnp.float32)
-        rayleigh, spread = quotient(vector_rows, sigma_rows)
+        vector_wide = vector.astype(jnp.float32)
+        rayleigh, spread = quotient(vector_wide, sigma_full)
         quotients.append(rayleigh)
+        residue = sigma_full - rayleigh * vector_wide
         if iteration + 1 < ITERS:
-            residue = sigma_full - rayleigh * vector.astype(jnp.float32)
             vector = (residue * lax.rsqrt(spread / entry_count + 1e-06)).astype(jnp.bfloat16)
         else:
-            residual = sigma_rows - rayleigh * vector_rows
+            residual = lax.dynamic_slice_in_dim(residue, row_start, share_rows, 2)
     thetas = jnp.stack(quotients).reshape(1, ITERS)
     return (residual, thetas)
 

time: 909 us -> 786 us (0.86)
  blocking collectives: 157 us -> 7.42 us
  other arithmetic: 17.8 us -> 28.5 us
    psum x5 -> x3, blocking collectives: 157 us -> 7.42 us  [gather_sector(): return lax.psum(slots, 'sector')]
    reduce_sum x5 -> x11, other arithmetic: 6.54 us -> 19.2 us  [the longest x3 9.77 us: quotient(): corr_part = jnp.sum(vector_wide * sigma_full)]
where the time goes in v1:
time: 786 us; the launch traced here: 785 us
  waiting for transfers between devices  629 us (80%)
  matrix products  82 us (10%)
  other arithmetic  28.5 us (4%)
  between operations  25.1 us (3%)
  local copies, waits for them, and re-layouts  10.1 us (1%)
    psum x3, waiting for transfers between devices, on_device(): sigma_full = lax.psum(partial_sigma, 'ops') * live  325 us
    ppermute x1, waiting for transfers between devices, from_behind(): return lax.ppermute(block, axis, route)  304 us
    dot_general x3, matrix products, on_device(): jnp.einsum('ckqad,ckqed->cqae', products, right_ops, preferred_element_ty...  60.9 us
    dot_general x1, matrix products, on_device(): jnp.einsum('cqba,ckqbd->ckqad', basis, half_env, preferred_element_type=j...  21.1 us
  transfers between devices with their start and end apart: 4, of which 4 were waited for; matrix products, arithmetic and copies ran while one was open for 0% of the time, Pallas kernels for 0%

profile of v1, /device:TPU:0, one launch (start us, length us, event | category | flops | bytes accessed | tf_op | source)
XLA Modules:
  0.0 785.4 jit_solution(4046029485822084687)
XLA Ops:
  7.2 0.0 copy-start
  7.2 0.0 copy-start.6
  7.2 0.0 copy-start.4
  7.2 0.0 all-reduce.4.cloned.1.call-start
  7.2 1.2 copy-done
  8.4 21.1 %convert_bitcast_fusion = bf16[1,12,4,384,384]{3,4,1,2,0:T(8,128)(2,1)} fusion(bf16[1,4,384,384]{3,2,1,0:T(8,128)(2,1)S(1)} %copy-done, bf16[1,12,4,384,384]{4,3,2,1,0:T(8,128)(2,1)} %param.12), kind=kOutput, calls=%fused_computation.19 | convolution fusion | flops 10885791744 | bytes 29491200 | tf_op jit(solution)/shard_map/cqba,ckqbd->ckqad/dot_general | solution.py:51
  29.5 2.9 collective-permute-start
  32.4 0.0 copy-done.6
  32.4 0.1 iota_compare_fusion
  32.5 304.3 %collective-permute-done = bf16[1,12,4,384,384]{3,4,1,2,0:T(8,128)(2,1)} collective-permute-done((bf16[1,12,4,384,384]{3,4,1,2,0:T(8,128)(2,1)}, bf16[1,12,4,384,384]{3,4,1,2,0:T(8,128)(2,1)}, u32[]{:S(2)}, u32[]{:S(2)}) %collective-permute-start) | collective-permute-done | bytes 14155808 | tf_op jit(solution)/shard_map/ppermute | solution.py:13
  336.8 0.0 copy-done.4
  336.8 20.6 %fusion.59 = f32[1,4,384,384]{3,2,1,0:T(8,128)} fusion(bf16[1,12,4,384,384]{3,4,1,2,0:T(8,128)(2,1)} %collective-permute-done, bf16[1,4,384,384]{3,2,1,0:T(8,128)(2,1)S(1)} %copy-done.4, pred[4,384]{1,0:T(4,128)(4,1)S(1)} %iota_compare_fusion, bf16[1,12,4,384,384]{4,3,2,1,0:T(8,128)(2,1)} %param.13), kind=kOutput, calls=%fused_computation.61 | convolution fusion | flops 10881073152 | bytes 31852032 | tf_op jit(solution)/shard_map/ckqad,ckqed->cqae/dot_general | solution.py:65
  357.4 0.0 copy-start.7
  357.4 0.0 copy-start.5
  357.4 0.0 all-reduce.4.cloned.1.call-update
  357.4 0.0 all-reduce.6.cloned.1.call-start
  357.5 0.6 copy-done.7
  358.0 0.7 and_reduce_fusion
  358.7 109.0 %all-reduce.4.cloned.1.call-done = f32[1,4,384,384]{3,2,1,0:T(8,128)} async-done(((f32[1,4,384,384]{3,2,1,0:T(8,128)}), f32[1,4,384,384]{3,2,1,0:T(8,128)}) %all-reduce.4.cloned.1.call-update) | async-done | bytes 2359312 | tf_op jit(solution)/shard_map/psum | solution.py:68
  467.7 0.0 copy-done.5
  467.8 0.0 copy-start.3
  467.8 3.2 fusion.45
  473.0 0.0 copy-done.3
  473.0 2.1 fusion.47
  475.0 2.6 stack.71
  477.7 0.6 broadcast_select_fusion.2
  478.2 0.1 copy.41
  478.4 2.5 psum.43
  480.9 0.6 slice_reduce_fusion.5
  482.8 0.6 add_reduce_fusion.1
  484.1 2.1 fusion.50
  486.2 20.1 %fusion.66 = f32[1,4,384,384]{3,2,1,0:T(8,128)} fusion(bf16[1,12,4,384,384]{3,4,1,2,0:T(8,128)(2,1)} %collective-permute-done, bf16[1,4,384,384]{3,2,1,0:T(8,128)(2,1)S(1)} %fusion.50, bf16[1,12,4,384,384]{4,3,2,1,0:T(8,128)(2,1)} %param.13), kind=kOutput, calls=%fused_computation.62 | convolution fusion | flops 10878713856 | bytes 31850496 | tf_op jit(solution)/shard_map/ckqad,ckqed->cqae/dot_general | solution.py:65
  506.3 0.0 all-reduce.6.cloned.1.call-update
  506.3 0.0 all-reduce.8.cloned.1.call-start
  506.4 107.9 %all-reduce.6.cloned.1.call-done = f32[1,4,384,384]{3,2,1,0:T(8,128)} async-done(((f32[1,4,384,384]{3,2,1,0:T(8,128)}), f32[1,4,384,384]{3,2,1,0:T(8,128)}) %all-reduce.6.cloned.1.call-update) | async-done | bytes 2359312 | tf_op jit(solution)/shard_map/psum | solution.py:68
  614.3 0.0 copy-start.2
  614.3 3.3 fusion.52
  619.6 0.0 copy-done.2
  619.6 1.8 fusion.54
  621.4 2.6 stack.77
  624.1 0.6 broadcast_select_fusion.1
  624.6 0.1 copy.46
  624.8 2.5 psum.45
  627.2 0.6 slice_reduce_fusion.4
  629.2 0.6 add_reduce_fusion
  630.5 2.4 fusion.90
  632.9 20.2 %fusion.73 = f32[1,4,384,384]{3,2,1,0:T(8,128)} fusion(bf16[1,12,4,384,384]{3,4,1,2,0:T(8,128)(2,1)} %collective-permute-done, bf16[1,4,384,384]{3,2,1,0:T(8,128)(2,1)} %get-tuple-element.58, bf16[1,12,4,384,384]{4,3,2,1,0:T(8,128)(2,1)} %param.13), kind=kOutput, calls=%fused_computation.63 | convolution fusion | flops 10878713856 | bytes 31850496 | tf_op jit(solution)/shard_map/ckqad,ckqed->cqae/dot_general | solution.py:65
  653.1 0.0 all-reduce.8.cloned.1.call-update
  653.2 107.9 %all-reduce.8.cloned.1.call-done = f32[1,4,384,384]{3,2,1,0:T(8,128)} async-done(((f32[1,4,384,384]{3,2,1,0:T(8,128)}), f32[1,4,384,384]{3,2,1,0:T(8,128)}) %all-reduce.8.cloned.1.call-update) | async-done | bytes 2359312 | tf_op jit(solution)/shard_map/psum | solution.py:68
  761.1 0.0 copy-start.1
  761.1 3.2 multiply_reduce_fusion.2
  766.2 2.5 multiply_reduce_fusion
  768.8 2.6 stack.83
  771.4 0.6 broadcast_select_fusion
  772.0 0.1 copy.51
  772.1 2.5 psum.47
  774.6 0.6 slice_reduce_fusion
  776.5 1.7 dynamic-slice_subtract_fusion
  778.3 0.6 maximum_bitcast_fusion
  778.8 0.0 copy-done.1
  (6 shorter events, 0.1 us)
Async XLA Ops:
  7.2 1.3 copy-start
  7.2 25.3 %copy-start.6 = (s32[1,4]{1,0:T(1,128)S(1)}, s32[1,4]{1,0:T(1,128)}, u32[]{:S(2)}) copy-start(s32[1,4]{1,0:T(1,128)} %param.15) | copy-start | bytes 52
  7.2 329.6 %copy-start.4 = (bf16[1,4,384,384]{3,2,1,0:T(8,128)(2,1)S(1)}, bf16[1,4,384,384]{3,2,1,0:T(8,128)(2,1)}, u32[]{:S(2)}) copy-start(bf16[1,4,384,384]{3,2,1,0:T(8,128)(2,1)} %param.11) | copy-start | bytes 3538948
  7.2 460.5 %all-reduce.4.cloned.1.call-start = ((), (), s32[]{:S(2)}) async-start(), calls=%async_computation | async-start | bytes 4718592 | tf_op jit(solution)/shard_map/psum | solution.py:68
  29.5 307.3 %collective-permute-start = (bf16[1,12,4,384,384]{3,4,1,2,0:T(8,128)(2,1)}, bf16[1,12,4,384,384]{3,4,1,2,0:T(8,128)(2,1)}, u32[]{:S(2)}, u32[]{:S(2)}) collective-permute-start(bf16[1,12,4,384,384]{3,4,1,2,0:T(8,128)(2,1)} %convert_bitcast_fusion), channel_id=1, source_target_pairs={{16,0},{0,16},{17,1},{1,17},{18,2},{2,18},{19,3},{3,19},{20,4},{4,... | collective-permute-start | bytes 42467336 | tf_op jit(solution)/shard_map/ppermute | solution.py:13
  357.4 0.7 copy-start.7
  357.4 110.4 %copy-start.5 = (bf16[1,4,384,384]{3,2,1,0:T(8,128)(2,1)S(1)}, bf16[1,4,384,384]{3,2,1,0:T(8,128)(2,1)}, u32[]{:S(2)}) copy-start(bf16[1,4,384,384]{3,2,1,0:T(8,128)(2,1)} %param.11) | copy-start | bytes 3538948
  357.4 256.9 %all-reduce.6.cloned.1.call-start = ((), (), s32[]{:S(2)}) async-start(), calls=%async_computation.1 | async-start | bytes 4718592 | tf_op jit(solution)/shard_map/psum | solution.py:68
  467.8 5.2 copy-start.3
  506.3 254.8 %all-reduce.8.cloned.1.call-start = ((), (), s32[]{:S(2)}) async-start(), calls=%async_computation.2 | async-start | bytes 4718592 | tf_op jit(solution)/shard_map/psum | solution.py:68
  614.3 5.3 copy-start.2
  761.1 17.8 %copy-start.1 = (bf16[1,4,384,384]{3,2,1,0:T(8,128)(2,1)S(1)}, bf16[1,4,384,384]{3,2,1,0:T(8,128)(2,1)}, u32[]{:S(2)}) copy-start(bf16[1,4,384,384]{3,2,1,0:T(8,128)(2,1)} %param.14) | copy-start | bytes 3538948
Sparse Core Ops, SparseCore 0:
  357.5 110.1 all-reduce.3
  506.5 107.7 all-reduce.5
  653.3 107.7 all-reduce.7

commit v2 on v1

--- a/solution.py
+++ b/solution.py
@@ -18,6 +18,86 @@
     limits = block_dims[:, :, None, None]
     inside = (index_rows[None, None, :, None] < limits) & (index_rows[None, None, None, :] < limits)
     return inside.astype(jnp.float32)
+
+ROW_TILE = 64
+LANE_TILE = 128
+CLASSES = 8
+
+
+def tile_counts(dims, block_size):
+    rows = jnp.clip((dims + ROW_TILE - 1) // ROW_TILE, 0, block_size // ROW_TILE)
+    cols = jnp.clip((dims + LANE_TILE - 1) // LANE_TILE, 0, block_size // LANE_TILE)
+    return rows, cols
+
+
+def tile_plan(dims, block_size):
+    rows, cols = tile_counts(dims, block_size)
+    row_ids = jnp.arange(block_size // ROW_TILE)[None, :, None]
+    col_ids = jnp.arange(block_size // LANE_TILE)[None, None, :]
+    needed = ((row_ids < rows[:, None, None]) & (col_ids < cols[:, None, None])).reshape(-1)
+    total = needed.shape[0]
+    place = jnp.cumsum(needed.astype(jnp.int32)) - 1
+    ids = jnp.arange(total, dtype=jnp.int32)
+    order = jnp.zeros(total, jnp.int32).at[jnp.where(needed, place, total)].set(ids, mode="drop")
+    return order, jnp.sum(needed.astype(jnp.int32))
+
+
+def size_classes(sectors, block_size):
+    total = sectors * (block_size // ROW_TILE) * (block_size // LANE_TILE)
+    return sorted({-(-k * total // CLASSES) for k in range(1, CLASSES + 1)})
+
+
+def tile_index(order, size, block_size):
+    per_row = block_size // LANE_TILE
+    per_sector = (block_size // ROW_TILE) * per_row
+    picked = order[:size]
+    return picked // per_sector, (picked // per_row) % (block_size // ROW_TILE), picked % per_row
+
+
+def tiled(array):
+    block_size = array.shape[-1]
+    return array.reshape(
+        array.shape[:-2] + (block_size // ROW_TILE, ROW_TILE, block_size // LANE_TILE, LANE_TILE)
+    )
+
+
+def pack(array, order, size, lead):
+    sector_ids, row_ids, col_ids = tile_index(order, size, array.shape[-1])
+    where = (slice(None),) * lead + (sector_ids, row_ids, slice(None), col_ids, slice(None))
+    return tiled(array)[where]
+
+
+def unpack(packed, order, count, size, like, lead):
+    sector_ids, row_ids, col_ids = tile_index(order, size, like.shape[-1])
+    sector_ids = jnp.where(jnp.arange(size) < count, sector_ids, like.shape[lead])
+    where = (slice(None),) * lead + (sector_ids, row_ids, slice(None), col_ids, slice(None))
+    room = jnp.zeros(tiled(like).shape, packed.dtype)
+    return room.at[where].set(packed, mode="drop").reshape(like.shape)
+
+
+def class_index(block_dims, block_size, classes):
+    every = lax.all_gather(block_dims[0], ("chain", "sector"))
+    rows, cols = tile_counts(every, block_size)
+    need = jnp.max(jnp.sum(rows * cols, axis=-1))
+    return jnp.sum((jnp.asarray(classes, jnp.int32) < need).astype(jnp.int32))
+
+
+def chain_move(env, send_order, recv_order, recv_count, choice, classes):
+    def branch(size):
+        def run(env, send_order, recv_order, recv_count):
+            arrived = from_behind(pack(env, send_order, size, 2), "chain", 1)
+            return unpack(arrived, recv_order, recv_count, size, env, 2)
+        return run
+    return lax.switch(choice, [branch(s) for s in classes], env, send_order, recv_order, recv_count)
+
+
+def ops_sum(partial, order, count, choice, classes):
+    def branch(size):
+        def run(partial, order, count):
+            summed = lax.psum(pack(partial, order, size, 1), "ops")
+            return unpack(summed, order, count, size, partial, 1)
+        return run
+    return lax.switch(choice, [branch(s) for s in classes], partial, order, count)
 
 
 def gather_sector(values):
@@ -45,13 +125,18 @@
 def on_device(psi, left_ops, right_ops, basis, block_dims):
     block_size = psi.shape[2]
     live = live_mask(block_dims, block_size)
+    classes = size_classes(psi.shape[1], block_size)
+    choice = class_index(block_dims, block_size, classes)
+    own_order, own_count = tile_plan(block_dims[0], block_size)
+    target_dims = from_behind(block_dims, "chain", -1)
+    send_order, _ = tile_plan(target_dims[0], block_size)
     half_env = jnp.einsum(
         "ckqab,cqbd->ckqad", left_ops, basis, preferred_element_type=jnp.float32
     ).astype(jnp.bfloat16)
     boundary_ops = jnp.einsum(
         "cqba,ckqbd->ckqad", basis, half_env, preferred_element_type=jnp.float32
     ).astype(jnp.bfloat16)
-    shifted = from_behind(boundary_ops, "chain", 1)
+    shifted = chain_move(boundary_ops, send_order, own_order, own_count, choice, classes)
     vector = jnp.where(live > 0, psi, jnp.zeros_like(psi))
     entry_count = float(SECTORS * block_size * block_size)
     share_rows = block_size // lax.axis_size("ops")
@@ -65,7 +150,7 @@
         partial_sigma = jnp.einsum(
             "ckqad,ckqed->cqae", products, right_ops, preferred_element_type=jnp.float32
         )
-        sigma_full = lax.psum(partial_sigma, "ops") * live
+        sigma_full = ops_sum(partial_sigma, own_order, own_count, choice, classes) * live
         vector_wide = vector.astype(jnp.float32)
         rayleigh, spread = quotient(vector_wide, sigma_full)
         quotients.append(rayleigh)

time: 786 us -> 1010 us (1.28); the launches traced: 785 us -> 997 us
  local copies, waits for them, and re-layouts: 10.1 us -> 267 us
  waiting for transfers between devices: 629 us -> 510 us
  loops' own time: 0 us -> 62 us
    reshape x0 -> x11, local copies, waits for them, and re-layouts: none -> 103 us  [the longest x8 91.4 us: tiled(): array.reshape(array.shape[:-2] + (block_size // ROW_TILE, ROW_TILE, block...]
    ppermute x1 -> x2, waiting for transfers between devices: 304 us -> 230 us  [from_behind(): return lax.ppermute(block, axis, route)]
    scatter x0 -> x9, local copies, waits for them, and re-layouts: none -> 67.4 us  [the longest x7 65.8 us: unpack(): return room.at[where].set(packed, mode='drop').reshape(like.shape)]
    another operation x0 -> x4, loops' own time: none -> 62 us  [the longest x3 38 us: ops_sum(): lax.switch(choice, [branch(s) for s in classes], partial, order, count)]
    cond x0 -> x2, local copies, waits for them, and re-layouts: none -> 56.5 us  [chain_move(): lax.switch(choice, [branch(s) for s in classes], env, send_order, recv_or...]
    psum x3, waiting for transfers between devices: 325 us -> 280 us  [run(): summed = lax.psum(pack(partial, order, size, 1), 'ops')]
    gather x0 -> x4, local copies, waits for them, and re-layouts: none -> 19.9 us  [pack(): return tiled(array)[where]]
  transfers between devices with their start and end apart: 4 -> 5, of which waited for: 4 -> 4; matrix products, arithmetic and copies ran while one was open for 0% -> 3% of each run, Pallas kernels for 0% -> 0%
where the time goes in v2:
time: 1010 us; the launch traced here: 997 us
  waiting for transfers between devices  510 us (50%)
  local copies, waits for them, and re-layouts  267 us (26%)
  matrix products  82.1 us (8%)
  loops' own time  62 us (6%)
  other arithmetic  34 us (3%)
  between operations  26.4 us (3%)
  blocking collectives  12.6 us (1%)
    psum x3, waiting for transfers between devices, run(): summed = lax.psum(pack(partial, order, size, 1), 'ops')  280 us
    ppermute x2, waiting for transfers between devices, from_behind(): return lax.ppermute(block, axis, route)  230 us
    reshape x8, local copies, waits for them, and re-layouts, tiled(): array.reshape(array.shape[:-2] + (block_size // ROW_TILE, ROW_TILE, block...  91.4 us
    scatter x7, local copies, waits for them, and re-layouts, unpack(): return room.at[where].set(packed, mode='drop').reshape(like.shape)  65.8 us
    dot_general x3, matrix products, on_device(): jnp.einsum('ckqad,ckqed->cqae', products, right_ops, preferred_element_ty...  61.1 us
    cond x2, local copies, waits for them, and re-layouts, chain_move(): lax.switch(choice, [branch(s) for s in classes], env, send_order, recv_or...  56.5 us
    another operation x3, loops' own time, ops_sum(): lax.switch(choice, [branch(s) for s in classes], partial, order, count)  38 us
    another operation x1, loops' own time, chain_move(): lax.switch(choice, [branch(s) for s in classes], env, send_order, recv_or...  24.1 us
  transfers between devices with their start and end apart: 5, of which 4 were waited for; matrix products, arithmetic and copies ran while one was open for 3% of the time, Pallas kernels for 0%

profile of v2, /device:TPU:0, one launch (start us, length us, event | category | flops | bytes accessed | tf_op | source)
XLA Modules:
  0.0 997.2 jit_solution(8939563958995975156)
XLA Ops:
  7.2 3.0 collective-permute-start.8
  10.2 0.7 fusion.452
  11.3 0.7 convert_reduce_fusion
  12.2 5.2 all-gather
  17.3 1.3 iota_compare_fusion
  18.8 0.8 scatter_custom_fusion.32
  19.7 21.1 %convert_bitcast_fusion = bf16[1,12,4,384,384]{3,4,1,2,0:T(8,128)(2,1)} fusion(bf16[1,4,384,384]{3,2,1,0:T(8,128)(2,1)S(1)} %copy-done, bf16[1,12,4,384,384]{4,3,2,1,0:T(8,128)(2,1)} %param.45), kind=kOutput, calls=%fused_computation.911 | convolution fusion | flops 10885791744 | bytes 29491200 | tf_op jit(solution)/shard_map/cqba,ckqbd->ckqad/dot_general | solution.py:136
  41.5 1.3 fusion.448
  43.5 0.7 and_reduce_fusion
  45.0 0.8 scatter_custom_fusion.33
  45.8 441.8 %conditional.4 = (bf16[12,4,384,384]{3,2,0,1:T(8,128)(2,1)}) conditional(s32[]{:T(128)} %clamp.28, (s32[]{:T(128)}, s32[72]{0:T(128)S(1)}, bf16[1,12,4,384,384]{3,4,1,2,0:T(8,128)(2,1)}, s32[72]{0:T(128)S(1)}) %tuple.124, (s32[]{:T(128)}, s32[72]{0:T(128)S(1)}, bf16[1,12,4,384,384]{3,4,1,2,0:T(8,128)(2,1)}, ...), branch_computations={%region_8.10_spmd, %region_10.12_spmd, %region_12.14_spmd, %region... | conditional | flops 6480 | bytes 254806912 | solution.py:91
  56.3 42.8 %reshape.1812 = bf16[12,4,6,64,3,128]{3,2,5,4,0,1:T(8,128)(2,1)} reshape(bf16[1,12,4,384,384]{3,4,1,2,0:T(8,128)(2,1)} %get-tuple-element.537) | data formatting | bytes 28311552 | tf_op jit(solution)/shard_map/cond/branch_5_fun/reshape | solution.py:59
  99.1 34.4 %copy.314 = bf16[12,4,6,64,3,128]{5,3,4,2,1,0:T(8,128)(2,1)} copy(bf16[12,4,6,64,3,128]{3,2,5,4,0,1:T(8,128)(2,1)} %reshape.1812) | data formatting | bytes 28311552 | tf_op jit(solution)/shard_map/cond/branch_5_fun/reshape | solution.py:59
  133.5 12.7 %gather_fusion.5 = bf16[54,12,64,128]{3,2,1,0:T(8,128)(2,1)} fusion(bf16[12,4,6,64,3,128]{5,3,4,2,1,0:T(8,128)(2,1)} %copy.314, s32[54]{0:T(128)S(1)} %fusion.72), kind=kCustom, calls=%fused_computation.5 | custom fusion | bytes 21234312 | tf_op jit(solution)/shard_map/cond/branch_5_fun/gather | solution.py:67
  146.9 230.1 %collective-permute-done.5 = bf16[54,1,12,64,128]{4,3,2,0,1:T(8,128)(2,1)} collective-permute-done((bf16[54,1,12,64,128]{4,3,2,0,1:T(8,128)(2,1)}, bf16[54,1,12,64,128]{4,3,2,0,1:T(8,128)(2,1)}, u32[]{:S(2)}, u32[]{:S(2)}) %collective-permute-start.5) | collective-permute-done | bytes 10616864 | tf_op jit(solution)/shard_map/cond/branch_5_fun/ppermute | solution.py:13
  377.0 8.6 broadcast.2387
  385.6 32.0 %scatter_fusion.5 = bf16[12,4,6,64,3,128]{5,3,4,2,1,0:T(8,128)(2,1)} fusion(bf16[12,4,6,64,3,128]{5,3,4,2,1,0:T(8,128)(2,1)} %broadcast.2387, s32[54]{0:T(128)S(1)} %fusion.77, bf16[54,12,64,128]{3,2,1,0:T(8,128)(2,1)} %bitcast.35), kind=kCustom, calls=%fused_computation.37 | custom fusion | bytes 31851144 | tf_op jit(solution)/shard_map/cond/branch_5_fun/scatter | solution.py:75
  417.6 20.5 %copy.450 = bf16[12,4,6,64,3,128]{5,4,3,2,0,1:T(4,128)(2,1)} copy(bf16[12,4,6,64,3,128]{5,3,4,2,1,0:T(8,128)(2,1)} %scatter_fusion.5) | data formatting | bytes 28311552 | tf_op jit(solution)/shard_map/cond | solution.py:91
  438.1 35.9 %reshape.1820 = bf16[12,4,384,384]{3,2,0,1:T(8,128)(2,1)} reshape(bf16[12,4,6,64,3,128]{5,4,3,2,0,1:T(4,128)(2,1)} %copy.450) | data formatting | bytes 28311552 | tf_op jit(solution)/shard_map/cond | solution.py:91
  487.7 20.6 %fusion.415 = f32[1,4,384,384]{3,2,1,0:T(8,128)S(1)} fusion(bf16[12,4,384,384]{3,2,0,1:T(8,128)(2,1)} %get-tuple-element.547, bf16[1,4,384,384]{3,2,1,0:T(8,128)(2,1)S(1)} %copy-done.2, pred[4,384]{1,0:T(4,128)(4,1)S(1)} %copy-done.9, bf16[1,12,4,384,384]{4,3,2,1,0:T(8,128)(2,1)} %param.46), kind=kOutput, calls=%fused_computation.956 | convolution fusion | flops 10881073152 | bytes 31852032 | tf_op jit(solution)/shard_map/ckqad,ckqed->cqae/dot_general | solution.py:150
  508.3 132.5 %conditional.5 = (f32[1,4,384,384]{3,2,1,0:T(8,128)S(1)}) conditional(s32[]{:T(128)} %clamp.28, (s32[]{:T(128)}, s32[72]{0:T(128)S(1)}, f32[1,4,384,384]{3,2,1,0:T(8,128)S(1)}) %tuple.125, (s32[]{:T(128)}, s32[72]{0:T(128)S(1)}, f32[1,4,384,384]{3,2,1,0:T(8,128)S(1)}) %tuple.125, (s32[]{:T(128)}, s32[72]{0:T(128)S(1)}, ...), branch_computations={%region_24.27_spmd, %region_27.30_spmd, %region_30.33_spmd, %regio... | conditional | flops 595872 | bytes 47189432 | solution.py:100
  515.3 2.5 reshape.977
  517.8 2.2 copy.330
  520.0 2.4 gather_fusion.13
  523.0 95.0 %all-reduce.35.cloned.1.call-done = f32[54,1,64,128]{3,2,0,1:T(8,128)} async-done(((f32[54,1,64,128]{3,2,0,1:T(8,128)}), f32[54,1,64,128]{3,2,0,1:T(8,128)}) %all-reduce.35.cloned.1.call-update) | async-done | bytes 1769488 | tf_op jit(solution)/shard_map/cond/branch_5_fun/psum | solution.py:97
  618.4 7.8 scatter_fusion.13
  626.2 3.4 copy.331
  629.6 3.8 reshape.812
  640.8 2.0 fusion.401
  644.8 2.1 fusion.403
  646.9 2.7 stack.71
  650.3 2.5 psum.189
  652.8 0.7 slice_reduce_fusion.5
  656.1 2.1 fusion.406
  658.2 20.2 %fusion.420 = f32[1,4,384,384]{3,2,1,0:T(8,128)S(1)} fusion(bf16[12,4,384,384]{3,2,0,1:T(8,128)(2,1)} %get-tuple-element.547, bf16[1,4,384,384]{3,2,1,0:T(8,128)(2,1)S(1)} %fusion.406, bf16[1,12,4,384,384]{4,3,2,1,0:T(8,128)(2,1)} %param.46), kind=kOutput, calls=%fused_computation.957 | convolution fusion | flops 10878713856 | bytes 31850496 | tf_op jit(solution)/shard_map/ckqad,ckqed->cqae/dot_general | solution.py:150
  678.4 130.4 %conditional.6 = (f32[1,4,384,384]{3,2,1,0:T(8,128)S(1)}) conditional(s32[]{:T(128)} %clamp.28, (s32[]{:T(128)}, s32[72]{0:T(128)S(1)}, f32[1,4,384,384]{3,2,1,0:T(8,128)S(1)}) %tuple.126, (s32[]{:T(128)}, s32[72]{0:T(128)S(1)}, f32[1,4,384,384]{3,2,1,0:T(8,128)S(1)}) %tuple.126, (s32[]{:T(128)}, s32[72]{0:T(128)S(1)}, ...), branch_computations={%region_57.60_spmd, %region_60.63_spmd, %region_63.66_spmd, %regio... | conditional | flops 595872 | bytes 47189432 | solution.py:100
  685.4 2.5 reshape.1041
  687.9 2.2 copy.346
  690.1 2.4 gather_fusion.21
  693.1 92.6 %all-reduce.51.cloned.1.call-done = f32[54,1,64,128]{3,2,0,1:T(8,128)} async-done(((f32[54,1,64,128]{3,2,0,1:T(8,128)}), f32[54,1,64,128]{3,2,0,1:T(8,128)}) %all-reduce.51.cloned.1.call-update) | async-done | bytes 1769488 | tf_op jit(solution)/shard_map/cond/branch_5_fun/psum | solution.py:97
  786.0 7.8 scatter_fusion.21
  793.8 3.4 copy.347
  797.3 3.8 reshape.828
  808.8 1.7 fusion.408
  812.5 1.8 fusion.410
  814.3 2.7 stack.77
  817.7 2.5 psum.190
  820.2 0.7 slice_reduce_fusion.4
  823.6 2.5 fusion.459
  826.1 20.3 %fusion.425 = f32[1,4,384,384]{3,2,1,0:T(8,128)S(1)} fusion(bf16[12,4,384,384]{3,2,0,1:T(8,128)(2,1)} %get-tuple-element.547, bf16[1,4,384,384]{3,2,1,0:T(8,128)(2,1)} %get-tuple-element.616, bf16[1,12,4,384,384]{4,3,2,1,0:T(8,128)(2,1)} %param.46), kind=kOutput, calls=%fused_computation.958 | convolution fusion | flops 10878713856 | bytes 31850496 | tf_op jit(solution)/shard_map/ckqad,ckqed->cqae/dot_general | solution.py:150
  846.4 124.9 %conditional.7 = (f32[1,4,384,384]{3,2,1,0:T(8,128)S(1)}) conditional(s32[]{:T(128)} %clamp.28, (s32[]{:T(128)}, s32[72]{0:T(128)S(1)}, f32[1,4,384,384]{3,2,1,0:T(8,128)S(1)}) %tuple.127, (s32[]{:T(128)}, s32[72]{0:T(128)S(1)}, f32[1,4,384,384]{3,2,1,0:T(8,128)S(1)}) %tuple.127, (s32[]{:T(128)}, s32[72]{0:T(128)S(1)}, ...), branch_computations={%region_89.92_spmd, %region_92.95_spmd, %region_95.98_spmd, %regio... | conditional | flops 595872 | bytes 47189432 | solution.py:100
  853.3 2.5 reshape.1105
  855.9 2.2 copy.362
  858.1 2.4 gather_fusion.29
  861.1 92.6 %all-reduce.67.cloned.1.call-done = f32[54,1,64,128]{3,2,0,1:T(8,128)} async-done(((f32[54,1,64,128]{3,2,0,1:T(8,128)}), f32[54,1,64,128]{3,2,0,1:T(8,128)}) %all-reduce.67.cloned.1.call-update) | async-done | bytes 1769488 | tf_op jit(solution)/shard_map/cond/branch_5_fun/psum | solution.py:97
  954.0 7.8 scatter_fusion.29
  961.9 3.4 copy.363
  965.3 3.8 reshape.844
  971.2 1.4 copy-done.3
  972.6 3.2 multiply_reduce_fusion.2
  977.8 2.6 multiply_reduce_fusion
  980.3 2.7 stack.83
  983.7 2.5 psum.191
  988.1 1.7 dynamic-slice_subtract_fusion
  (72 shorter events, 10.4 us)
Async XLA Ops:
  7.2 12.5 %copy-start = (bf16[1,4,384,384]{3,2,1,0:T(8,128)(2,1)S(1)}, bf16[1,4,384,384]{3,2,1,0:T(8,128)(2,1)}, u32[]{:S(2)}) copy-start(bf16[1,4,384,384]{3,2,1,0:T(8,128)(2,1)} %param.47) | copy-start | bytes 3538948
  7.2 37.0 %collective-permute-start.8 = (s32[1,4]{1,0:T(1,128)}, s32[1,4]{1,0:T(1,128)S(1)}, u32[]{:S(2)}, u32[]{:S(2)}) collective-permute-start(s32[1,4]{1,0:T(1,128)} %param.48), channel_id=1, source_target_pairs={{16,0},{0,16},{17,1},{1,17},{18,2},{2,18},{19,3},{3,19},{20,4},{4,... | collective-permute-start | bytes 56 | tf_op jit(solution)/shard_map/ppermute | solution.py:13
  19.7 21.9 %copy-start.12 = (s32[8]{0:T(128)S(1)}, s32[8]{0:T(128)}, u32[]{:S(2)}) copy-start(s32[8]{0:T(128)} %constant.1748.clone) | copy-start | bytes 100
  19.7 23.8 %copy-start.11 = (s32[2]{0:T(128)S(1)}, s32[2]{0:T(128)}, u32[]{:S(2)}) copy-start(s32[2]{0:T(128)} %constant.1739.clone.1) | copy-start | bytes 28
  45.8 441.8 %copy-start.2 = (bf16[1,4,384,384]{3,2,1,0:T(8,128)(2,1)S(1)}, bf16[1,4,384,384]{3,2,1,0:T(8,128)(2,1)}, u32[]{:S(2)}) copy-start(bf16[1,4,384,384]{3,2,1,0:T(8,128)(2,1)} %param.44) | copy-start | bytes 3538948
  45.8 441.8 %copy-start.9 = (pred[4,384]{1,0:T(4,128)(4,1)S(1)}, pred[4,384]{1,0:T(4,128)(4,1)}, u32[]{:S(2)}) copy-start(pred[4,384]{1,0:T(4,128)(4,1)} %iota_compare_fusion) | copy-start | bytes 4612
  146.2 230.7 %collective-permute-start.5 = (bf16[54,1,12,64,128]{4,3,2,0,1:T(8,128)(2,1)}, bf16[54,1,12,64,128]{4,3,2,0,1:T(8,128)(2,1)}, u32[]{:S(2)}, u32[]{:S(2)}) collective-permute-start(bf16[54,1,12,64,128]{4,3,2,0,1:T(8,128)(2,1)} %bitcast.1130), channel_id=1, source_target_pairs={{16,0},{0,16},{17,1},{1,17},{18,2},{2,18},{19,3},{3,19},{20,4},{4,... | collective-permute-start | bytes 31850504 | tf_op jit(solution)/shard_map/cond/branch_5_fun/ppermute | solution.py:13
  515.2 102.9 %all-reduce.35.cloned.1.call-start = ((), (), s32[]{:S(2)}) async-start(), calls=%async_computation.5 | async-start | bytes 3538944 | tf_op jit(solution)/shard_map/cond/branch_5_fun/psum | solution.py:97
  685.3 100.4 %all-reduce.51.cloned.1.call-start = ((), (), s32[]{:S(2)}) async-start(), calls=%async_computation.13 | async-start | bytes 3538944 | tf_op jit(solution)/shard_map/cond/branch_5_fun/psum | solution.py:97
  853.2 100.5 %all-reduce.67.cloned.1.call-start = ((), (), s32[]{:S(2)}) async-start(), calls=%async_computation.21 | async-start | bytes 3538944 | tf_op jit(solution)/shard_map/cond/branch_5_fun/psum | solution.py:97
  971.2 1.4 copy-start.3
  972.6 17.8 %copy-start.1 = (bf16[1,4,384,384]{3,2,1,0:T(8,128)(2,1)S(1)}, bf16[1,4,384,384]{3,2,1,0:T(8,128)(2,1)}, u32[]{:S(2)}) copy-start(bf16[1,4,384,384]{3,2,1,0:T(8,128)(2,1)} %param.47) | copy-start | bytes 3538948
Sparse Core Ops, SparseCore 0:
  522.6 95.4 all-reduce.34
  692.6 93.0 all-reduce.50
  860.7 93.0 all-reduce.66

commit v3 on v1

--- a/solution.py
+++ b/solution.py
@@ -18,6 +18,52 @@
     limits = block_dims[:, :, None, None]
     inside = (index_rows[None, None, :, None] < limits) & (index_rows[None, None, None, :] < limits)
     return inside.astype(jnp.float32)
+
+
+def ring_order(axis):
+    count = lax.axis_size(axis)
+    ys = 2
+    zs = count // ys
+    if count % ys or zs % 2:
+        return list(range(count))
+    cycle = [z * ys for z in range(zs)]
+    for step, z in enumerate(range(zs - 1, -1, -1)):
+        cols = range(1, ys) if step % 2 == 0 else range(ys - 1, 0, -1)
+        cycle += [z * ys + y for y in cols]
+    return cycle
+
+
+def ring_sum(partial, axis):
+    cycle = ring_order(axis)
+    count = len(cycle)
+    place = jnp.asarray([cycle.index(i) for i in range(count)], jnp.int32)[lax.axis_index(axis)]
+    shape = partial.shape
+    chunks = partial.reshape(2, count, -1, shape[-1])
+    forward = [(cycle[p], cycle[(p + 1) % count]) for p in range(count)]
+    backward = [(cycle[p], cycle[(p - 1) % count]) for p in range(count)]
+    routes = (forward, backward)
+    signs = (1, -1)
+
+    def chunk(half, index):
+        return lax.dynamic_index_in_dim(chunks[half], index % count, 0, keepdims=False)
+
+    moving = [chunk(h, place - signs[h]) for h in range(2)]
+    for step in range(count - 1):
+        for h in range(2):
+            arrived = lax.ppermute(moving[h], axis, routes[h])
+            moving[h] = arrived + chunk(h, place - signs[h] * (step + 2))
+    gathered = []
+    for h in range(2):
+        table = jnp.zeros(chunks.shape[1:], partial.dtype)
+        table = lax.dynamic_update_index_in_dim(table, moving[h], place % count, 0)
+        current = moving[h]
+        for step in range(count - 1):
+            current = lax.ppermute(current, axis, routes[h])
+            table = lax.dynamic_update_index_in_dim(
+                table, current, (place - signs[h] * (step + 1)) % count, 0
+            )
+        gathered.append(table)
+    return jnp.stack(gathered).reshape(shape)
 
 
 def gather_sector(values):
@@ -65,7 +111,7 @@
         partial_sigma = jnp.einsum(
             "ckqad,ckqed->cqae", products, right_ops, preferred_element_type=jnp.float32
         )
-        sigma_full = lax.psum(partial_sigma, "ops") * live
+        sigma_full = ring_sum(partial_sigma, "ops") * live
         vector_wide = vector.astype(jnp.float32)
         rayleigh, spread = quotient(vector_wide, sigma_full)
         quotients.append(rayleigh)

time: 786 us -> 718 us (0.913)
  waiting for transfers between devices: 629 us -> 457 us
  starting transfers between devices: 3.05 us -> 99.5 us
    psum x3 -> x0, waiting for transfers between devices: 325 us -> none  [on_device(): sigma_full = lax.psum(partial_sigma, 'ops') * live]
    ppermute x0 -> x84, waiting for transfers between devices: none -> 154 us  [the longest x42 79 us: ring_sum(): current = lax.ppermute(current, axis, routes[h])]
    ppermute x0 -> x84, starting transfers between devices: none -> 96.6 us  [the longest x42 51.3 us: ring_sum(): current = lax.ppermute(current, axis, routes[h])]
  transfers between devices with their start and end apart: 4 -> 85, of which waited for: 4 -> 58; matrix products, arithmetic and copies ran while one was open for 0% -> 0% of each run, Pallas kernels for 0% -> 0%
where the time goes in v3:
time: 718 us; the launch traced here: 714 us
  waiting for transfers between devices  457 us (64%)
  starting transfers between devices  99.5 us (14%)
  matrix products  81.2 us (11%)
  other arithmetic  25.5 us (4%)
  between operations  25.5 us (4%)
  local copies, waits for them, and re-layouts  17.3 us (2%)
  blocking collectives  7.42 us (1%)
    ppermute x1, waiting for transfers between devices, from_behind(): return lax.ppermute(block, axis, route)  303 us
    ppermute x42, waiting for transfers between devices, ring_sum(): current = lax.ppermute(current, axis, routes[h])  79 us
    ppermute x42, waiting for transfers between devices, ring_sum(): arrived = lax.ppermute(moving[h], axis, routes[h])  75.2 us
    dot_general x3, matrix products, on_device(): jnp.einsum('ckqad,ckqed->cqae', products, right_ops, preferred_element_ty...  60.1 us
    ppermute x42, starting transfers between devices, ring_sum(): current = lax.ppermute(current, axis, routes[h])  51.3 us
    ppermute x42, starting transfers between devices, ring_sum(): arrived = lax.ppermute(moving[h], axis, routes[h])  45.3 us
    dot_general x1, matrix products, on_device(): jnp.einsum('cqba,ckqbd->ckqad', basis, half_env, preferred_element_type=j...  21.1 us
  transfers between devices with their start and end apart: 85, of which 58 were waited for; matrix products, arithmetic and copies ran while one was open for 0% of the time, Pallas kernels for 0%

profile of v3, /device:TPU:0, one launch (start us, length us, event | category | flops | bytes accessed | tf_op | source)
XLA Modules:
  0.0 713.5 jit_solution(16643081846317007757)
XLA Ops:
  1.9 21.1 %convert_bitcast_fusion = bf16[1,12,4,384,384]{3,4,1,2,0:T(8,128)(2,1)} fusion(bf16[1,4,384,384]{3,2,1,0:T(8,128)(2,1)S(1)} %copy-done, bf16[1,12,4,384,384]{4,3,2,1,0:T(8,128)(2,1)} %param.15), kind=kOutput, calls=%fused_computation.19 | convolution fusion | flops 10885791744 | bytes 29491200 | tf_op jit(solution)/shard_map/cqba,ckqbd->ckqad/dot_general | solution.py:97
  23.0 2.9 collective-permute-start
  27.3 303.0 %collective-permute-done = bf16[1,12,4,384,384]{3,4,1,2,0:T(8,128)(2,1)} collective-permute-done((bf16[1,12,4,384,384]{3,4,1,2,0:T(8,128)(2,1)}, bf16[1,12,4,384,384]{3,4,1,2,0:T(8,128)(2,1)}, u32[]{:S(2)}, u32[]{:S(2)}) %collective-permute-start) | collective-permute-done | bytes 14155808 | tf_op jit(solution)/shard_map/ppermute | solution.py:13
  330.3 20.6 %fusion.59 = f32[4,384,384]{2,1,0:T(8,128)} fusion(bf16[1,12,4,384,384]{3,4,1,2,0:T(8,128)(2,1)} %collective-permute-done, bf16[1,4,384,384]{3,2,1,0:T(8,128)(2,1)S(1)} %copy-done.2, pred[4,384]{1,0:T(4,128)(4,1)S(1)} %iota_compare_fusion, bf16[1,12,4,384,384]{4,3,2,1,0:T(8,128)(2,1)} %param.16), kind=kOutput, calls=%fused_computation.64 | convolution fusion | flops 10881073152 | bytes 31852032 | tf_op jit(solution)/shard_map/ckqad,ckqed->cqae/dot_general | solution.py:111
  369.5 3.0 collective-permute-done.15
  372.8 1.9 collective-permute-start.3
  374.7 4.0 collective-permute-done.16
  378.9 2.3 collective-permute-start.4
  381.2 3.9 collective-permute-done.17
  387.3 3.5 collective-permute-done.18
  392.9 3.0 collective-permute-done.19
  398.1 3.3 collective-permute-done.20
  404.1 4.3 collective-permute-done.21
  410.6 3.5 collective-permute-done.22
  416.2 3.0 collective-permute-done.23
  421.3 3.9 collective-permute-done.24
  425.2 2.4 collective-permute-start.12
  427.6 4.1 collective-permute-done.25
  431.8 2.1 collective-permute-start.13
  433.9 3.0 collective-permute-done.26
  437.0 2.0 collective-permute-start.14
  439.0 3.0 collective-permute-done.27
  442.1 5.0 collective-permute-done.28
  452.3 2.1 fusion.47
  454.3 2.6 stack.202
  457.7 2.5 psum.21
  463.5 2.1 fusion.50
  465.5 19.3 %fusion.66 = f32[4,384,384]{2,1,0:T(8,128)S(1)} fusion(bf16[1,12,4,384,384]{3,4,1,2,0:T(8,128)(2,1)} %collective-permute-done, bf16[1,4,384,384]{3,2,1,0:T(8,128)(2,1)S(1)} %fusion.50, bf16[1,12,4,384,384]{4,3,2,1,0:T(8,128)(2,1)} %param.16), kind=kOutput, calls=%fused_computation.65 | convolution fusion | flops 10878713856 | bytes 31850496 | tf_op jit(solution)/shard_map/ckqad,ckqed->cqae/dot_general | solution.py:111
  487.2 3.8 collective-permute-done.29
  493.2 3.0 collective-permute-done.30
  498.4 3.3 collective-permute-done.31
  503.9 4.2 collective-permute-done.32
  510.3 4.2 collective-permute-done.33
  516.6 3.4 collective-permute-done.34
  522.2 3.0 collective-permute-done.35
  527.6 3.8 collective-permute-done.36
  533.5 4.5 collective-permute-done.37
  540.1 3.7 collective-permute-done.38
  545.9 3.0 collective-permute-done.39
  551.0 3.0 collective-permute-done.40
  556.2 3.0 collective-permute-done.41
  562.1 8.9 %collective-permute-start.56 = (f32[96,384]{1,0:T(8,128)S(1)}, f32[96,384]{1,0:T(8,128)S(1)}, u32[]{:S(2)}, u32[]{:S(2)}) collective-permute-start(f32[96,384]{1,0:T(8,128)S(1)} %collective-permute-done.55), channel_id=1, source_target_pairs={{0,2},{4,0},{8,4},{12,8},{14,12},{10,14},{6,10},{2,6},{1,3},{5,1},... | collective-permute-start | bytes 442376 | tf_op jit(solution)/shard_map/ppermute | solution.py:61
  571.1 4.9 collective-permute-done.56
  581.5 2.6 stack.225
  584.9 2.5 psum.22
  590.7 2.4 fusion.90
  593.1 20.2 %fusion.73 = f32[4,384,384]{2,1,0:T(8,128)} fusion(bf16[1,12,4,384,384]{3,4,1,2,0:T(8,128)(2,1)} %collective-permute-done, bf16[1,4,384,384]{3,2,1,0:T(8,128)(2,1)} %get-tuple-element.58, bf16[1,12,4,384,384]{4,3,2,1,0:T(8,128)(2,1)} %param.16), kind=kOutput, calls=%fused_computation.66 | convolution fusion | flops 10878713856 | bytes 31850496 | tf_op jit(solution)/shard_map/ckqad,ckqed->cqae/dot_general | solution.py:111
  617.3 3.8 collective-permute-done.57
  623.3 3.0 collective-permute-done.58
  628.5 3.3 collective-permute-done.59
  634.0 4.2 collective-permute-done.60
  640.5 4.0 collective-permute-done.61
  646.7 3.4 collective-permute-done.62
  652.3 3.0 collective-permute-done.63
  657.7 3.9 collective-permute-done.64
  663.7 4.4 collective-permute-done.65
  670.2 3.5 collective-permute-done.66
  675.9 3.0 collective-permute-done.67
  681.0 3.0 collective-permute-done.68
  686.1 3.0 collective-permute-done.69
  691.3 3.0 collective-permute-done.70
  700.5 2.7 multiply_reduce_fusion
  703.2 2.7 stack.248
  706.6 2.5 psum.23
  (264 shorter events, 106.6 us)
Async XLA Ops:
  23.0 307.3 %collective-permute-start = (bf16[1,12,4,384,384]{3,4,1,2,0:T(8,128)(2,1)}, bf16[1,12,4,384,384]{3,4,1,2,0:T(8,128)(2,1)}, u32[]{:S(2)}, u32[]{:S(2)}) collective-permute-start(bf16[1,12,4,384,384]{3,4,1,2,0:T(8,128)(2,1)} %convert_bitcast_fusion), channel_id=1, source_target_pairs={{16,0},{0,16},{17,1},{1,17},{18,2},{2,18},{19,3},{3,19},{20,4},{4,... | collective-permute-start | bytes 42467336 | tf_op jit(solution)/shard_map/ppermute | solution.py:13
  352.7 14.8 %collective-permute-start.1 = (f32[96,384]{1,0:T(8,128)S(1)}, f32[96,384]{1,0:T(8,128)S(1)}, u32[]{:S(2)}, u32[]{:S(2)}) collective-permute-start(f32[96,384]{1,0:T(8,128)S(1)} %dynamic-slice_bitcast_fusion.5), channel_id=1, source_target_pairs={{0,4},{4,8},{8,12},{12,14},{14,10},{10,6},{6,2},{2,0},{1,5},{5,9},... | collective-permute-start | bytes 442376 | tf_op jit(solution)/shard_map/ppermute | solution.py:53
  367.3 5.2 collective-permute-start.15
  367.6 5.2 collective-permute-start.2
  372.5 6.2 collective-permute-start.16
  372.8 6.0 collective-permute-start.3
  378.7 6.3 collective-permute-start.17
  378.9 6.6 collective-permute-start.4
  385.1 5.6 collective-permute-start.18
  385.5 5.8 collective-permute-start.5
  390.8 5.2 collective-permute-start.19
  391.4 5.2 collective-permute-start.6
  396.0 5.5 collective-permute-start.20
  396.6 5.5 collective-permute-start.7
  401.5 6.9 collective-permute-start.21
  402.2 6.8 collective-permute-start.8
  408.5 5.6 collective-permute-start.22
  409.0 5.9 collective-permute-start.9
  419.2 6.0 collective-permute-start.24
  420.0 5.2 collective-permute-start.11
  425.2 6.6 collective-permute-start.25
  425.2 6.5 collective-permute-start.12
  431.8 5.2 collective-permute-start.13
  485.1 6.0 collective-permute-start.29
  486.9 6.0 collective-permute-start.43
  491.0 5.2 collective-permute-start.30
  492.9 5.2 collective-permute-start.44
  496.3 5.4 collective-permute-start.31
  498.1 5.4 collective-permute-start.45
  501.7 6.4 collective-permute-start.32
  503.6 6.6 collective-permute-start.46
  508.1 6.3 collective-permute-start.33
  510.2 6.1 collective-permute-start.47
  514.5 5.5 collective-permute-start.34
  516.3 5.5 collective-permute-start.48
  520.0 5.2 collective-permute-start.35
  521.9 5.3 collective-permute-start.49
  525.4 6.0 collective-permute-start.36
  527.3 6.0 collective-permute-start.50
  531.4 6.6 collective-permute-start.37
  533.3 6.5 collective-permute-start.51
  538.0 5.8 collective-permute-start.38
  539.8 5.6 collective-permute-start.52
  545.4 5.2 collective-permute-start.53
  555.7 6.3 collective-permute-start.55
  559.2 11.8 %collective-permute-start.42 = (f32[96,384]{1,0:T(8,128)S(1)}, f32[96,384]{1,0:T(8,128)S(1)}, u32[]{:S(2)}, u32[]{:S(2)}) collective-permute-start(f32[96,384]{1,0:T(8,128)S(1)} %collective-permute-done.41), channel_id=1, source_target_pairs={{0,4},{4,8},{8,12},{12,14},{14,10},{10,6},{6,2},{2,0},{1,5},{5,9},... | collective-permute-start | bytes 442376 | tf_op jit(solution)/shard_map/ppermute | solution.py:61
  562.1 13.8 %collective-permute-start.56 = (f32[96,384]{1,0:T(8,128)S(1)}, f32[96,384]{1,0:T(8,128)S(1)}, u32[]{:S(2)}, u32[]{:S(2)}) collective-permute-start(f32[96,384]{1,0:T(8,128)S(1)} %collective-permute-done.55), channel_id=1, source_target_pairs={{0,2},{4,0},{8,4},{12,8},{14,12},{10,14},{6,10},{2,6},{1,3},{5,1},... | collective-permute-start | bytes 442376 | tf_op jit(solution)/shard_map/ppermute | solution.py:61
  615.1 6.0 collective-permute-start.57
  616.8 6.0 collective-permute-start.71
  626.4 5.4 collective-permute-start.59
  628.0 5.4 collective-permute-start.73
  631.8 6.4 collective-permute-start.60
  633.5 6.6 collective-permute-start.74
  638.2 6.3 collective-permute-start.61
  640.1 6.1 collective-permute-start.75
  644.6 5.6 collective-permute-start.62
  646.2 5.4 collective-permute-start.76
  651.6 5.3 collective-permute-start.77
  655.5 6.2 collective-permute-start.64
  657.0 6.4 collective-permute-start.78
  661.6 6.5 collective-permute-start.65
  663.4 6.1 collective-permute-start.79
  668.1 5.6 collective-permute-start.66
  669.5 5.5 collective-permute-start.80
  (29 other events, 510.1 us)

commit v4 on v3

--- a/solution.py
+++ b/solution.py
@@ -66,6 +66,52 @@
     return jnp.stack(gathered).reshape(shape)
 
 
+ROW_TILE = 64
+CLASSES = 8
+
+
+def row_counts(dims, block_size):
+    return jnp.clip((dims + ROW_TILE - 1) // ROW_TILE, 0, block_size // ROW_TILE)
+
+
+def row_plan(dims, block_size):
+    rows = row_counts(dims, block_size)
+    needed = (jnp.arange(block_size // ROW_TILE)[None, :] < rows[:, None]).reshape(-1)
+    total = needed.shape[0]
+    place = jnp.cumsum(needed.astype(jnp.int32)) - 1
+    ids = jnp.arange(total, dtype=jnp.int32)
+    order = jnp.zeros(total, jnp.int32).at[jnp.where(needed, place, total)].set(ids, mode="drop")
+    return order, jnp.sum(rows)
+
+
+def size_classes(sectors, block_size):
+    total = sectors * (block_size // ROW_TILE)
+    return sorted({-(-k * total // CLASSES) for k in range(1, CLASSES + 1)})
+
+
+def class_index(block_dims, block_size, classes):
+    every = lax.all_gather(block_dims[0], ("chain", "sector"))
+    need = jnp.max(jnp.sum(row_counts(every, block_size), axis=-1))
+    return jnp.sum((jnp.asarray(classes, jnp.int32) < need).astype(jnp.int32))
+
+
+def chain_move(env, send_order, recv_order, recv_count, choice, classes):
+    block_size = env.shape[-1]
+    ops_here = env.shape[1]
+    blocks = env.reshape(ops_here, -1, ROW_TILE, block_size)
+
+    def branch(size):
+        def run(blocks, send_order, recv_order, recv_count):
+            packed = blocks[:, send_order[:size]]
+            arrived = from_behind(packed, "chain", 1)
+            slots = jnp.where(jnp.arange(size) < recv_count, recv_order[:size], blocks.shape[1])
+            room = jnp.zeros(blocks.shape, blocks.dtype)
+            return room.at[:, slots].set(arrived, mode="drop")
+        return run
+    moved = lax.switch(choice, [branch(s) for s in classes], blocks, send_order, recv_order, recv_count)
+    return moved.reshape(env.shape)
+
+
 def gather_sector(values):
     count = lax.axis_size("sector")
     slots = jnp.zeros((count, values.shape[0]), jnp.float32)
@@ -91,13 +137,18 @@
 def on_device(psi, left_ops, right_ops, basis, block_dims):
     block_size = psi.shape[2]
     live = live_mask(block_dims, block_size)
+    classes = size_classes(psi.shape[1], block_size)
+    choice = class_index(block_dims, block_size, classes)
+    own_order, own_count = row_plan(block_dims[0], block_size)
+    target_dims = from_behind(block_dims, "chain", -1)
+    send_order, _ = row_plan(target_dims[0], block_size)
     half_env = jnp.einsum(
         "ckqab,cqbd->ckqad", left_ops, basis, preferred_element_type=jnp.float32
     ).astype(jnp.bfloat16)
     boundary_ops = jnp.einsum(
         "cqba,ckqbd->ckqad", basis, half_env, preferred_element_type=jnp.float32
     ).astype(jnp.bfloat16)
-    shifted = from_behind(boundary_ops, "chain", 1)
+    shifted = chain_move(boundary_ops, send_order, own_order, own_count, choice, classes)
     vector = jnp.where(live > 0, psi, jnp.zeros_like(psi))
     entry_count = float(SECTORS * block_size * block_size)
     share_rows = block_size // lax.axis_size("ops")

time: 718 us -> 723 us (level); the launches traced: 714 us -> 736 us
  local copies, waits for them, and re-layouts: 17.3 us -> 93.3 us
  waiting for transfers between devices: 457 us -> 381 us
  loops' own time: 0 us -> 15 us
  starting transfers between devices: 99.5 us -> 90.5 us
  other arithmetic: 25.5 us -> 33.3 us
    ppermute x1 -> x2, waiting for transfers between devices: 303 us -> 229 us  [from_behind(): return lax.ppermute(block, axis, route)]
    scatter x0 -> x3, local copies, waits for them, and re-layouts: none -> 26.5 us  [the longest x1 25.2 us: run(): return room.at[:, slots].set(arrived, mode='drop')]
    another operation x6 -> x9, local copies, waits for them, and re-layouts: 0.28 us -> 26.4 us
    another operation x0 -> x1, loops' own time: none -> 15 us  [chain_move(): lax.switch(choice, [branch(s) for s in classes], blocks, send_order, recv...]
    cond x0 -> x1, local copies, waits for them, and re-layouts: none -> 13 us  [chain_move(): lax.switch(choice, [branch(s) for s in classes], blocks, send_order, recv...]
    gather x0 -> x1, local copies, waits for them, and re-layouts: none -> 11 us  [run(): packed = blocks[:, send_order[:size]]]
    ppermute x42, starting transfers between devices: 51.3 us -> 43.7 us  [ring_sum(): current = lax.ppermute(current, axis, routes[h])]
  transfers between devices with their start and end apart: 85 -> 86, of which waited for: 58 -> 61; matrix products, arithmetic and copies ran while one was open for 0% -> 4% of each run, Pallas kernels for 0% -> 0%
where the time goes in v4:
time: 723 us; the launch traced here: 736 us
  waiting for transfers between devices  381 us (53%)
  local copies, waits for them, and re-layouts  93.3 us (13%)
  starting transfers between devices  90.5 us (13%)
  matrix products  83.8 us (12%)
  other arithmetic  33.3 us (5%)
  between operations  26.4 us (4%)
  loops' own time  15 us (2%)
  blocking collectives  13 us (2%)
    ppermute x2, waiting for transfers between devices, from_behind(): return lax.ppermute(block, axis, route)  229 us
    ppermute x42, waiting for transfers between devices, ring_sum(): current = lax.ppermute(current, axis, routes[h])  75.8 us
    ppermute x42, waiting for transfers between devices, ring_sum(): arrived = lax.ppermute(moving[h], axis, routes[h])  75.3 us
    dot_general x3, matrix products, on_device(): jnp.einsum('ckqad,ckqed->cqae', products, right_ops, preferred_element_ty...  62.7 us
    ppermute x42, starting transfers between devices, ring_sum(): arrived = lax.ppermute(moving[h], axis, routes[h])  43.7 us
    ppermute x42, starting transfers between devices, ring_sum(): current = lax.ppermute(current, axis, routes[h])  43.7 us
    another operation x9, local copies, waits for them, and re-layouts  26.4 us
    scatter x1, local copies, waits for them, and re-layouts, run(): return room.at[:, slots].set(arrived, mode='drop')  25.2 us
  transfers between devices with their start and end apart: 86, of which 61 were waited for; matrix products, arithmetic and copies ran while one was open for 4% of the time, Pallas kernels for 0%

profile of v4, /device:TPU:0, one launch (start us, length us, event | category | flops | bytes accessed | tf_op | source)
XLA Modules:
  0.0 735.7 jit_solution(6878848328127316762)
XLA Ops:
  0.6 3.0 collective-permute-start.8
  7.3 5.2 all-gather
  17.1 21.0 %convert_bitcast_fusion = bf16[1,12,4,384,384]{3,4,1,2,0:T(8,128)(2,1)} fusion(bf16[1,4,384,384]{3,2,1,0:T(8,128)(2,1)S(1)} %copy-done, bf16[1,12,4,384,384]{4,3,2,1,0:T(8,128)(2,1)} %param.24), kind=kOutput, calls=%fused_computation.87 | convolution fusion | flops 10885791744 | bytes 29491200 | tf_op jit(solution)/shard_map/cqba,ckqbd->ckqad/dot_general | solution.py:148
  40.1 321.0 %conditional.1 = (bf16[12,4,384,384]{3,2,0,1:T(8,128)(2,1)}) conditional(s32[]{:T(128)} %clamp.22, (s32[4]{0:T(128)S(1)}, s32[4]{0:T(128)S(1)}, pred[4]{0:T(512)(128)(4,1)S(1)}, s32[4]{0:T(128)S(1)}, s32[4]{0:T(128)S(1)}, /*index=5*/s32[4]{0:T(128)S(1)}, s32[4]{0:T(128)S(1)}, s32[24]{0:T(128)S(1)}, ...), branch_computations={%region_7.10_spmd, %region_10.13_spmd, %region_13.16_spmd, %region... | conditional | flops 1255 | bytes 198185792 | solution.py:111
  47.1 18.8 %copy.126 = bf16[1,12,4,384,384]{4,3,2,1,0:T(8,128)(2,1)} copy(bf16[1,12,4,384,384]{3,4,1,2,0:T(8,128)(2,1)} %get-tuple-element.810) | data formatting | bytes 28311552 | tf_op jit(solution)/shard_map
  65.9 11.0 %gather_fusion.5 = bf16[18,12,64,384]{3,2,1,0:T(8,128)(2,1)} fusion(bf16[12,24,64,384]{3,2,1,0:T(8,128)(2,1)} %bitcast.395, s32[1024]{0:T(1024)S(1)} %pad_clamp_fusion.5), kind=kCustom, calls=%fused_computation.5 | custom fusion | bytes 21233736 | tf_op jit(solution)/shard_map/cond/branch_5_fun/gather | solution.py:105
  78.3 229.4 %collective-permute-done.5 = bf16[12,18,64,384]{3,2,0,1:T(8,128)(2,1)} collective-permute-done((bf16[12,18,64,384]{3,2,0,1:T(8,128)(2,1)}, bf16[12,18,64,384]{3,2,0,1:T(8,128)(2,1)}, u32[]{:S(2)}, u32[]{:S(2)}) %collective-permute-start.5) | collective-permute-done | bytes 10616864 | tf_op jit(solution)/shard_map/cond/branch_5_fun/ppermute | solution.py:13
  307.7 7.4 %broadcast.488 = bf16[12,24,64,384]{3,2,1,0:T(8,128)(2,1)} broadcast(bf16[]{:T(256)} %constant.799.clone), dimensions={} | broadcast | bytes 14155778 | tf_op jit(solution)/shard_map/broadcast.51
  315.0 25.2 %scatter_fusion.5 = bf16[12,24,64,384]{3,2,1,0:T(8,128)(2,1)} fusion(bf16[12,24,64,384]{3,2,1,0:T(8,128)(2,1)} %broadcast.488, s32[18]{0:T(128)S(1)} %compare_select_fusion.16, bf16[18,12,64,384]{3,2,1,0:T(8,128)(2,1)} %bitcast.22), kind=kCustom, calls=%fused_computation.13 | custom fusion | bytes 31850568 | tf_op jit(solution)/shard_map/cond/branch_5_fun/scatter | solution.py:109
  340.2 13.0 %copy.168 = bf16[12,4,384,384]{3,2,0,1:T(8,128)(2,1)} copy(bf16[12,4,384,384]{3,2,1,0:T(8,128)(2,1)} %bitcast.387) | data formatting | bytes 28311552 | tf_op jit(solution)/shard_map/cond | solution.py:111
  361.1 21.5 %fusion.47 = f32[4,384,384]{2,1,0:T(8,128)} fusion(bf16[12,4,384,384]{3,2,0,1:T(8,128)(2,1)} %get-tuple-element.832, bf16[1,4,384,384]{3,2,1,0:T(8,128)(2,1)S(1)} %copy-done.2, pred[4,384]{1,0:T(4,128)(4,1)S(1)} %copy-done.4, bf16[1,12,4,384,384]{4,3,2,1,0:T(8,128)(2,1)} %param.25), kind=kOutput, calls=%fused_computation.135 | convolution fusion | flops 10881073152 | bytes 31852032 | tf_op jit(solution)/shard_map/ckqad,ckqed->cqae/dot_general | solution.py:162
  402.5 3.2 collective-permute-done.23
  408.5 2.7 collective-permute-done.24
  413.7 2.7 collective-permute-done.25
  418.9 3.6 collective-permute-done.26
  425.0 4.1 collective-permute-done.27
  431.5 3.6 collective-permute-done.28
  437.3 2.9 collective-permute-done.29
  442.5 3.9 collective-permute-done.30
  446.4 2.1 collective-permute-start.18
  448.4 4.3 collective-permute-done.31
  454.8 3.4 collective-permute-done.32
  460.4 3.0 collective-permute-done.33
  465.5 3.0 collective-permute-done.34
  470.7 3.0 collective-permute-done.35
  474.7 4.1 collective-permute-done.36
  484.9 2.6 stack.202
  488.3 2.7 psum.21
  496.3 20.2 %fusion.52 = f32[4,384,384]{2,1,0:T(8,128)S(1)} fusion(bf16[12,4,384,384]{3,2,0,1:T(8,128)(2,1)} %get-tuple-element.832, bf16[1,4,384,384]{3,2,1,0:T(8,128)(2,1)S(1)} %fusion.38, bf16[1,12,4,384,384]{4,3,2,1,0:T(8,128)(2,1)} %param.25), kind=kOutput, calls=%fused_computation.136 | convolution fusion | flops 10878713856 | bytes 31850496 | tf_op jit(solution)/shard_map/ckqad,ckqed->cqae/dot_general | solution.py:162
  518.8 3.8 collective-permute-done.37
  524.8 3.0 collective-permute-done.38
  530.0 3.3 collective-permute-done.39
  535.5 4.2 collective-permute-done.40
  542.1 4.0 collective-permute-done.41
  548.2 3.4 collective-permute-done.42
  553.8 3.0 collective-permute-done.43
  559.2 3.8 collective-permute-done.44
  565.2 4.4 collective-permute-done.45
  571.7 3.6 collective-permute-done.46
  577.4 3.0 collective-permute-done.47
  582.6 3.0 collective-permute-done.48
  587.7 3.0 collective-permute-done.49
  592.9 3.0 collective-permute-done.50
  603.1 2.6 stack.225
  606.4 2.7 psum.22
  612.4 2.4 fusion.85
  614.8 21.1 %fusion.57 = f32[4,384,384]{2,1,0:T(8,128)} fusion(bf16[12,4,384,384]{3,2,0,1:T(8,128)(2,1)} %get-tuple-element.832, bf16[1,4,384,384]{3,2,1,0:T(8,128)(2,1)} %get-tuple-element.853, bf16[1,12,4,384,384]{4,3,2,1,0:T(8,128)(2,1)} %param.25), kind=kOutput, calls=%fused_computation.137 | convolution fusion | flops 10878713856 | bytes 31850496 | tf_op jit(solution)/shard_map/ckqad,ckqed->cqae/dot_general | solution.py:162
  639.8 3.8 collective-permute-done.65
  645.8 3.0 collective-permute-done.66
  651.0 3.3 collective-permute-done.67
  656.5 4.4 collective-permute-done.68
  663.1 3.9 collective-permute-done.69
  669.3 3.1 collective-permute-done.70
  674.6 3.0 collective-permute-done.71
  680.0 4.2 collective-permute-done.72
  686.4 3.9 collective-permute-done.73
  692.5 3.2 collective-permute-done.74
  697.8 3.0 collective-permute-done.75
  703.0 3.0 collective-permute-done.76
  708.1 3.0 collective-permute-done.77
  713.2 3.0 collective-permute-done.78
  722.5 2.6 multiply_reduce_fusion
  725.1 2.7 stack.248
  728.5 2.5 psum.23
  (300 shorter events, 130.5 us)
Async XLA Ops:
  0.6 37.5 %collective-permute-start.8 = (s32[1,4]{1,0:T(1,128)}, s32[1,4]{1,0:T(1,128)S(1)}, u32[]{:S(2)}, u32[]{:S(2)}) collective-permute-start(s32[1,4]{1,0:T(1,128)} %param.27), channel_id=1, source_target_pairs={{16,0},{0,16},{17,1},{1,17},{18,2},{2,18},{19,3},{3,19},{20,4},{4,... | collective-permute-start | bytes 56 | tf_op jit(solution)/shard_map/ppermute | solution.py:13
  76.9 230.7 %collective-permute-start.5 = (bf16[12,18,64,384]{3,2,0,1:T(8,128)(2,1)}, bf16[12,18,64,384]{3,2,0,1:T(8,128)(2,1)}, u32[]{:S(2)}, u32[]{:S(2)}) collective-permute-start(bf16[12,18,64,384]{3,2,0,1:T(8,128)(2,1)} %bitcast.409), channel_id=1, source_target_pairs={{16,0},{0,16},{17,1},{1,17},{18,2},{2,18},{19,3},{3,19},{20,4},{4,... | collective-permute-start | bytes 31850504 | tf_op jit(solution)/shard_map/cond/branch_5_fun/ppermute | solution.py:13
  385.1 14.8 %collective-permute-start.9 = (f32[96,384]{1,0:T(8,128)}, f32[96,384]{1,0:T(8,128)}, u32[]{:S(2)}, u32[]{:S(2)}) collective-permute-start(f32[96,384]{1,0:T(8,128)} %dynamic-slice_bitcast_fusion.5), channel_id=1, source_target_pairs={{0,4},{4,8},{8,12},{12,14},{14,10},{10,6},{6,2},{2,0},{1,5},{5,9},... | collective-permute-start | bytes 442376 | tf_op jit(solution)/shard_map/ppermute | solution.py:53
  399.4 6.3 collective-permute-start.23
  400.9 6.0 collective-permute-start.10
  405.7 5.5 collective-permute-start.24
  406.9 5.2 collective-permute-start.11
  411.2 5.2 collective-permute-start.25
  412.1 5.2 collective-permute-start.12
  416.4 6.1 collective-permute-start.26
  417.3 6.4 collective-permute-start.13
  422.5 6.6 collective-permute-start.27
  423.7 6.1 collective-permute-start.14
  429.2 5.9 collective-permute-start.28
  429.8 5.7 collective-permute-start.15
  435.1 5.2 collective-permute-start.29
  435.7 5.3 collective-permute-start.16
  440.4 6.0 collective-permute-start.30
  441.0 5.4 collective-permute-start.17
  446.3 6.4 collective-permute-start.31
  446.4 6.6 collective-permute-start.18
  452.7 5.5 collective-permute-start.32
  452.9 6.0 collective-permute-start.19
  458.9 5.4 collective-permute-start.20
  464.4 5.2 collective-permute-start.21
  516.7 6.0 collective-permute-start.37
  518.4 6.0 collective-permute-start.51
  522.6 5.2 collective-permute-start.38
  524.4 5.2 collective-permute-start.52
  527.9 5.4 collective-permute-start.39
  529.6 5.4 collective-permute-start.53
  533.3 6.4 collective-permute-start.40
  535.1 6.6 collective-permute-start.54
  539.7 6.3 collective-permute-start.41
  541.7 6.1 collective-permute-start.55
  546.1 5.5 collective-permute-start.42
  547.8 5.5 collective-permute-start.56
  551.6 5.2 collective-permute-start.43
  553.4 5.3 collective-permute-start.57
  557.0 6.1 collective-permute-start.44
  558.8 6.0 collective-permute-start.58
  563.0 6.6 collective-permute-start.45
  564.8 6.5 collective-permute-start.59
  569.6 5.7 collective-permute-start.46
  571.3 5.6 collective-permute-start.60
  576.9 5.2 collective-permute-start.61
  637.7 6.0 collective-permute-start.65
  638.9 6.0 collective-permute-start.79
  648.9 5.4 collective-permute-start.67
  650.2 5.4 collective-permute-start.81
  654.4 6.6 collective-permute-start.68
  655.6 6.6 collective-permute-start.82
  661.0 6.1 collective-permute-start.69
  662.3 6.1 collective-permute-start.83
  667.1 5.3 collective-permute-start.70
  668.4 5.3 collective-permute-start.84
  672.4 5.2 collective-permute-start.71
  673.7 5.3 collective-permute-start.85
  677.7 6.5 collective-permute-start.72
  679.1 6.5 collective-permute-start.86
  684.2 6.1 collective-permute-start.73
  685.6 6.0 collective-permute-start.87
  690.4 5.3 collective-permute-start.74
  691.6 5.3 collective-permute-start.88
  (28 other events, 790.0 us)

commit v5 on v3

--- a/solution.py
+++ b/solution.py
@@ -91,13 +91,19 @@
 def on_device(psi, left_ops, right_ops, basis, block_dims):
     block_size = psi.shape[2]
     live = live_mask(block_dims, block_size)
-    half_env = jnp.einsum(
-        "ckqab,cqbd->ckqad", left_ops, basis, preferred_element_type=jnp.float32
-    ).astype(jnp.bfloat16)
-    boundary_ops = jnp.einsum(
-        "cqba,ckqbd->ckqad", basis, half_env, preferred_element_type=jnp.float32
-    ).astype(jnp.bfloat16)
-    shifted = from_behind(boundary_ops, "chain", 1)
+    ops_here = left_ops.shape[1]
+    pieces = 3 if ops_here % 3 == 0 else (2 if ops_here % 2 == 0 else 1)
+    width = ops_here // pieces
+    spans = [slice(i * width, (i + 1) * width) for i in range(pieces)]
+    shifted = []
+    for span in spans:
+        half_env = jnp.einsum(
+            "ckqab,cqbd->ckqad", left_ops[:, span], basis, preferred_element_type=jnp.float32
+        ).astype(jnp.bfloat16)
+        boundary_ops = jnp.einsum(
+            "cqba,ckqbd->ckqad", basis, half_env, preferred_element_type=jnp.float32
+        ).astype(jnp.bfloat16)
+        shifted.append(from_behind(boundary_ops, "chain", 1))
     vector = jnp.where(live > 0, psi, jnp.zeros_like(psi))
     entry_count = float(SECTORS * block_size * block_size)
     share_rows = block_size // lax.axis_size("ops")
@@ -105,12 +111,15 @@
     residual = None
     quotients = []
     for iteration in range(ITERS):
-        products = jnp.einsum(
-            "ckqab,cqbd->ckqad", shifted, vector, preferred_element_type=jnp.float32
-        ).astype(jnp.bfloat16)
-        partial_sigma = jnp.einsum(
-            "ckqad,ckqed->cqae", products, right_ops, preferred_element_type=jnp.float32
-        )
+        partial_sigma = None
+        for span, moved in zip(spans, shifted):
+            products = jnp.einsum(
+                "ckqab,cqbd->ckqad", moved, vector, preferred_element_type=jnp.float32
+            ).astype(jnp.bfloat16)
+            term = jnp.einsum(
+                "ckqad,ckqed->cqae", products, right_ops[:, span], preferred_element_type=jnp.float32
+            )
+            partial_sigma = term if partial_sigma is None else partial_sigma + term
         sigma_full = ring_sum(partial_sigma, "ops") * live
         vector_wide = vector.astype(jnp.float32)
         rayleigh, spread = quotient(vector_wide, sigma_full)

time: 718 us -> 725 us (level)
  waiting for transfers between devices: 457 us -> 400 us
  matrix products: 81.2 us -> 117 us
  local copies, waits for them, and re-layouts: 17.3 us -> 39.3 us
    ppermute x1 -> x3, waiting for transfers between devices: 303 us -> 253 us  [from_behind(): return lax.ppermute(block, axis, route)]
    dot_general x3 -> x9, matrix products: 60.1 us -> 90.4 us  [on_device(): jnp.einsum('ckqad,ckqed->cqae', products, right_ops[:, span], preferred_e...]
    slice x0 -> x2, local copies, waits for them, and re-layouts: none -> 24 us  [the longest x1 12 us: on_device(): right_ops[:, span]]
    ppermute x42, starting transfers between devices: 45.3 us -> 56.9 us  [ring_sum(): arrived = lax.ppermute(moving[h], axis, routes[h])]
    ppermute x42, starting transfers between devices: 51.3 us -> 43.5 us  [ring_sum(): current = lax.ppermute(current, axis, routes[h])]
    dot_general x1 -> x3, matrix products: 21.1 us -> 26.5 us  [on_device(): jnp.einsum('cqba,ckqbd->ckqad', basis, half_env, preferred_element_type=j...]
  transfers between devices with their start and end apart: 85 -> 87, of which waited for: 58 -> 61; matrix products, arithmetic and copies ran while one was open for 0% -> 7% of each run, Pallas kernels for 0% -> 0%
where the time goes in v5:
time: 725 us; the launch traced here: 721 us
  waiting for transfers between devices  400 us (55%)
  matrix products  117 us (16%)
  starting transfers between devices  105 us (14%)
  local copies, waits for them, and re-layouts  39.3 us (5%)
  other arithmetic  27.2 us (4%)
  between operations  25.5 us (4%)
  blocking collectives  7.42 us (1%)
    ppermute x3, waiting for transfers between devices, from_behind(): return lax.ppermute(block, axis, route)  253 us
    dot_general x9, matrix products, on_device(): jnp.einsum('ckqad,ckqed->cqae', products, right_ops[:, span], preferred_e...  90.4 us
    ppermute x42, waiting for transfers between devices, ring_sum(): current = lax.ppermute(current, axis, routes[h])  76.1 us
    ppermute x42, waiting for transfers between devices, ring_sum(): arrived = lax.ppermute(moving[h], axis, routes[h])  70.9 us
    ppermute x42, starting transfers between devices, ring_sum(): arrived = lax.ppermute(moving[h], axis, routes[h])  56.9 us
    ppermute x42, starting transfers between devices, ring_sum(): current = lax.ppermute(current, axis, routes[h])  43.5 us
    dot_general x3, matrix products, on_device(): jnp.einsum('cqba,ckqbd->ckqad', basis, half_env, preferred_element_type=j...  26.5 us
  transfers between devices with their start and end apart: 87, of which 61 were waited for; matrix products, arithmetic and copies ran while one was open for 7% of the time, Pallas kernels for 0%

profile of v5, /device:TPU:0, one launch (start us, length us, event | category | flops | bytes accessed | tf_op | source)
XLA Modules:
  0.0 721.3 jit_solution(14275244726463861379)
XLA Ops:
  0.6 12.0 %fusion.174 = (bf16[1,4,4,384,384]{4,3,2,1,0:T(8,128)(2,1)}, bf16[1,4,4,384,384]{4,3,2,1,0:T(8,128)(2,1)}, bf16[1,4,4,384,384]{4,3,2,1,0:T(8,128)(2,1)}) fusion(bf16[1,12,4,384,384]{4,3,2,1,0:T(8,128)(2,1)} %param.15), kind=kLoop, calls=%fused_computation.240 | loop fusion | bytes 28311552 | tf_op jit(solution)/shard_map/slice | solution.py:101
  12.7 8.8 %convert_bitcast_fusion = bf16[1,4,4,384,384]{3,4,1,2,0:T(8,128)(2,1)} fusion(bf16[1,4,4,384,384]{4,3,2,1,0:T(8,128)(2,1)} %get-tuple-element.73, bf16[1,4,384,384]{3,2,1,0:T(8,128)(2,1)S(1)} %copy-done), kind=kOutput, calls=%fused_computation.68 | convolution fusion | flops 3628597248 | bytes 10616832 | tf_op jit(solution)/shard_map/cqba,ckqbd->ckqad/dot_general | solution.py:103
  21.5 2.9 collective-permute-start.2
  24.4 8.9 %convert_bitcast_fusion.1 = bf16[1,4,4,384,384]{3,4,1,2,0:T(8,128)(2,1)} fusion(bf16[1,4,4,384,384]{4,3,2,1,0:T(8,128)(2,1)} %get-tuple-element.72, bf16[1,4,384,384]{3,2,1,0:T(8,128)(2,1)S(1)} %copy-done), kind=kOutput, calls=%fused_computation.71 | convolution fusion | flops 3628597248 | bytes 10616832 | tf_op jit(solution)/shard_map/cqba,ckqbd->ckqad/dot_general | solution.py:103
  33.3 8.9 %convert_bitcast_fusion.2 = bf16[1,4,4,384,384]{3,4,1,2,0:T(8,128)(2,1)} fusion(bf16[1,4,4,384,384]{4,3,2,1,0:T(8,128)(2,1)} %get-tuple-element.71, bf16[1,4,384,384]{3,2,1,0:T(8,128)(2,1)S(1)} %copy-done), kind=kOutput, calls=%fused_computation.74 | convolution fusion | flops 3628597248 | bytes 10616832 | tf_op jit(solution)/shard_map/cqba,ckqbd->ckqad/dot_general | solution.py:103
  45.5 12.0 %fusion.175 = (bf16[1,4,4,384,384]{4,3,2,1,0:T(8,128)(2,1)}, bf16[1,4,4,384,384]{4,3,2,1,0:T(8,128)(2,1)}, bf16[1,4,4,384,384]{4,3,2,1,0:T(8,128)(2,1)}) fusion(bf16[1,12,4,384,384]{4,3,2,1,0:T(8,128)(2,1)} %param.16), kind=kLoop, calls=%fused_computation.241 | loop fusion | bytes 28311552 | tf_op jit(solution)/shard_map/slice | solution.py:120
  57.6 69.8 %collective-permute-done.2 = bf16[1,4,4,384,384]{3,4,1,2,0:T(8,128)(2,1)} collective-permute-done((bf16[1,4,4,384,384]{3,4,1,2,0:T(8,128)(2,1)}, bf16[1,4,4,384,384]{3,4,1,2,0:T(8,128)(2,1)}, u32[]{:S(2)}, u32[]{:S(2)}) %collective-permute-start.2) | collective-permute-done | bytes 4718624 | tf_op jit(solution)/shard_map/ppermute | solution.py:13
  127.4 8.2 %fusion.15 = f32[4,384,384,1]{2,1,3,0:T(8,128)S(1)} fusion(bf16[1,4,4,384,384]{4,3,2,1,0:T(8,128)(2,1)} %get-tuple-element.76, bf16[1,4,4,384,384]{3,4,1,2,0:T(8,128)(2,1)} %collective-permute-done.2, bf16[1,4,384,384]{3,2,1,0:T(8,128)(2,1)S(1)} %copy-done.2, pred[4,384]{1,0:T(4,128)(4,1)S(1)} %iota_compare_fusion), kind=kOutput, calls=%fused_computation.21 | convolution fusion | flops 3628597248 | bytes 12977664 | tf_op jit(solution)/shard_map/ckqad,ckqed->cqae/dot_general | solution.py:119
  135.6 92.9 %collective-permute-done.1 = bf16[1,4,4,384,384]{3,4,1,2,0:T(8,128)(2,1)} collective-permute-done((bf16[1,4,4,384,384]{3,4,1,2,0:T(8,128)(2,1)}, bf16[1,4,4,384,384]{3,4,1,2,0:T(8,128)(2,1)}, u32[]{:S(2)}, u32[]{:S(2)}) %collective-permute-start.1) | collective-permute-done | bytes 4718624 | tf_op jit(solution)/shard_map/ppermute | solution.py:13
  228.5 10.5 %fusion.19 = f32[4,384,384,1]{2,1,3,0:T(8,128)} fusion(bf16[1,4,4,384,384]{4,3,2,1,0:T(8,128)(2,1)} %get-tuple-element.75, bf16[1,4,4,384,384]{3,4,1,2,0:T(8,128)(2,1)} %collective-permute-done.1, bf16[1,4,384,384]{3,2,1,0:T(8,128)(2,1)S(1)} %copy-done.2, pred[4,384]{1,0:T(4,128)(4,1)S(1)} %iota_compare_fusion), kind=kOutput, calls=%fused_computation.25 | convolution fusion | flops 3628597248 | bytes 12977664 | tf_op jit(solution)/shard_map/ckqad,ckqed->cqae/dot_general | solution.py:119
  238.9 89.8 %collective-permute-done = bf16[1,4,4,384,384]{3,4,1,2,0:T(8,128)(2,1)} collective-permute-done((bf16[1,4,4,384,384]{3,4,1,2,0:T(8,128)(2,1)}, bf16[1,4,4,384,384]{3,4,1,2,0:T(8,128)(2,1)}, u32[]{:S(2)}, u32[]{:S(2)}) %collective-permute-start) | collective-permute-done | bytes 4718624 | tf_op jit(solution)/shard_map/ppermute | solution.py:13
  328.7 11.2 %fusion.80 = f32[1,4,384,384]{3,2,1,0:T(8,128)} fusion(f32[4,384,384,1]{2,1,3,0:T(8,128)S(1)} %fusion.15, f32[4,384,384,1]{2,1,3,0:T(8,128)} %fusion.19, bf16[1,4,4,384,384]{4,3,2,1,0:T(8,128)(2,1)} %get-tuple-element.74, bf16[1,4,4,384,384]{3,4,1,2,0:T(8,128)(2,1)} %collective-permute-done, bf16[1,4,384,384]{3,2,1,0:T(8,128)(2,1)S(1)} %copy-done.2, ...), kind=kOutput, calls=%fused_computation.105 | convolution fusion | flops 3629776896 | bytes 17696256 | tf_op jit(solution)/shard_map/ckqad,ckqed->cqae/dot_general | solution.py:119
  365.2 3.1 collective-permute-done.18
  368.6 14.1 %collective-permute-start.6 = (f32[96,384]{1,0:T(8,128)S(1)}, f32[96,384]{1,0:T(8,128)S(1)}, u32[]{:S(2)}, u32[]{:S(2)}) collective-permute-start(f32[96,384]{1,0:T(8,128)S(1)} %bitcast_add_fusion.45), channel_id=1, source_target_pairs={{0,4},{4,8},{8,12},{12,14},{14,10},{10,6},{6,2},{2,0},{1,5},{5,9},... | collective-permute-start | bytes 442376 | tf_op jit(solution)/shard_map/ppermute | solution.py:53
  382.8 4.4 collective-permute-done.6
  389.4 3.6 collective-permute-done.7
  395.1 3.0 collective-permute-done.8
  400.4 3.6 collective-permute-done.9
  406.4 4.4 collective-permute-done.10
  413.0 3.7 collective-permute-done.11
  418.8 3.0 collective-permute-done.12
  424.0 3.4 collective-permute-done.13
  429.5 3.0 collective-permute-done.14
  434.7 3.0 collective-permute-done.15
  439.8 3.0 collective-permute-done.16
  450.2 2.7 stack.202
  453.6 2.5 psum.21
  461.4 10.2 %fusion.11 = f32[4,384,384,1]{2,1,3,0:T(8,128)} fusion(bf16[1,4,4,384,384]{4,3,2,1,0:T(8,128)(2,1)} %get-tuple-element.75, bf16[1,4,4,384,384]{3,4,1,2,0:T(8,128)(2,1)} %collective-permute-done.1, bf16[1,4,384,384]{3,2,1,0:T(8,128)(2,1)S(1)} %fusion.70), kind=kOutput, calls=%fused_computation.17 | convolution fusion | flops 3626237952 | bytes 12976128 | tf_op jit(solution)/shard_map/ckqad,ckqed->cqae/dot_general | solution.py:119
  471.6 10.3 %fusion.9 = f32[4,384,384,1]{2,1,3,0:T(8,128)} fusion(bf16[1,4,4,384,384]{4,3,2,1,0:T(8,128)(2,1)} %get-tuple-element.76, bf16[1,4,4,384,384]{3,4,1,2,0:T(8,128)(2,1)} %collective-permute-done.2, bf16[1,4,384,384]{3,2,1,0:T(8,128)(2,1)S(1)} %fusion.70), kind=kOutput, calls=%fused_computation.15 | convolution fusion | flops 3626237952 | bytes 12976128 | tf_op jit(solution)/shard_map/ckqad,ckqed->cqae/dot_general | solution.py:119
  481.9 10.7 %fusion.79 = f32[1,4,384,384]{3,2,1,0:T(8,128)S(1)} fusion(f32[4,384,384,1]{2,1,3,0:T(8,128)} %fusion.9, f32[4,384,384,1]{2,1,3,0:T(8,128)} %fusion.11, bf16[1,4,4,384,384]{4,3,2,1,0:T(8,128)(2,1)} %get-tuple-element.74, bf16[1,4,4,384,384]{3,4,1,2,0:T(8,128)(2,1)} %collective-permute-done, bf16[1,4,384,384]{3,2,1,0:T(8,128)(2,1)S(1)} %fusion.70), kind=kOutput, calls=%fused_computation.102 | convolution fusion | flops 3627417600 | bytes 17694720 | tf_op jit(solution)/shard_map/ckqad,ckqed->cqae/dot_general | solution.py:119
  494.9 3.8 collective-permute-done.31
  500.9 3.0 collective-permute-done.32
  506.1 3.3 collective-permute-done.33
  511.6 4.2 collective-permute-done.34
  518.2 4.0 collective-permute-done.35
  524.3 3.4 collective-permute-done.36
  529.9 3.0 collective-permute-done.37
  535.3 3.9 collective-permute-done.38
  541.4 4.3 collective-permute-done.39
  547.8 3.5 collective-permute-done.40
  553.4 3.0 collective-permute-done.41
  558.5 3.0 collective-permute-done.42
  563.7 3.0 collective-permute-done.43
  568.8 3.0 collective-permute-done.44
  579.1 2.7 stack.225
  590.6 8.2 %fusion.5 = f32[4,384,384,1]{2,1,3,0:T(8,128)S(1)} fusion(bf16[1,4,4,384,384]{4,3,2,1,0:T(8,128)(2,1)} %get-tuple-element.75, bf16[1,4,4,384,384]{3,4,1,2,0:T(8,128)(2,1)} %collective-permute-done.1, bf16[1,4,384,384]{3,2,1,0:T(8,128)(2,1)} %get-tuple-element.58), kind=kOutput, calls=%fused_computation.11 | convolution fusion | flops 3626237952 | bytes 12976128 | tf_op jit(solution)/shard_map/ckqad,ckqed->cqae/dot_general | solution.py:119
  598.8 10.3 %fusion.3 = f32[4,384,384,1]{2,1,3,0:T(8,128)} fusion(bf16[1,4,4,384,384]{4,3,2,1,0:T(8,128)(2,1)} %get-tuple-element.76, bf16[1,4,4,384,384]{3,4,1,2,0:T(8,128)(2,1)} %collective-permute-done.2, bf16[1,4,384,384]{3,2,1,0:T(8,128)(2,1)S(1)} %copy-done.3), kind=kOutput, calls=%fused_computation.9 | convolution fusion | flops 3626237952 | bytes 12976128 | tf_op jit(solution)/shard_map/ckqad,ckqed->cqae/dot_general | solution.py:119
  609.1 10.9 %fusion.78 = f32[1,4,384,384]{3,2,1,0:T(8,128)} fusion(f32[4,384,384,1]{2,1,3,0:T(8,128)} %fusion.3, f32[4,384,384,1]{2,1,3,0:T(8,128)S(1)} %fusion.5, bf16[1,4,4,384,384]{4,3,2,1,0:T(8,128)(2,1)} %get-tuple-element.74, bf16[1,4,4,384,384]{3,4,1,2,0:T(8,128)(2,1)} %collective-permute-done, bf16[1,4,384,384]{3,2,1,0:T(8,128)(2,1)S(1)} %copy-done.3), kind=kOutput, calls=%fused_computation.99 | convolution fusion | flops 3627417600 | bytes 17694720 | tf_op jit(solution)/shard_map/ckqad,ckqed->cqae/dot_general | solution.py:119
  624.6 4.1 collective-permute-done.59
  631.9 3.0 collective-permute-done.60
  637.1 3.3 collective-permute-done.61
  642.5 4.2 collective-permute-done.62
  649.1 4.0 collective-permute-done.63
  655.3 3.4 collective-permute-done.64
  661.1 2.8 collective-permute-done.65
  666.4 3.6 collective-permute-done.66
  672.4 4.2 collective-permute-done.67
  678.8 3.7 collective-permute-done.68
  684.6 3.0 collective-permute-done.69
  689.8 3.0 collective-permute-done.70
  694.9 3.0 collective-permute-done.71
  700.1 3.0 collective-permute-done.72
  708.2 2.7 multiply_reduce_fusion
  710.9 2.7 stack.248
  (276 shorter events, 133.6 us)
Async XLA Ops:
  21.5 105.9 %collective-permute-start.2 = (bf16[1,4,4,384,384]{3,4,1,2,0:T(8,128)(2,1)}, bf16[1,4,4,384,384]{3,4,1,2,0:T(8,128)(2,1)}, u32[]{:S(2)}, u32[]{:S(2)}) collective-permute-start(bf16[1,4,4,384,384]{3,4,1,2,0:T(8,128)(2,1)} %convert_bitcast_fusion), channel_id=1, source_target_pairs={{16,0},{0,16},{17,1},{1,17},{18,2},{2,18},{19,3},{3,19},{20,4},{4,... | collective-permute-start | bytes 14155784 | tf_op jit(solution)/shard_map/ppermute | solution.py:13
  33.3 195.2 %collective-permute-start.1 = (bf16[1,4,4,384,384]{3,4,1,2,0:T(8,128)(2,1)}, bf16[1,4,4,384,384]{3,4,1,2,0:T(8,128)(2,1)}, u32[]{:S(2)}, u32[]{:S(2)}) collective-permute-start(bf16[1,4,4,384,384]{3,4,1,2,0:T(8,128)(2,1)} %convert_bitcast_fusion.1), channel_id=1, source_target_pairs={{16,0},{0,16},{17,1},{1,17},{18,2},{2,18},{19,3},{3,19},{20,4},{4,... | collective-permute-start | bytes 14155784 | tf_op jit(solution)/shard_map/ppermute | solution.py:13
  42.2 286.6 %collective-permute-start = (bf16[1,4,4,384,384]{3,4,1,2,0:T(8,128)(2,1)}, bf16[1,4,4,384,384]{3,4,1,2,0:T(8,128)(2,1)}, u32[]{:S(2)}, u32[]{:S(2)}) collective-permute-start(bf16[1,4,4,384,384]{3,4,1,2,0:T(8,128)(2,1)} %convert_bitcast_fusion.2), channel_id=1, source_target_pairs={{16,0},{0,16},{17,1},{1,17},{18,2},{2,18},{19,3},{3,19},{20,4},{4,... | collective-permute-start | bytes 14155784 | tf_op jit(solution)/shard_map/ppermute | solution.py:13
  342.4 14.8 %collective-permute-start.3 = (f32[96,384]{1,0:T(8,128)}, f32[96,384]{1,0:T(8,128)}, u32[]{:S(2)}, u32[]{:S(2)}) collective-permute-start(f32[96,384]{1,0:T(8,128)} %dynamic-slice_bitcast_fusion.5), channel_id=1, source_target_pairs={{0,4},{4,8},{8,12},{12,14},{14,10},{10,6},{6,2},{2,0},{1,5},{5,9},... | collective-permute-start | bytes 442376 | tf_op jit(solution)/shard_map/ppermute | solution.py:53
  357.0 5.2 collective-permute-start.17
  358.1 5.2 collective-permute-start.4
  362.2 6.2 collective-permute-start.18
  363.3 5.2 collective-permute-start.5
  368.4 14.3 %collective-permute-start.19 = (f32[96,384]{1,0:T(8,128)S(1)}, f32[96,384]{1,0:T(8,128)S(1)}, u32[]{:S(2)}, u32[]{:S(2)}) collective-permute-start(f32[96,384]{1,0:T(8,128)S(1)} %bitcast_add_fusion.39), channel_id=1, source_target_pairs={{0,2},{4,0},{8,4},{12,8},{14,12},{10,14},{6,10},{2,6},{1,3},{5,1},... | collective-permute-start | bytes 442376 | tf_op jit(solution)/shard_map/ppermute | solution.py:53
  368.6 18.7 %collective-permute-start.6 = (f32[96,384]{1,0:T(8,128)S(1)}, f32[96,384]{1,0:T(8,128)S(1)}, u32[]{:S(2)}, u32[]{:S(2)}) collective-permute-start(f32[96,384]{1,0:T(8,128)S(1)} %bitcast_add_fusion.45), channel_id=1, source_target_pairs={{0,4},{4,8},{8,12},{12,14},{14,10},{10,6},{6,2},{2,0},{1,5},{5,9},... | collective-permute-start | bytes 442376 | tf_op jit(solution)/shard_map/ppermute | solution.py:53
  382.7 6.2 collective-permute-start.20
  387.2 5.7 collective-permute-start.7
  388.9 5.3 collective-permute-start.21
  393.0 5.2 collective-permute-start.8
  394.2 5.2 collective-permute-start.22
  398.2 5.7 collective-permute-start.9
  399.4 6.2 collective-permute-start.23
  404.1 6.8 collective-permute-start.10
  405.8 6.3 collective-permute-start.24
  410.8 5.9 collective-permute-start.11
  412.0 5.5 collective-permute-start.25
  417.6 5.2 collective-permute-start.26
  421.8 5.6 collective-permute-start.13
  422.8 5.8 collective-permute-start.27
  428.6 5.2 collective-permute-start.28
  492.7 6.0 collective-permute-start.31
  494.3 6.0 collective-permute-start.45
  498.7 5.2 collective-permute-start.32
  500.3 5.2 collective-permute-start.46
  503.9 5.4 collective-permute-start.33
  505.5 5.4 collective-permute-start.47
  509.4 6.4 collective-permute-start.34
  511.0 6.5 collective-permute-start.48
  515.8 6.3 collective-permute-start.35
  517.5 6.2 collective-permute-start.49
  522.2 5.5 collective-permute-start.36
  523.7 5.5 collective-permute-start.50
  527.7 5.2 collective-permute-start.37
  529.3 5.3 collective-permute-start.51
  533.0 6.2 collective-permute-start.38
  534.7 6.0 collective-permute-start.52
  539.2 6.5 collective-permute-start.39
  540.7 6.5 collective-permute-start.53
  545.7 5.6 collective-permute-start.40
  547.2 5.7 collective-permute-start.54
  552.9 5.2 collective-permute-start.55
  622.5 6.2 collective-permute-start.59
  624.3 7.2 collective-permute-start.73
  629.7 5.2 collective-permute-start.60
  634.9 5.4 collective-permute-start.61
  636.8 5.4 collective-permute-start.75
  640.4 6.4 collective-permute-start.62
  642.3 6.6 collective-permute-start.76
  646.8 6.3 collective-permute-start.63
  648.9 6.1 collective-permute-start.77
  653.1 5.5 collective-permute-start.64
  655.0 5.4 collective-permute-start.78
  660.4 5.4 collective-permute-start.79
  664.0 5.9 collective-permute-start.66
  665.9 6.5 collective-permute-start.80
  669.9 6.7 collective-permute-start.67
  672.4 5.9 collective-permute-start.81
  676.7 5.9 collective-permute-start.68
  678.3 5.5 collective-permute-start.82
  (30 other events, 260.7 us)

commit v6 on v3

--- a/solution.py
+++ b/solution.py
@@ -66,6 +66,49 @@
     return jnp.stack(gathered).reshape(shape)
 
 
+def ring_sigma(moved, vector, right_ops, axis):
+    cycle = ring_order(axis)
+    count = len(cycle)
+    place = jnp.asarray([cycle.index(i) for i in range(count)], jnp.int32)[lax.axis_index(axis)]
+    _, ops_here, sectors, block_size, _ = moved.shape
+    rows = sectors * block_size // (2 * count)
+    forward = [(cycle[p], cycle[(p + 1) % count]) for p in range(count)]
+    backward = [(cycle[p], cycle[(p - 1) % count]) for p in range(count)]
+    routes = (forward, backward)
+    signs = (1, -1)
+
+    def chunk(half, index):
+        start = (half * count + index % count) * rows
+        sector, row = start // block_size, start % block_size
+        left = lax.dynamic_slice(moved, (0, 0, sector, row, 0), (1, ops_here, 1, rows, block_size))
+        vec = lax.dynamic_slice(vector, (0, sector, 0, 0), (1, 1, block_size, block_size))
+        right = lax.dynamic_slice(right_ops, (0, 0, sector, 0, 0), (1, ops_here, 1, block_size, block_size))
+        products = jnp.einsum(
+            "ckqab,cqbd->ckqad", left, vec, preferred_element_type=jnp.float32
+        ).astype(jnp.bfloat16)
+        return jnp.einsum(
+            "ckqad,ckqed->cqae", products, right, preferred_element_type=jnp.float32
+        ).reshape(rows, block_size)
+
+    moving = [chunk(h, place - signs[h]) for h in range(2)]
+    for step in range(count - 1):
+        for h in range(2):
+            arrived = lax.ppermute(moving[h], axis, routes[h])
+            moving[h] = arrived + chunk(h, place - signs[h] * (step + 2))
+    gathered = []
+    for h in range(2):
+        table = jnp.zeros((count, rows, block_size), jnp.float32)
+        table = lax.dynamic_update_index_in_dim(table, moving[h], place % count, 0)
+        current = moving[h]
+        for step in range(count - 1):
+            current = lax.ppermute(current, axis, routes[h])
+            table = lax.dynamic_update_index_in_dim(
+                table, current, (place - signs[h] * (step + 1)) % count, 0
+            )
+        gathered.append(table)
+    return jnp.stack(gathered).reshape(1, sectors, block_size, block_size)
+
+
 def gather_sector(values):
     count = lax.axis_size("sector")
     slots = jnp.zeros((count, values.shape[0]), jnp.float32)
@@ -105,13 +148,7 @@
     residual = None
     quotients = []
     for iteration in range(ITERS):
-        products = jnp.einsum(
-            "ckqab,cqbd->ckqad", shifted, vector, preferred_element_type=jnp.float32
-        ).astype(jnp.bfloat16)
-        partial_sigma = jnp.einsum(
-            "ckqad,ckqed->cqae", products, right_ops, preferred_element_type=jnp.float32
-        )
-        sigma_full = ring_sum(partial_sigma, "ops") * live
+        sigma_full = ring_sigma(shifted, vector, right_ops, "ops") * live
         vector_wide = vector.astype(jnp.float32)
         rayleigh, spread = quotient(vector_wide, sigma_full)
         quotients.append(rayleigh)

time: 718 us -> 826 us (1.15)
  matrix products: 81.2 us -> 266 us
  waiting for transfers between devices: 457 us -> 379 us
  starting transfers between devices: 99.5 us -> 91 us
    dot_general x3 -> x48, matrix products: 60.1 us -> 245 us  [chunk(): jnp.einsum('ckqad,ckqed->cqae', products, right, preferred_element_type=j...]
    ppermute x84, waiting for transfers between devices: 154 us -> 89.1 us  [the longest x42 76.3 us: ring_sigma(): current = lax.ppermute(current, axis, routes[h])]
    ppermute x1, waiting for transfers between devices: 303 us -> 290 us  [from_behind(): return lax.ppermute(block, axis, route)]
    ppermute x84, starting transfers between devices: 96.6 us -> 88.1 us  [the longest x42 47.1 us: ring_sigma(): arrived = lax.ppermute(moving[h], axis, routes[h])]
  transfers between devices with their start and end apart: 85 -> 85, of which waited for: 58 -> 36; matrix products, arithmetic and copies ran while one was open for 0% -> 29% of each run, Pallas kernels for 0% -> 0%
where the time goes in v6:
time: 826 us; the launch traced here: 818 us
  waiting for transfers between devices  379 us (46%)
  matrix products  266 us (32%)
  starting transfers between devices  91 us (11%)
  other arithmetic  30.7 us (4%)
  between operations  26.7 us (3%)
  local copies, waits for them, and re-layouts  17 us (2%)
    ppermute x1, waiting for transfers between devices, from_behind(): return lax.ppermute(block, axis, route)  290 us
    dot_general x48, matrix products, chunk(): jnp.einsum('ckqad,ckqed->cqae', products, right, preferred_element_type=j...  245 us
    ppermute x42, waiting for transfers between devices, ring_sigma(): current = lax.ppermute(current, axis, routes[h])  76.3 us
    ppermute x42, starting transfers between devices, ring_sigma(): arrived = lax.ppermute(moving[h], axis, routes[h])  47.1 us
    ppermute x42, starting transfers between devices, ring_sigma(): current = lax.ppermute(current, axis, routes[h])  41 us
    dot_general x1, matrix products, on_device(): jnp.einsum('cqba,ckqbd->ckqad', basis, half_env, preferred_element_type=j...  21.2 us
  transfers between devices with their start and end apart: 85, of which 36 were waited for; matrix products, arithmetic and copies ran while one was open for 29% of the time, Pallas kernels for 0%

profile of v6, /device:TPU:0, one launch (start us, length us, event | category | flops | bytes accessed | tf_op | source)
XLA Modules:
  0.0 817.8 jit_solution(621357043255876257)
XLA Ops:
  1.9 21.2 %convert_bitcast_fusion = bf16[1,12,4,384,384]{3,4,1,2,0:T(8,128)(2,1)} fusion(bf16[1,4,384,384]{3,2,1,0:T(8,128)(2,1)S(1)} %copy-done, bf16[1,12,4,384,384]{4,3,2,1,0:T(8,128)(2,1)} %param.15), kind=kOutput, calls=%fused_computation.4 | convolution fusion | flops 10885791744 | bytes 29491200 | tf_op jit(solution)/shard_map/cqba,ckqbd->ckqad/dot_general | solution.py:140
  40.3 290.0 %collective-permute-done = bf16[1,12,4,384,384]{3,4,1,2,0:T(8,128)(2,1)} collective-permute-done((bf16[1,12,4,384,384]{3,4,1,2,0:T(8,128)(2,1)}, bf16[1,12,4,384,384]{3,4,1,2,0:T(8,128)(2,1)}, u32[]{:S(2)}, u32[]{:S(2)}) %collective-permute-start) | collective-permute-done | bytes 14155808 | tf_op jit(solution)/shard_map/ppermute | solution.py:13
  330.4 4.8 fusion.319
  337.4 5.2 fusion.439
  342.9 5.2 fusion.334
  348.1 5.2 fusion.349
  355.0 5.2 fusion.364
  360.2 5.2 fusion.454
  367.6 4.8 fusion.379
  372.4 4.8 fusion.469
  379.7 5.2 fusion.394
  384.8 5.2 fusion.484
  392.2 5.2 fusion.409
  397.4 5.2 fusion.499
  404.8 5.2 fusion.424
  410.0 5.2 fusion.514
  417.8 5.2 fusion.544
  423.0 4.8 fusion.529
  430.1 4.0 collective-permute-done.21
  450.2 3.8 collective-permute-done.24
  471.5 3.6 collective-permute-done.28
  494.8 4.8 fusion.324
  501.8 5.2 fusion.444
  507.2 5.2 fusion.429
  512.4 5.2 fusion.339
  519.4 5.2 fusion.354
  524.6 5.2 fusion.459
  531.9 5.2 fusion.369
  537.1 4.8 fusion.474
  544.4 4.8 fusion.384
  549.2 5.2 fusion.489
  556.9 5.2 fusion.399
  562.1 5.2 fusion.504
  569.5 5.2 fusion.414
  574.6 5.2 fusion.519
  582.4 5.2 fusion.549
  587.6 4.8 fusion.534
  594.8 4.5 collective-permute-done.49
  601.5 3.7 collective-permute-done.50
  612.4 3.6 collective-permute-done.52
  618.2 4.4 collective-permute-done.53
  624.7 3.6 collective-permute-done.54
  633.9 4.7 collective-permute-done.56
  653.3 3.7 fusion.943
  657.0 4.8 fusion.329
  663.5 5.2 fusion.449
  669.3 5.2 fusion.434
  674.5 5.2 fusion.344
  681.1 5.2 fusion.359
  686.3 5.2 fusion.464
  693.7 5.2 fusion.374
  698.8 4.8 fusion.479
  706.1 4.8 fusion.389
  710.9 5.2 fusion.494
  718.3 5.2 fusion.404
  723.5 5.2 fusion.509
  730.9 5.2 fusion.419
  736.1 5.2 fusion.524
  743.7 5.2 fusion.554
  748.9 4.8 fusion.539
  756.0 4.2 collective-permute-done.77
  773.1 4.0 collective-permute-done.80
  779.3 4.3 collective-permute-done.81
  795.1 4.3 collective-permute-done.84
  (303 shorter events, 178.7 us)
Async XLA Ops:
  23.1 307.3 %collective-permute-start = (bf16[1,12,4,384,384]{3,4,1,2,0:T(8,128)(2,1)}, bf16[1,12,4,384,384]{3,4,1,2,0:T(8,128)(2,1)}, u32[]{:S(2)}, u32[]{:S(2)}) collective-permute-start(bf16[1,12,4,384,384]{3,4,1,2,0:T(8,128)(2,1)} %convert_bitcast_fusion), channel_id=1, source_target_pairs={{16,0},{0,16},{17,1},{1,17},{18,2},{2,18},{19,3},{3,19},{20,4},{4,... | collective-permute-start | bytes 42467336 | tf_op jit(solution)/shard_map/ppermute | solution.py:13
  335.2 18.0 %collective-permute-start.1 = (f32[96,384]{1,0:T(8,128)S(1)}, f32[96,384]{1,0:T(8,128)S(1)}, u32[]{:S(2)}, u32[]{:S(2)}) collective-permute-start(f32[96,384]{1,0:T(8,128)S(1)} %fusion.319), channel_id=1, source_target_pairs={{0,4},{4,8},{8,12},{12,14},{14,10},{10,6},{6,2},{2,0},{1,5},{5,9},... | collective-permute-start | bytes 442376 | tf_op jit(solution)/shard_map/ppermute | solution.py:96
  342.6 22.8 %collective-permute-start.15 = (f32[96,384]{1,0:T(8,128)S(1)}, f32[96,384]{1,0:T(8,128)S(1)}, u32[]{:S(2)}, u32[]{:S(2)}) collective-permute-start(f32[96,384]{1,0:T(8,128)S(1)} %fusion.439), channel_id=1, source_target_pairs={{0,2},{4,0},{8,4},{12,8},{14,12},{10,14},{6,10},{2,6},{1,3},{5,1},... | collective-permute-start | bytes 442376 | tf_op jit(solution)/shard_map/ppermute | solution.py:96
  353.3 12.2 %collective-permute-start.2 = (f32[96,384]{1,0:T(8,128)S(1)}, f32[96,384]{1,0:T(8,128)S(1)}, u32[]{:S(2)}, u32[]{:S(2)}) collective-permute-start(f32[96,384]{1,0:T(8,128)S(1)} %add.1176), channel_id=1, source_target_pairs={{0,4},{4,8},{8,12},{12,14},{14,10},{10,6},{6,2},{2,0},{1,5},{5,9},... | collective-permute-start | bytes 442376 | tf_op jit(solution)/shard_map/ppermute | solution.py:96
  365.4 11.8 %collective-permute-start.16 = (f32[96,384]{1,0:T(8,128)S(1)}, f32[96,384]{1,0:T(8,128)S(1)}, u32[]{:S(2)}, u32[]{:S(2)}) collective-permute-start(f32[96,384]{1,0:T(8,128)S(1)} %add.1226), channel_id=1, source_target_pairs={{0,2},{4,0},{8,4},{12,8},{14,12},{10,14},{6,10},{2,6},{1,3},{5,1},... | collective-permute-start | bytes 442376 | tf_op jit(solution)/shard_map/ppermute | solution.py:96
  365.5 12.6 %collective-permute-start.3 = (f32[96,384]{1,0:T(8,128)S(1)}, f32[96,384]{1,0:T(8,128)S(1)}, u32[]{:S(2)}, u32[]{:S(2)}) collective-permute-start(f32[96,384]{1,0:T(8,128)S(1)} %add.1181), channel_id=1, source_target_pairs={{0,4},{4,8},{8,12},{12,14},{14,10},{10,6},{6,2},{2,0},{1,5},{5,9},... | collective-permute-start | bytes 442376 | tf_op jit(solution)/shard_map/ppermute | solution.py:96
  377.3 12.8 %collective-permute-start.17 = (f32[96,384]{1,0:T(8,128)S(1)}, f32[96,384]{1,0:T(8,128)S(1)}, u32[]{:S(2)}, u32[]{:S(2)}) collective-permute-start(f32[96,384]{1,0:T(8,128)S(1)} %add.1232), channel_id=1, source_target_pairs={{0,2},{4,0},{8,4},{12,8},{14,12},{10,14},{6,10},{2,6},{1,3},{5,1},... | collective-permute-start | bytes 442376 | tf_op jit(solution)/shard_map/ppermute | solution.py:96
  378.1 12.4 %collective-permute-start.4 = (f32[96,384]{1,0:T(8,128)S(1)}, f32[96,384]{1,0:T(8,128)S(1)}, u32[]{:S(2)}, u32[]{:S(2)}) collective-permute-start(f32[96,384]{1,0:T(8,128)S(1)} %add.1186), channel_id=1, source_target_pairs={{0,4},{4,8},{8,12},{12,14},{14,10},{10,6},{6,2},{2,0},{1,5},{5,9},... | collective-permute-start | bytes 442376 | tf_op jit(solution)/shard_map/ppermute | solution.py:96
  390.1 12.5 %collective-permute-start.18 = (f32[96,384]{1,0:T(8,128)S(1)}, f32[96,384]{1,0:T(8,128)S(1)}, u32[]{:S(2)}, u32[]{:S(2)}) collective-permute-start(f32[96,384]{1,0:T(8,128)S(1)} %add.1238), channel_id=1, source_target_pairs={{0,2},{4,0},{8,4},{12,8},{14,12},{10,14},{6,10},{2,6},{1,3},{5,1},... | collective-permute-start | bytes 442376 | tf_op jit(solution)/shard_map/ppermute | solution.py:96
  390.5 12.9 %collective-permute-start.5 = (f32[96,384]{1,0:T(8,128)S(1)}, f32[96,384]{1,0:T(8,128)S(1)}, u32[]{:S(2)}, u32[]{:S(2)}) collective-permute-start(f32[96,384]{1,0:T(8,128)S(1)} %add.1191), channel_id=1, source_target_pairs={{0,4},{4,8},{8,12},{12,14},{14,10},{10,6},{6,2},{2,0},{1,5},{5,9},... | collective-permute-start | bytes 442376 | tf_op jit(solution)/shard_map/ppermute | solution.py:96
  402.7 12.5 %collective-permute-start.19 = (f32[96,384]{1,0:T(8,128)S(1)}, f32[96,384]{1,0:T(8,128)S(1)}, u32[]{:S(2)}, u32[]{:S(2)}) collective-permute-start(f32[96,384]{1,0:T(8,128)S(1)} %add.1244), channel_id=1, source_target_pairs={{0,2},{4,0},{8,4},{12,8},{14,12},{10,14},{6,10},{2,6},{1,3},{5,1},... | collective-permute-start | bytes 442376 | tf_op jit(solution)/shard_map/ppermute | solution.py:96
  403.4 12.2 %collective-permute-start.6 = (f32[96,384]{1,0:T(8,128)S(1)}, f32[96,384]{1,0:T(8,128)S(1)}, u32[]{:S(2)}, u32[]{:S(2)}) collective-permute-start(f32[96,384]{1,0:T(8,128)S(1)} %add.1196), channel_id=1, source_target_pairs={{0,4},{4,8},{8,12},{12,14},{14,10},{10,6},{6,2},{2,0},{1,5},{5,9},... | collective-permute-start | bytes 442376 | tf_op jit(solution)/shard_map/ppermute | solution.py:96
  415.2 12.6 %collective-permute-start.20 = (f32[96,384]{1,0:T(8,128)S(1)}, f32[96,384]{1,0:T(8,128)S(1)}, u32[]{:S(2)}, u32[]{:S(2)}) collective-permute-start(f32[96,384]{1,0:T(8,128)S(1)} %add.1250), channel_id=1, source_target_pairs={{0,2},{4,0},{8,4},{12,8},{14,12},{10,14},{6,10},{2,6},{1,3},{5,1},... | collective-permute-start | bytes 442376 | tf_op jit(solution)/shard_map/ppermute | solution.py:96
  415.6 12.6 %collective-permute-start.7 = (f32[96,384]{1,0:T(8,128)S(1)}, f32[96,384]{1,0:T(8,128)S(1)}, u32[]{:S(2)}, u32[]{:S(2)}) collective-permute-start(f32[96,384]{1,0:T(8,128)S(1)} %add.1201), channel_id=1, source_target_pairs={{0,4},{4,8},{8,12},{12,14},{14,10},{10,6},{6,2},{2,0},{1,5},{5,9},... | collective-permute-start | bytes 442376 | tf_op jit(solution)/shard_map/ppermute | solution.py:96
  427.9 6.3 collective-permute-start.21
  428.4 8.6 %collective-permute-start.8 = (f32[96,384]{1,0:T(8,128)S(1)}, f32[96,384]{1,0:T(8,128)S(1)}, u32[]{:S(2)}, u32[]{:S(2)}) collective-permute-start(f32[96,384]{1,0:T(8,128)S(1)} %get-tuple-element.68), channel_id=1, source_target_pairs={{0,4},{4,8},{8,12},{12,14},{14,10},{10,6},{6,2},{2,0},{1,5},{5,9},... | collective-permute-start | bytes 442376 | tf_op jit(solution)/shard_map/ppermute | solution.py:104
  441.1 6.1 collective-permute-start.23
  442.4 6.2 collective-permute-start.10
  447.1 6.8 collective-permute-start.24
  448.6 6.9 collective-permute-start.11
  454.0 5.8 collective-permute-start.25
  455.5 5.7 collective-permute-start.12
  499.7 18.0 %collective-permute-start.29 = (f32[96,384]{1,0:T(8,128)S(1)}, f32[96,384]{1,0:T(8,128)S(1)}, u32[]{:S(2)}, u32[]{:S(2)}) collective-permute-start(f32[96,384]{1,0:T(8,128)S(1)} %fusion.324), channel_id=1, source_target_pairs={{0,4},{4,8},{8,12},{12,14},{14,10},{10,6},{6,2},{2,0},{1,5},{5,9},... | collective-permute-start | bytes 442376 | tf_op jit(solution)/shard_map/ppermute | solution.py:96
  507.0 22.8 %collective-permute-start.43 = (f32[96,384]{1,0:T(8,128)S(1)}, f32[96,384]{1,0:T(8,128)S(1)}, u32[]{:S(2)}, u32[]{:S(2)}) collective-permute-start(f32[96,384]{1,0:T(8,128)S(1)} %fusion.444), channel_id=1, source_target_pairs={{0,2},{4,0},{8,4},{12,8},{14,12},{10,14},{6,10},{2,6},{1,3},{5,1},... | collective-permute-start | bytes 442376 | tf_op jit(solution)/shard_map/ppermute | solution.py:96
  517.7 12.6 %collective-permute-start.30 = (f32[96,384]{1,0:T(8,128)S(1)}, f32[96,384]{1,0:T(8,128)S(1)}, u32[]{:S(2)}, u32[]{:S(2)}) collective-permute-start(f32[96,384]{1,0:T(8,128)S(1)} %add.1276), channel_id=1, source_target_pairs={{0,4},{4,8},{8,12},{12,14},{14,10},{10,6},{6,2},{2,0},{1,5},{5,9},... | collective-permute-start | bytes 442376 | tf_op jit(solution)/shard_map/ppermute | solution.py:96
  529.8 12.2 %collective-permute-start.44 = (f32[96,384]{1,0:T(8,128)S(1)}, f32[96,384]{1,0:T(8,128)S(1)}, u32[]{:S(2)}, u32[]{:S(2)}) collective-permute-start(f32[96,384]{1,0:T(8,128)S(1)} %add.1326), channel_id=1, source_target_pairs={{0,2},{4,0},{8,4},{12,8},{14,12},{10,14},{6,10},{2,6},{1,3},{5,1},... | collective-permute-start | bytes 442376 | tf_op jit(solution)/shard_map/ppermute | solution.py:96
  530.3 12.2 %collective-permute-start.31 = (f32[96,384]{1,0:T(8,128)S(1)}, f32[96,384]{1,0:T(8,128)S(1)}, u32[]{:S(2)}, u32[]{:S(2)}) collective-permute-start(f32[96,384]{1,0:T(8,128)S(1)} %add.1281), channel_id=1, source_target_pairs={{0,4},{4,8},{8,12},{12,14},{14,10},{10,6},{6,2},{2,0},{1,5},{5,9},... | collective-permute-start | bytes 442376 | tf_op jit(solution)/shard_map/ppermute | solution.py:96
  542.0 12.4 %collective-permute-start.45 = (f32[96,384]{1,0:T(8,128)S(1)}, f32[96,384]{1,0:T(8,128)S(1)}, u32[]{:S(2)}, u32[]{:S(2)}) collective-permute-start(f32[96,384]{1,0:T(8,128)S(1)} %add.1332), channel_id=1, source_target_pairs={{0,2},{4,0},{8,4},{12,8},{14,12},{10,14},{6,10},{2,6},{1,3},{5,1},... | collective-permute-start | bytes 442376 | tf_op jit(solution)/shard_map/ppermute | solution.py:96
  542.5 12.4 %collective-permute-start.32 = (f32[96,384]{1,0:T(8,128)S(1)}, f32[96,384]{1,0:T(8,128)S(1)}, u32[]{:S(2)}, u32[]{:S(2)}) collective-permute-start(f32[96,384]{1,0:T(8,128)S(1)} %add.1286), channel_id=1, source_target_pairs={{0,4},{4,8},{8,12},{12,14},{14,10},{10,6},{6,2},{2,0},{1,5},{5,9},... | collective-permute-start | bytes 442376 | tf_op jit(solution)/shard_map/ppermute | solution.py:96
  554.4 12.8 %collective-permute-start.46 = (f32[96,384]{1,0:T(8,128)S(1)}, f32[96,384]{1,0:T(8,128)S(1)}, u32[]{:S(2)}, u32[]{:S(2)}) collective-permute-start(f32[96,384]{1,0:T(8,128)S(1)} %add.1338), channel_id=1, source_target_pairs={{0,2},{4,0},{8,4},{12,8},{14,12},{10,14},{6,10},{2,6},{1,3},{5,1},... | collective-permute-start | bytes 442376 | tf_op jit(solution)/shard_map/ppermute | solution.py:96
  554.9 12.6 %collective-permute-start.33 = (f32[96,384]{1,0:T(8,128)S(1)}, f32[96,384]{1,0:T(8,128)S(1)}, u32[]{:S(2)}, u32[]{:S(2)}) collective-permute-start(f32[96,384]{1,0:T(8,128)S(1)} %add.1291), channel_id=1, source_target_pairs={{0,4},{4,8},{8,12},{12,14},{14,10},{10,6},{6,2},{2,0},{1,5},{5,9},... | collective-permute-start | bytes 442376 | tf_op jit(solution)/shard_map/ppermute | solution.py:96
  567.3 12.5 %collective-permute-start.47 = (f32[96,384]{1,0:T(8,128)S(1)}, f32[96,384]{1,0:T(8,128)S(1)}, u32[]{:S(2)}, u32[]{:S(2)}) collective-permute-start(f32[96,384]{1,0:T(8,128)S(1)} %add.1344), channel_id=1, source_target_pairs={{0,2},{4,0},{8,4},{12,8},{14,12},{10,14},{6,10},{2,6},{1,3},{5,1},... | collective-permute-start | bytes 442376 | tf_op jit(solution)/shard_map/ppermute | solution.py:96
  567.5 12.6 %collective-permute-start.34 = (f32[96,384]{1,0:T(8,128)S(1)}, f32[96,384]{1,0:T(8,128)S(1)}, u32[]{:S(2)}, u32[]{:S(2)}) collective-permute-start(f32[96,384]{1,0:T(8,128)S(1)} %add.1296), channel_id=1, source_target_pairs={{0,4},{4,8},{8,12},{12,14},{14,10},{10,6},{6,2},{2,0},{1,5},{5,9},... | collective-permute-start | bytes 442376 | tf_op jit(solution)/shard_map/ppermute | solution.py:96
  579.9 12.6 %collective-permute-start.48 = (f32[96,384]{1,0:T(8,128)S(1)}, f32[96,384]{1,0:T(8,128)S(1)}, u32[]{:S(2)}, u32[]{:S(2)}) collective-permute-start(f32[96,384]{1,0:T(8,128)S(1)} %add.1350), channel_id=1, source_target_pairs={{0,2},{4,0},{8,4},{12,8},{14,12},{10,14},{6,10},{2,6},{1,3},{5,1},... | collective-permute-start | bytes 442376 | tf_op jit(solution)/shard_map/ppermute | solution.py:96
  580.1 12.6 %collective-permute-start.35 = (f32[96,384]{1,0:T(8,128)S(1)}, f32[96,384]{1,0:T(8,128)S(1)}, u32[]{:S(2)}, u32[]{:S(2)}) collective-permute-start(f32[96,384]{1,0:T(8,128)S(1)} %add.1301), channel_id=1, source_target_pairs={{0,4},{4,8},{8,12},{12,14},{14,10},{10,6},{6,2},{2,0},{1,5},{5,9},... | collective-permute-start | bytes 442376 | tf_op jit(solution)/shard_map/ppermute | solution.py:96
  592.5 6.8 collective-permute-start.49
  592.8 6.7 collective-permute-start.36
  599.4 5.8 collective-permute-start.50
  599.5 6.0 collective-permute-start.37
  610.3 5.8 collective-permute-start.52
  616.1 6.5 collective-permute-start.53
  616.1 6.7 collective-permute-start.40
  622.6 5.7 collective-permute-start.54
  622.8 5.9 collective-permute-start.41
  661.8 17.9 %collective-permute-start.57 = (f32[96,384]{1,0:T(8,128)S(1)}, f32[96,384]{1,0:T(8,128)S(1)}, u32[]{:S(2)}, u32[]{:S(2)}) collective-permute-start(f32[96,384]{1,0:T(8,128)S(1)} %fusion.329), channel_id=1, source_target_pairs={{0,4},{4,8},{8,12},{12,14},{14,10},{10,6},{6,2},{2,0},{1,5},{5,9},... | collective-permute-start | bytes 442376 | tf_op jit(solution)/shard_map/ppermute | solution.py:96
  668.7 22.8 %collective-permute-start.71 = (f32[96,384]{1,0:T(8,128)S(1)}, f32[96,384]{1,0:T(8,128)S(1)}, u32[]{:S(2)}, u32[]{:S(2)}) collective-permute-start(f32[96,384]{1,0:T(8,128)S(1)} %fusion.449), channel_id=1, source_target_pairs={{0,2},{4,0},{8,4},{12,8},{14,12},{10,14},{6,10},{2,6},{1,3},{5,1},... | collective-permute-start | bytes 442376 | tf_op jit(solution)/shard_map/ppermute | solution.py:96
  679.7 12.6 %collective-permute-start.58 = (f32[96,384]{1,0:T(8,128)S(1)}, f32[96,384]{1,0:T(8,128)S(1)}, u32[]{:S(2)}, u32[]{:S(2)}) collective-permute-start(f32[96,384]{1,0:T(8,128)S(1)} %add.1375), channel_id=1, source_target_pairs={{0,4},{4,8},{8,12},{12,14},{14,10},{10,6},{6,2},{2,0},{1,5},{5,9},... | collective-permute-start | bytes 442376 | tf_op jit(solution)/shard_map/ppermute | solution.py:96
  691.5 12.2 %collective-permute-start.72 = (f32[96,384]{1,0:T(8,128)S(1)}, f32[96,384]{1,0:T(8,128)S(1)}, u32[]{:S(2)}, u32[]{:S(2)}) collective-permute-start(f32[96,384]{1,0:T(8,128)S(1)} %add.1425), channel_id=1, source_target_pairs={{0,2},{4,0},{8,4},{12,8},{14,12},{10,14},{6,10},{2,6},{1,3},{5,1},... | collective-permute-start | bytes 442376 | tf_op jit(solution)/shard_map/ppermute | solution.py:96
  692.3 12.2 %collective-permute-start.59 = (f32[96,384]{1,0:T(8,128)S(1)}, f32[96,384]{1,0:T(8,128)S(1)}, u32[]{:S(2)}, u32[]{:S(2)}) collective-permute-start(f32[96,384]{1,0:T(8,128)S(1)} %add.1380), channel_id=1, source_target_pairs={{0,4},{4,8},{8,12},{12,14},{14,10},{10,6},{6,2},{2,0},{1,5},{5,9},... | collective-permute-start | bytes 442376 | tf_op jit(solution)/shard_map/ppermute | solution.py:96
  703.7 12.4 %collective-permute-start.73 = (f32[96,384]{1,0:T(8,128)S(1)}, f32[96,384]{1,0:T(8,128)S(1)}, u32[]{:S(2)}, u32[]{:S(2)}) collective-permute-start(f32[96,384]{1,0:T(8,128)S(1)} %add.1431), channel_id=1, source_target_pairs={{0,2},{4,0},{8,4},{12,8},{14,12},{10,14},{6,10},{2,6},{1,3},{5,1},... | collective-permute-start | bytes 442376 | tf_op jit(solution)/shard_map/ppermute | solution.py:96
  704.5 12.4 %collective-permute-start.60 = (f32[96,384]{1,0:T(8,128)S(1)}, f32[96,384]{1,0:T(8,128)S(1)}, u32[]{:S(2)}, u32[]{:S(2)}) collective-permute-start(f32[96,384]{1,0:T(8,128)S(1)} %add.1385), channel_id=1, source_target_pairs={{0,4},{4,8},{8,12},{12,14},{14,10},{10,6},{6,2},{2,0},{1,5},{5,9},... | collective-permute-start | bytes 442376 | tf_op jit(solution)/shard_map/ppermute | solution.py:96
  716.2 12.5 %collective-permute-start.74 = (f32[96,384]{1,0:T(8,128)S(1)}, f32[96,384]{1,0:T(8,128)S(1)}, u32[]{:S(2)}, u32[]{:S(2)}) collective-permute-start(f32[96,384]{1,0:T(8,128)S(1)} %add.1437), channel_id=1, source_target_pairs={{0,2},{4,0},{8,4},{12,8},{14,12},{10,14},{6,10},{2,6},{1,3},{5,1},... | collective-permute-start | bytes 442376 | tf_op jit(solution)/shard_map/ppermute | solution.py:96
  716.9 12.6 %collective-permute-start.61 = (f32[96,384]{1,0:T(8,128)S(1)}, f32[96,384]{1,0:T(8,128)S(1)}, u32[]{:S(2)}, u32[]{:S(2)}) collective-permute-start(f32[96,384]{1,0:T(8,128)S(1)} %add.1390), channel_id=1, source_target_pairs={{0,4},{4,8},{8,12},{12,14},{14,10},{10,6},{6,2},{2,0},{1,5},{5,9},... | collective-permute-start | bytes 442376 | tf_op jit(solution)/shard_map/ppermute | solution.py:96
  728.7 12.5 %collective-permute-start.75 = (f32[96,384]{1,0:T(8,128)S(1)}, f32[96,384]{1,0:T(8,128)S(1)}, u32[]{:S(2)}, u32[]{:S(2)}) collective-permute-start(f32[96,384]{1,0:T(8,128)S(1)} %add.1443), channel_id=1, source_target_pairs={{0,2},{4,0},{8,4},{12,8},{14,12},{10,14},{6,10},{2,6},{1,3},{5,1},... | collective-permute-start | bytes 442376 | tf_op jit(solution)/shard_map/ppermute | solution.py:96
  729.5 12.6 %collective-permute-start.62 = (f32[96,384]{1,0:T(8,128)S(1)}, f32[96,384]{1,0:T(8,128)S(1)}, u32[]{:S(2)}, u32[]{:S(2)}) collective-permute-start(f32[96,384]{1,0:T(8,128)S(1)} %add.1395), channel_id=1, source_target_pairs={{0,4},{4,8},{8,12},{12,14},{14,10},{10,6},{6,2},{2,0},{1,5},{5,9},... | collective-permute-start | bytes 442376 | tf_op jit(solution)/shard_map/ppermute | solution.py:96
  741.3 12.4 %collective-permute-start.76 = (f32[96,384]{1,0:T(8,128)S(1)}, f32[96,384]{1,0:T(8,128)S(1)}, u32[]{:S(2)}, u32[]{:S(2)}) collective-permute-start(f32[96,384]{1,0:T(8,128)S(1)} %add.1449), channel_id=1, source_target_pairs={{0,2},{4,0},{8,4},{12,8},{14,12},{10,14},{6,10},{2,6},{1,3},{5,1},... | collective-permute-start | bytes 442376 | tf_op jit(solution)/shard_map/ppermute | solution.py:96
  742.1 12.5 %collective-permute-start.63 = (f32[96,384]{1,0:T(8,128)S(1)}, f32[96,384]{1,0:T(8,128)S(1)}, u32[]{:S(2)}, u32[]{:S(2)}) collective-permute-start(f32[96,384]{1,0:T(8,128)S(1)} %add.1400), channel_id=1, source_target_pairs={{0,4},{4,8},{8,12},{12,14},{14,10},{10,6},{6,2},{2,0},{1,5},{5,9},... | collective-permute-start | bytes 442376 | tf_op jit(solution)/shard_map/ppermute | solution.py:96
  753.8 6.5 collective-permute-start.77
  754.6 6.5 collective-permute-start.64
  771.0 6.1 collective-permute-start.80
  771.8 6.4 collective-permute-start.67
  777.1 6.4 collective-permute-start.81
  778.2 6.2 collective-permute-start.68
  784.3 5.6 collective-permute-start.69
  (30 other events, 244.3 us)

commit v7 on v3

--- a/solution.py
+++ b/solution.py
@@ -68,9 +68,8 @@
 
 def gather_sector(values):
     count = lax.axis_size("sector")
-    slots = jnp.zeros((count, values.shape[0]), jnp.float32)
-    slots = slots.at[lax.axis_index("sector")].set(values)
-    return lax.psum(slots, "sector")
+    mine = jnp.arange(count)[:, None] == lax.axis_index("sector")
+    return lax.psum(jnp.where(mine, values[None, :], 0.0), "sector")
 
 
 def quotient(vector_wide, sigma_full):

time: 718 us -> 702 us (0.978)
  starting transfers between devices: 99.5 us -> 91.2 us
    ppermute x42, starting transfers between devices: 51.3 us -> 43 us  [ring_sum(): current = lax.ppermute(current, axis, routes[h])]
  transfers between devices with their start and end apart: 85 -> 85, of which waited for: 58 -> 59; matrix products, arithmetic and copies ran while one was open for 0% -> 0% of each run, Pallas kernels for 0% -> 0%
where the time goes in v7:
time: 702 us; the launch traced here: 701 us
  waiting for transfers between devices  456 us (65%)
  starting transfers between devices  91.2 us (13%)
  matrix products  81.3 us (12%)
  between operations  25.2 us (4%)
  other arithmetic  23.1 us (3%)
  local copies, waits for them, and re-layouts  17 us (2%)
  blocking collectives  7.34 us (1%)
    ppermute x1, waiting for transfers between devices, from_behind(): return lax.ppermute(block, axis, route)  303 us
    ppermute x42, waiting for transfers between devices, ring_sum(): current = lax.ppermute(current, axis, routes[h])  77.5 us
    ppermute x42, waiting for transfers between devices, ring_sum(): arrived = lax.ppermute(moving[h], axis, routes[h])  75.2 us
    dot_general x3, matrix products, on_device(): jnp.einsum('ckqad,ckqed->cqae', products, right_ops, preferred_element_ty...  60.1 us
    ppermute x42, starting transfers between devices, ring_sum(): arrived = lax.ppermute(moving[h], axis, routes[h])  45.2 us
    ppermute x42, starting transfers between devices, ring_sum(): current = lax.ppermute(current, axis, routes[h])  43 us
    dot_general x1, matrix products, on_device(): jnp.einsum('cqba,ckqbd->ckqad', basis, half_env, preferred_element_type=j...  21.2 us
  transfers between devices with their start and end apart: 85, of which 59 were waited for; matrix products, arithmetic and copies ran while one was open for 0% of the time, Pallas kernels for 0%

profile of v7, /device:TPU:0, one launch (start us, length us, event | category | flops | bytes accessed | tf_op | source)
XLA Modules:
  0.0 700.8 jit_solution(13306984614487514268)
XLA Ops:
  1.9 21.2 %convert_bitcast_fusion = bf16[1,12,4,384,384]{3,4,1,2,0:T(8,128)(2,1)} fusion(bf16[1,4,384,384]{3,2,1,0:T(8,128)(2,1)S(1)} %copy-done, bf16[1,12,4,384,384]{4,3,2,1,0:T(8,128)(2,1)} %param.9), kind=kOutput, calls=%fused_computation.19 | convolution fusion | flops 10885791744 | bytes 29491200 | tf_op jit(solution)/shard_map/cqba,ckqbd->ckqad/dot_general | solution.py:96
  23.1 2.9 collective-permute-start
  27.4 303.0 %collective-permute-done = bf16[1,12,4,384,384]{3,4,1,2,0:T(8,128)(2,1)} collective-permute-done((bf16[1,12,4,384,384]{3,4,1,2,0:T(8,128)(2,1)}, bf16[1,12,4,384,384]{3,4,1,2,0:T(8,128)(2,1)}, u32[]{:S(2)}, u32[]{:S(2)}) %collective-permute-start) | collective-permute-done | bytes 14155808 | tf_op jit(solution)/shard_map/ppermute | solution.py:13
  330.4 20.6 %fusion.59 = f32[4,384,384]{2,1,0:T(8,128)} fusion(bf16[1,12,4,384,384]{3,4,1,2,0:T(8,128)(2,1)} %collective-permute-done, bf16[1,4,384,384]{3,2,1,0:T(8,128)(2,1)S(1)} %copy-done.2, pred[4,384]{1,0:T(4,128)(4,1)S(1)} %iota_compare_fusion, bf16[1,12,4,384,384]{4,3,2,1,0:T(8,128)(2,1)} %param.10), kind=kOutput, calls=%fused_computation.64 | convolution fusion | flops 10881073152 | bytes 31852032 | tf_op jit(solution)/shard_map/ckqad,ckqed->cqae/dot_general | solution.py:110
  368.8 3.0 collective-permute-done.15
  372.1 1.9 collective-permute-start.3
  374.0 4.0 collective-permute-done.16
  378.3 2.2 collective-permute-start.4
  380.5 3.9 collective-permute-done.17
  386.6 3.5 collective-permute-done.18
  392.3 3.0 collective-permute-done.19
  397.5 3.4 collective-permute-done.20
  401.6 1.9 collective-permute-start.8
  403.5 4.2 collective-permute-done.21
  409.9 3.5 collective-permute-done.22
  415.5 3.0 collective-permute-done.23
  420.7 3.9 collective-permute-done.24
  424.6 2.3 collective-permute-start.12
  426.9 4.1 collective-permute-done.25
  431.1 2.1 collective-permute-start.13
  433.2 3.0 collective-permute-done.26
  436.3 2.0 collective-permute-start.14
  438.3 3.0 collective-permute-done.27
  441.4 5.0 collective-permute-done.28
  451.6 2.1 fusion.47
  453.7 2.7 stack.202
  456.4 2.4 psum.21
  462.1 2.1 fusion.50
  464.2 19.3 %fusion.66 = f32[4,384,384]{2,1,0:T(8,128)S(1)} fusion(bf16[1,12,4,384,384]{3,4,1,2,0:T(8,128)(2,1)} %collective-permute-done, bf16[1,4,384,384]{3,2,1,0:T(8,128)(2,1)S(1)} %fusion.50, bf16[1,12,4,384,384]{4,3,2,1,0:T(8,128)(2,1)} %param.10), kind=kOutput, calls=%fused_computation.65 | convolution fusion | flops 10878713856 | bytes 31850496 | tf_op jit(solution)/shard_map/ckqad,ckqed->cqae/dot_general | solution.py:110
  485.8 3.8 collective-permute-done.29
  491.9 3.0 collective-permute-done.30
  497.1 3.3 collective-permute-done.31
  502.5 4.2 collective-permute-done.32
  508.9 4.2 collective-permute-done.33
  515.3 3.4 collective-permute-done.34
  520.8 3.0 collective-permute-done.35
  526.3 3.8 collective-permute-done.36
  532.2 4.5 collective-permute-done.37
  538.8 3.6 collective-permute-done.38
  544.5 3.0 collective-permute-done.39
  549.7 3.0 collective-permute-done.40
  554.8 3.0 collective-permute-done.41
  560.2 2.8 collective-permute-done.42
  570.5 2.7 stack.225
  573.3 2.4 psum.22
  578.9 2.4 fusion.90
  581.4 20.2 %fusion.73 = f32[4,384,384]{2,1,0:T(8,128)} fusion(bf16[1,12,4,384,384]{3,4,1,2,0:T(8,128)(2,1)} %collective-permute-done, bf16[1,4,384,384]{3,2,1,0:T(8,128)(2,1)} %get-tuple-element.22, bf16[1,12,4,384,384]{4,3,2,1,0:T(8,128)(2,1)} %param.10), kind=kOutput, calls=%fused_computation.66 | convolution fusion | flops 10878713856 | bytes 31850496 | tf_op jit(solution)/shard_map/ckqad,ckqed->cqae/dot_general | solution.py:110
  605.6 3.8 collective-permute-done.57
  611.6 3.0 collective-permute-done.58
  616.8 3.3 collective-permute-done.59
  622.2 4.2 collective-permute-done.60
  628.8 4.0 collective-permute-done.61
  635.0 3.4 collective-permute-done.62
  640.5 3.0 collective-permute-done.63
  646.0 3.9 collective-permute-done.64
  652.0 4.3 collective-permute-done.65
  658.5 3.5 collective-permute-done.66
  664.1 3.0 collective-permute-done.67
  669.2 3.0 collective-permute-done.68
  674.4 3.0 collective-permute-done.69
  679.5 3.0 collective-permute-done.70
  688.7 2.7 multiply_reduce_fusion
  691.4 2.6 stack.248
  694.1 2.4 psum.23
  (253 shorter events, 103.4 us)
Async XLA Ops:
  23.1 307.3 %collective-permute-start = (bf16[1,12,4,384,384]{3,4,1,2,0:T(8,128)(2,1)}, bf16[1,12,4,384,384]{3,4,1,2,0:T(8,128)(2,1)}, u32[]{:S(2)}, u32[]{:S(2)}) collective-permute-start(bf16[1,12,4,384,384]{3,4,1,2,0:T(8,128)(2,1)} %convert_bitcast_fusion), channel_id=1, source_target_pairs={{16,0},{0,16},{17,1},{1,17},{18,2},{2,18},{19,3},{3,19},{20,4},{4,... | collective-permute-start | bytes 42467336 | tf_op jit(solution)/shard_map/ppermute | solution.py:13
  352.8 14.1 %collective-permute-start.1 = (f32[96,384]{1,0:T(8,128)S(1)}, f32[96,384]{1,0:T(8,128)S(1)}, u32[]{:S(2)}, u32[]{:S(2)}) collective-permute-start(f32[96,384]{1,0:T(8,128)S(1)} %dynamic-slice_bitcast_fusion.5), channel_id=1, source_target_pairs={{0,4},{4,8},{8,12},{12,14},{14,10},{10,6},{6,2},{2,0},{1,5},{5,9},... | collective-permute-start | bytes 442376 | tf_op jit(solution)/shard_map/ppermute | solution.py:53
  366.6 5.2 collective-permute-start.15
  366.9 5.2 collective-permute-start.2
  371.9 6.2 collective-permute-start.16
  372.1 6.1 collective-permute-start.3
  378.1 6.3 collective-permute-start.17
  378.3 6.6 collective-permute-start.4
  384.4 5.7 collective-permute-start.18
  384.9 5.8 collective-permute-start.5
  390.1 5.2 collective-permute-start.19
  390.7 5.2 collective-permute-start.6
  395.3 5.5 collective-permute-start.20
  396.0 5.5 collective-permute-start.7
  400.9 6.8 collective-permute-start.21
  401.6 6.8 collective-permute-start.8
  407.8 5.6 collective-permute-start.22
  408.3 5.9 collective-permute-start.9
  418.5 6.0 collective-permute-start.24
  419.3 5.3 collective-permute-start.11
  424.5 6.5 collective-permute-start.25
  424.6 6.4 collective-permute-start.12
  431.1 5.2 collective-permute-start.13
  483.7 6.0 collective-permute-start.29
  485.5 6.0 collective-permute-start.43
  489.7 5.2 collective-permute-start.30
  491.5 5.2 collective-permute-start.44
  494.9 5.4 collective-permute-start.31
  496.7 5.4 collective-permute-start.45
  500.4 6.4 collective-permute-start.32
  502.2 6.6 collective-permute-start.46
  506.8 6.3 collective-permute-start.33
  508.8 6.1 collective-permute-start.47
  513.1 5.6 collective-permute-start.34
  514.9 5.5 collective-permute-start.48
  518.7 5.2 collective-permute-start.35
  520.5 5.3 collective-permute-start.49
  524.0 6.0 collective-permute-start.36
  525.9 6.0 collective-permute-start.50
  530.0 6.6 collective-permute-start.37
  531.9 6.5 collective-permute-start.51
  536.7 5.8 collective-permute-start.38
  538.4 5.6 collective-permute-start.52
  544.0 5.2 collective-permute-start.53
  559.5 5.4 collective-permute-start.56
  603.4 6.0 collective-permute-start.57
  605.1 6.0 collective-permute-start.71
  609.4 5.2 collective-permute-start.58
  611.1 5.2 collective-permute-start.72
  614.6 5.4 collective-permute-start.59
  616.3 5.4 collective-permute-start.73
  620.1 6.4 collective-permute-start.60
  621.8 6.6 collective-permute-start.74
  626.5 6.3 collective-permute-start.61
  628.4 6.1 collective-permute-start.75
  632.8 5.5 collective-permute-start.62
  634.5 5.3 collective-permute-start.76
  639.8 5.3 collective-permute-start.77
  643.7 6.2 collective-permute-start.64
  645.3 6.5 collective-permute-start.78
  649.9 6.5 collective-permute-start.65
  651.7 6.0 collective-permute-start.79
  656.4 5.6 collective-permute-start.66
  657.8 5.4 collective-permute-start.80
  (28 other events, 504.6 us)

commit v8 on v7

--- a/solution.py
+++ b/solution.py
@@ -33,37 +33,57 @@
     return cycle
 
 
-def ring_sum(partial, axis):
+def ring_sum(partial, axis, gather=True):
     cycle = ring_order(axis)
     count = len(cycle)
     place = jnp.asarray([cycle.index(i) for i in range(count)], jnp.int32)[lax.axis_index(axis)]
-    shape = partial.shape
-    chunks = partial.reshape(2, count, -1, shape[-1])
+    ids = jnp.asarray(cycle, jnp.int32)
+    _, sectors, block_size, _ = partial.shape
+    rows = block_size // (2 * count)
+    blocks = partial.reshape(sectors, count, 2, rows, block_size)
     forward = [(cycle[p], cycle[(p + 1) % count]) for p in range(count)]
     backward = [(cycle[p], cycle[(p - 1) % count]) for p in range(count)]
     routes = (forward, backward)
     signs = (1, -1)
 
+    def chunk_id(index):
+        return ids[index % count]
+
     def chunk(half, index):
-        return lax.dynamic_index_in_dim(chunks[half], index % count, 0, keepdims=False)
+        picked = lax.dynamic_index_in_dim(blocks, chunk_id(index), 1, keepdims=False)
+        return picked[:, half]
 
     moving = [chunk(h, place - signs[h]) for h in range(2)]
     for step in range(count - 1):
         for h in range(2):
             arrived = lax.ppermute(moving[h], axis, routes[h])
             moving[h] = arrived + chunk(h, place - signs[h] * (step + 2))
-    gathered = []
+    if not gather:
+        return jnp.stack(moving, axis=1).reshape(1, sectors, 2 * rows, block_size)
+    table = jnp.zeros(blocks.shape, partial.dtype)
     for h in range(2):
-        table = jnp.zeros(chunks.shape[1:], partial.dtype)
-        table = lax.dynamic_update_index_in_dim(table, moving[h], place % count, 0)
         current = moving[h]
+        index = place
+        table = lax.dynamic_update_slice(
+            table, current[:, None, None], (0, chunk_id(index), h, 0, 0)
+        )
         for step in range(count - 1):
             current = lax.ppermute(current, axis, routes[h])
-            table = lax.dynamic_update_index_in_dim(
-                table, current, (place - signs[h] * (step + 1)) % count, 0
+            index = place - signs[h] * (step + 1)
+            table = lax.dynamic_update_slice(
+                table, current[:, None, None], (0, chunk_id(index), h, 0, 0)
             )
-        gathered.append(table)
-    return jnp.stack(gathered).reshape(shape)
+    return table.reshape(partial.shape)
+
+
+def ops_total(value, axis):
+    count = lax.axis_size(axis)
+    here = lax.axis_index(axis)
+    table = jnp.where(jnp.arange(count)[:, None] == here, value[None, :], 0.0)
+    for shift in range(1, count):
+        sent = lax.ppermute(value, axis, [(i, (i + shift) % count) for i in range(count)])
+        table = jnp.where(jnp.arange(count)[:, None] == (here - shift) % count, sent[None, :], table)
+    return jnp.sum(table, axis=0)
 
 
 def gather_sector(values):
@@ -110,15 +130,22 @@
         partial_sigma = jnp.einsum(
             "ckqad,ckqed->cqae", products, right_ops, preferred_element_type=jnp.float32
         )
-        sigma_full = ring_sum(partial_sigma, "ops") * live
         vector_wide = vector.astype(jnp.float32)
-        rayleigh, spread = quotient(vector_wide, sigma_full)
-        quotients.append(rayleigh)
-        residue = sigma_full - rayleigh * vector_wide
         if iteration + 1 < ITERS:
+            sigma_full = ring_sum(partial_sigma, "ops") * live
+            rayleigh, spread = quotient(vector_wide, sigma_full)
+            quotients.append(rayleigh)
+            residue = sigma_full - rayleigh * vector_wide
             vector = (residue * lax.rsqrt(spread / entry_count + 1e-06)).astype(jnp.bfloat16)
         else:
-            residual = lax.dynamic_slice_in_dim(residue, row_start, share_rows, 2)
+            corr_part = ops_total(jnp.sum(vector_wide * partial_sigma)[None], "ops")[0]
+            table = gather_sector(jnp.stack([jnp.sum(vector_wide * vector_wide), corr_part]))
+            rayleigh = jnp.sum(table[:, 1]) / jnp.sum(table[:, 0])
+            quotients.append(rayleigh)
+            sigma_rows = ring_sum(partial_sigma, "ops", gather=False)
+            live_rows = lax.dynamic_slice_in_dim(live, row_start, share_rows, 2)
+            vector_rows = lax.dynamic_slice_in_dim(vector_wide, row_start, share_rows, 2)
+            residual = sigma_rows * live_rows - rayleigh * vector_rows
     thetas = jnp.stack(quotients).reshape(1, ITERS)
     return (residual, thetas)
 

time: 702 us -> 771 us (1.098)
  between operations: 25.2 us -> 95.5 us
  waiting for transfers between devices: 456 us -> 424 us
  other arithmetic: 23.1 us -> 34.1 us
  starting transfers between devices: 91.2 us -> 101 us
    ppermute x1, waiting for transfers between devices: 303 us -> 249 us  [from_behind(): return lax.ppermute(block, axis, route)]
    ppermute x42 -> x28, waiting for transfers between devices: 77.5 us -> 108 us  [ring_sum(): current = lax.ppermute(current, axis, routes[h])]
    ppermute x0 -> x7, starting transfers between devices: none -> 11.3 us  [ops_total(): lax.ppermute(value, axis, [(i, (i + shift) % count) for i in range(count)])]
    ppermute x42, waiting for transfers between devices: 75.2 us -> 64.4 us  [ring_sum(): arrived = lax.ppermute(moving[h], axis, routes[h])]
    squeeze x6 -> x9, local copies, waits for them, and re-layouts: 0.1 us -> 10.5 us  [the longest x3 6.69 us: chunk(): lax.dynamic_index_in_dim(blocks, chunk_id(index), 1, keepdims=False)]
    ppermute x42 -> x28, starting transfers between devices: 43 us -> 40.9 us  [ring_sum(): current = lax.ppermute(current, axis, routes[h])]
  transfers between devices with their start and end apart: 85 -> 78, of which waited for: 59 -> 58; matrix products, arithmetic and copies ran while one was open for 0% -> 3% of each run, Pallas kernels for 0% -> 0%
where the time goes in v8:
time: 771 us; the launch traced here: 769 us
  waiting for transfers between devices  424 us (55%)
  starting transfers between devices  101 us (13%)
  between operations  95.5 us (12%)
  matrix products  83.2 us (11%)
  other arithmetic  34.1 us (4%)
  local copies, waits for them, and re-layouts  24.4 us (3%)
    ppermute x1, waiting for transfers between devices, from_behind(): return lax.ppermute(block, axis, route)  249 us
    ppermute x28, waiting for transfers between devices, ring_sum(): current = lax.ppermute(current, axis, routes[h])  108 us
    ppermute x42, waiting for transfers between devices, ring_sum(): arrived = lax.ppermute(moving[h], axis, routes[h])  64.4 us
    dot_general x3, matrix products, on_device(): jnp.einsum('ckqad,ckqed->cqae', products, right_ops, preferred_element_ty...  62 us
    ppermute x42, starting transfers between devices, ring_sum(): arrived = lax.ppermute(moving[h], axis, routes[h])  45.6 us
    ppermute x28, starting transfers between devices, ring_sum(): current = lax.ppermute(current, axis, routes[h])  40.9 us
    dot_general x1, matrix products, on_device(): jnp.einsum('cqba,ckqbd->ckqad', basis, half_env, preferred_element_type=j...  21.2 us
  transfers between devices with their start and end apart: 78, of which 58 were waited for; matrix products, arithmetic and copies ran while one was open for 3% of the time, Pallas kernels for 0%

profile of v8, /device:TPU:0, one launch (start us, length us, event | category | flops | bytes accessed | tf_op | source)
XLA Modules:
  0.0 769.1 jit_solution(471660689235058400)
XLA Ops:
  1.9 21.2 %convert_bitcast_fusion = bf16[1,12,4,384,384]{3,4,1,2,0:T(8,128)(2,1)} fusion(bf16[1,4,384,384]{3,2,1,0:T(8,128)(2,1)S(1)} %copy-done, bf16[1,12,4,384,384]{4,3,2,1,0:T(8,128)(2,1)} %param.12), kind=kOutput, calls=%fused_computation.19 | convolution fusion | flops 10885791744 | bytes 29491200 | tf_op jit(solution)/shard_map/cqba,ckqbd->ckqad/dot_general | solution.py:116
  23.1 2.9 collective-permute-start
  81.7 248.7 %collective-permute-done = bf16[1,12,4,384,384]{3,4,1,2,0:T(8,128)(2,1)} collective-permute-done((bf16[1,12,4,384,384]{3,4,1,2,0:T(8,128)(2,1)}, bf16[1,12,4,384,384]{3,4,1,2,0:T(8,128)(2,1)}, u32[]{:S(2)}, u32[]{:S(2)}) %collective-permute-start) | collective-permute-done | bytes 14155808 | tf_op jit(solution)/shard_map/ppermute | solution.py:13
  330.4 20.5 %fusion.4 = f32[4,384,384,1]{2,1,3,0:T(8,128)} fusion(bf16[1,12,4,384,384]{3,4,1,2,0:T(8,128)(2,1)} %collective-permute-done, bf16[1,4,384,384]{3,2,1,0:T(8,128)(2,1)S(1)} %copy-done.2, pred[4,384]{1,0:T(4,128)(4,1)S(1)} %iota_compare_fusion, bf16[1,12,4,384,384]{4,3,2,1,0:T(8,128)(2,1)} %param.13), kind=kOutput, calls=%fused_computation.4 | convolution fusion | flops 10881073152 | bytes 31852032 | tf_op jit(solution)/shard_map/ckqad,ckqed->cqae/dot_general | solution.py:130
  350.9 3.6 dynamic-slice_bitcast_fusion.16
  364.6 2.5 collective-permute-done.2
  370.4 3.3 collective-permute-done.3
  373.7 2.4 collective-permute-start.4
  377.0 3.2 collective-permute-done.4
  383.2 2.5 collective-permute-done.5
  388.7 2.3 collective-permute-done.6
  393.9 2.7 collective-permute-done.7
  399.3 4.3 collective-permute-done.8
  405.2 3.9 collective-permute-done.9
  410.6 3.7 collective-permute-done.10
  415.8 4.5 collective-permute-done.11
  421.9 3.5 collective-permute-done.12
  427.1 3.5 collective-permute-done.13
  432.2 3.5 collective-permute-done.14
  438.5 4.3 collective-permute-done.22
  442.8 2.5 collective-permute-start.23
  446.2 2.8 collective-permute-done.23
  451.2 3.0 collective-permute-done.24
  456.3 3.0 collective-permute-done.25
  461.4 3.0 collective-permute-done.26
  466.6 3.0 collective-permute-done.27
  471.7 3.0 collective-permute-done.28
  480.4 2.5 stack.68
  483.0 2.4 psum.21
  490.7 19.3 %fusion.2 = f32[4,384,384,1]{2,1,3,0:T(8,128)S(1)} fusion(bf16[1,12,4,384,384]{3,4,1,2,0:T(8,128)(2,1)} %collective-permute-done, bf16[1,4,384,384]{3,2,1,0:T(8,128)(2,1)S(1)} %fusion.49, bf16[1,12,4,384,384]{4,3,2,1,0:T(8,128)(2,1)} %param.13), kind=kOutput, calls=%fused_computation.2 | convolution fusion | flops 10878713856 | bytes 31850496 | tf_op jit(solution)/shard_map/ckqad,ckqed->cqae/dot_general | solution.py:130
  548.0 2.6 collective-permute-done.30
  559.9 3.6 collective-permute-done.32
  565.7 4.5 collective-permute-done.33
  572.4 3.9 collective-permute-done.34
  578.5 3.3 collective-permute-done.35
  584.1 3.1 collective-permute-done.36
  588.7 4.6 collective-permute-done.37
  594.8 4.7 collective-permute-done.38
  601.0 3.9 collective-permute-done.39
  606.5 3.5 collective-permute-done.40
  611.7 3.5 collective-permute-done.41
  616.8 3.5 collective-permute-done.42
  622.6 3.2 collective-permute-done.50
  626.1 4.8 collective-permute-done.51
  631.3 5.8 collective-permute-done.52
  637.6 4.6 collective-permute-done.53
  642.8 4.6 collective-permute-done.54
  648.0 4.6 collective-permute-done.55
  653.1 4.6 collective-permute-done.56
  663.1 2.6 stack.74
  665.8 2.4 psum.22
  671.5 2.4 fusion.111
  673.8 22.1 %multiply_reduce_fusion = (f32[]{:T(128)}, f32[]{:T(128)}, f32[4,384,384,1]{2,1,3,0:T(8,128)S(1)}) fusion(bf16[1,4,384,384]{3,2,1,0:T(8,128)(2,1)} %get-tuple-element.19, bf16[1,12,4,384,384]{3,4,1,2,0:T(8,128)(2,1)} %collective-permute-done, bf16[1,12,4,384,384]{4,3,2,1,0:T(8,128)(2,1)} %param.13), kind=kOutput, calls=%fused_computation.53 | convolution fusion | flops 10881662976 | bytes 31850504 | tf_op jit(solution)/shard_map/ckqad,ckqed->cqae/dot_general | solution.py:130
  696.0 4.4 collective-permute-start.71
  700.9 3.6 collective-permute-start.74
  713.2 2.3 collective-permute-start.57
  718.3 5.6 fusion.110
  725.4 2.5 psum.23
  733.4 3.8 collective-permute-done.58
  740.4 3.0 collective-permute-done.59
  745.6 3.3 collective-permute-done.60
  751.1 4.4 collective-permute-done.61
  757.7 3.9 collective-permute-done.62
  763.8 3.0 collective-permute-done.63
  (268 shorter events, 135.6 us)
Async XLA Ops:
  23.1 307.3 %collective-permute-start = (bf16[1,12,4,384,384]{3,4,1,2,0:T(8,128)(2,1)}, bf16[1,12,4,384,384]{3,4,1,2,0:T(8,128)(2,1)}, u32[]{:S(2)}, u32[]{:S(2)}) collective-permute-start(bf16[1,12,4,384,384]{3,4,1,2,0:T(8,128)(2,1)} %convert_bitcast_fusion), channel_id=1, source_target_pairs={{16,0},{0,16},{17,1},{1,17},{18,2},{2,18},{19,3},{3,19},{20,4},{4,... | collective-permute-start | bytes 42467336 | tf_op jit(solution)/shard_map/ppermute | solution.py:13
  355.2 5.5 collective-permute-start.1
  361.6 5.5 collective-permute-start.2
  364.4 5.7 collective-permute-start.15
  367.1 6.6 collective-permute-start.3
  370.1 6.9 collective-permute-start.16
  373.7 6.5 collective-permute-start.4
  377.0 5.9 collective-permute-start.17
  380.3 5.4 collective-permute-start.5
  382.9 5.2 collective-permute-start.18
  385.7 5.2 collective-permute-start.6
  388.1 5.2 collective-permute-start.19
  391.0 5.6 collective-permute-start.7
  393.3 5.7 collective-permute-start.20
  396.8 6.8 collective-permute-start.8
  399.0 36.7 %collective-permute-start.21 = (f32[4,24,384]{2,1,0:T(8,128)S(1)}, f32[4,24,384]{2,1,0:T(8,128)S(1)}, u32[]{:S(2)}, u32[]{:S(2)}) collective-permute-start(f32[4,24,384]{2,1,0:T(8,128)S(1)} %fusion.97), channel_id=1, source_target_pairs={{0,2},{4,0},{8,4},{12,8},{14,12},{10,14},{6,10},{2,6},{1,3},{5,1},... | collective-permute-start | bytes 442376 | tf_op jit(solution)/shard_map/ppermute | solution.py:59
  403.6 5.6 collective-permute-start.9
  409.2 5.1 collective-permute-start.10
  414.3 6.0 collective-permute-start.11
  420.3 5.2 collective-permute-start.12
  436.5 6.3 collective-permute-start.22
  442.8 6.2 collective-permute-start.23
  449.0 5.2 collective-permute-start.24
  512.2 31.7 %collective-permute-start.29 = (f32[4,24,384]{2,1,0:T(8,128)S(1)}, f32[4,24,384]{2,1,0:T(8,128)S(1)}, u32[]{:S(2)}, u32[]{:S(2)}) collective-permute-start(f32[4,24,384]{2,1,0:T(8,128)S(1)} %slice_bitcast_fusion.31), channel_id=1, source_target_pairs={{0,4},{4,8},{8,12},{12,14},{14,10},{10,6},{6,2},{2,0},{1,5},{5,9},... | collective-permute-start | bytes 442376 | tf_op jit(solution)/shard_map/ppermute | solution.py:59
  545.0 5.7 collective-permute-start.30
  547.5 5.7 collective-permute-start.43
  551.6 5.2 collective-permute-start.31
  554.1 5.2 collective-permute-start.44
  557.7 5.8 collective-permute-start.32
  559.4 5.7 collective-permute-start.45
  563.5 6.7 collective-permute-start.33
  565.1 6.7 collective-permute-start.46
  570.2 6.0 collective-permute-start.34
  571.9 6.0 collective-permute-start.47
  576.3 5.4 collective-permute-start.35
  577.9 5.7 collective-permute-start.48
  581.9 5.3 collective-permute-start.36
  583.6 36.7 %collective-permute-start.49 = (f32[4,24,384]{2,1,0:T(8,128)S(1)}, f32[4,24,384]{2,1,0:T(8,128)S(1)}, u32[]{:S(2)}, u32[]{:S(2)}) collective-permute-start(f32[4,24,384]{2,1,0:T(8,128)S(1)} %fusion.83), channel_id=1, source_target_pairs={{0,2},{4,0},{8,4},{12,8},{14,12},{10,14},{6,10},{2,6},{1,3},{5,1},... | collective-permute-start | bytes 442376 | tf_op jit(solution)/shard_map/ppermute | solution.py:59
  587.2 6.1 collective-permute-start.37
  593.3 6.2 collective-permute-start.38
  599.5 5.4 collective-permute-start.39
  620.4 5.4 collective-permute-start.50
  630.9 6.2 collective-permute-start.52
  696.0 14.5 %collective-permute-start.71 = (f32[1]{0:T(128)}, f32[1]{0:T(128)}, u32[]{:S(2)}, u32[]{:S(2)}) collective-permute-start(f32[1]{0:T(128)} %bitcast.267), channel_id=1, source_target_pairs={{0,14},{2,0},{4,2},{6,4},{8,6},{10,8},{12,10},{14,12},{1,15},{3,1}... | collective-permute-start | bytes 20 | tf_op jit(solution)/shard_map/ppermute | solution.py:84
  700.3 11.3 %collective-permute-start.72 = (f32[1]{0:T(128)}, f32[1]{0:T(128)}, u32[]{:S(2)}, u32[]{:S(2)}) collective-permute-start(f32[1]{0:T(128)} %bitcast.267), channel_id=1, source_target_pairs={{0,12},{2,14},{4,0},{6,2},{8,4},{10,6},{12,8},{14,10},{1,13},{3,15... | collective-permute-start | bytes 20 | tf_op jit(solution)/shard_map/ppermute | solution.py:84
  700.9 12.2 %collective-permute-start.73 = (f32[1]{0:T(128)}, f32[1]{0:T(128)}, u32[]{:S(2)}, u32[]{:S(2)}) collective-permute-start(f32[1]{0:T(128)} %bitcast.267), channel_id=1, source_target_pairs={{0,10},{2,12},{4,14},{6,0},{8,2},{10,4},{12,6},{14,8},{1,11},{3,13... | collective-permute-start | bytes 20 | tf_op jit(solution)/shard_map/ppermute | solution.py:84
  700.9 14.5 %collective-permute-start.74 = (f32[1]{0:T(128)}, f32[1]{0:T(128)}, u32[]{:S(2)}, u32[]{:S(2)}) collective-permute-start(f32[1]{0:T(128)} %bitcast.267), channel_id=1, source_target_pairs={{0,8},{2,10},{4,12},{6,14},{8,0},{10,2},{12,4},{14,6},{1,9},{3,11}... | collective-permute-start | bytes 20 | tf_op jit(solution)/shard_map/ppermute | solution.py:84
  704.6 10.9 %collective-permute-start.75 = (f32[1]{0:T(128)}, f32[1]{0:T(128)}, u32[]{:S(2)}, u32[]{:S(2)}) collective-permute-start(f32[1]{0:T(128)} %bitcast.267), channel_id=1, source_target_pairs={{0,6},{2,8},{4,10},{6,12},{8,14},{10,0},{12,2},{14,4},{1,7},{3,9},... | collective-permute-start | bytes 20 | tf_op jit(solution)/shard_map/ppermute | solution.py:84
  710.5 5.8 collective-permute-start.76
  711.7 6.6 collective-permute-start.77
  713.2 17.2 %collective-permute-start.57 = (f32[4,24,384]{2,1,0:T(8,128)}, f32[4,24,384]{2,1,0:T(8,128)S(1)}, u32[]{:S(2)}, u32[]{:S(2)}) collective-permute-start(f32[4,24,384]{2,1,0:T(8,128)} %slice_bitcast_fusion.15), channel_id=1, source_target_pairs={{0,4},{4,8},{8,12},{12,14},{14,10},{10,6},{6,2},{2,0},{1,5},{5,9},... | collective-permute-start | bytes 442376 | tf_op jit(solution)/shard_map/ppermute | solution.py:59
  715.5 15.9 %collective-permute-start.64 = (f32[4,24,384]{2,1,0:T(8,128)}, f32[4,24,384]{2,1,0:T(8,128)S(1)}, u32[]{:S(2)}, u32[]{:S(2)}) collective-permute-start(f32[4,24,384]{2,1,0:T(8,128)} %slice_bitcast_fusion.7), channel_id=1, source_target_pairs={{0,2},{4,0},{8,4},{12,8},{14,12},{10,14},{6,10},{2,6},{1,3},{5,1},... | collective-permute-start | bytes 442376 | tf_op jit(solution)/shard_map/ppermute | solution.py:59
  731.3 6.0 collective-permute-start.58
  731.4 7.2 collective-permute-start.65
  738.2 5.2 collective-permute-start.59
  738.6 5.5 collective-permute-start.66
  743.4 5.5 collective-permute-start.60
  744.1 5.2 collective-permute-start.67
  748.9 6.6 collective-permute-start.61
  749.3 6.4 collective-permute-start.68
  755.5 6.1 collective-permute-start.62
  755.7 6.3 collective-permute-start.69
  761.6 5.2 collective-permute-start.63
  762.0 5.2 collective-permute-start.70
  (37 other events, 1246.1 us)

commit v9 on v7

--- a/solution.py
+++ b/solution.py
@@ -112,13 +112,20 @@
         )
         sigma_full = ring_sum(partial_sigma, "ops") * live
         vector_wide = vector.astype(jnp.float32)
-        rayleigh, spread = quotient(vector_wide, sigma_full)
-        quotients.append(rayleigh)
-        residue = sigma_full - rayleigh * vector_wide
         if iteration + 1 < ITERS:
+            rayleigh, spread = quotient(vector_wide, sigma_full)
+            quotients.append(rayleigh)
+            residue = sigma_full - rayleigh * vector_wide
             vector = (residue * lax.rsqrt(spread / entry_count + 1e-06)).astype(jnp.bfloat16)
         else:
-            residual = lax.dynamic_slice_in_dim(residue, row_start, share_rows, 2)
+            table = gather_sector(
+                jnp.stack([jnp.sum(vector_wide * vector_wide), jnp.sum(vector_wide * sigma_full)])
+            )
+            rayleigh = jnp.sum(table[:, 1]) / jnp.sum(table[:, 0])
+            quotients.append(rayleigh)
+            sigma_rows = lax.dynamic_slice_in_dim(sigma_full, row_start, share_rows, 2)
+            vector_rows = lax.dynamic_slice_in_dim(vector_wide, row_start, share_rows, 2)
+            residual = sigma_rows - rayleigh * vector_rows
     thetas = jnp.stack(quotients).reshape(1, ITERS)
     return (residual, thetas)
 

time: 702 us -> 696 us (level)
  no operation moved by 1% of the time
where the time goes in v9:
time: 696 us; the launch traced here: 695 us
  waiting for transfers between devices  456 us (66%)
  starting transfers between devices  91.3 us (13%)
  matrix products  81.3 us (12%)
  between operations  23.4 us (3%)
  other arithmetic  21.9 us (3%)
  local copies, waits for them, and re-layouts  14.2 us (2%)
  blocking collectives  7.34 us (1%)
    ppermute x1, waiting for transfers between devices, from_behind(): return lax.ppermute(block, axis, route)  303 us
    ppermute x42, waiting for transfers between devices, ring_sum(): current = lax.ppermute(current, axis, routes[h])  77.8 us
    ppermute x42, waiting for transfers between devices, ring_sum(): arrived = lax.ppermute(moving[h], axis, routes[h])  75.1 us
    dot_general x3, matrix products, on_device(): jnp.einsum('ckqad,ckqed->cqae', products, right_ops, preferred_element_ty...  60.1 us
    ppermute x42, starting transfers between devices, ring_sum(): arrived = lax.ppermute(moving[h], axis, routes[h])  45.2 us
    ppermute x42, starting transfers between devices, ring_sum(): current = lax.ppermute(current, axis, routes[h])  43.2 us
    dot_general x1, matrix products, on_device(): jnp.einsum('cqba,ckqbd->ckqad', basis, half_env, preferred_element_type=j...  21.2 us
  transfers between devices with their start and end apart: 85, of which 59 were waited for; matrix products, arithmetic and copies ran while one was open for 0% of the time, Pallas kernels for 0%

profile of v9, /device:TPU:0, one launch (start us, length us, event | category | flops | bytes accessed | tf_op | source)
XLA Modules:
  0.0 695.5 jit_solution(17337312110681399108)
XLA Ops:
  1.9 21.2 %convert_bitcast_fusion = bf16[1,12,4,384,384]{3,4,1,2,0:T(8,128)(2,1)} fusion(bf16[1,4,384,384]{3,2,1,0:T(8,128)(2,1)S(1)} %copy-done, bf16[1,12,4,384,384]{4,3,2,1,0:T(8,128)(2,1)} %param.9), kind=kOutput, calls=%fused_computation.19 | convolution fusion | flops 10885791744 | bytes 29491200 | tf_op jit(solution)/shard_map/cqba,ckqbd->ckqad/dot_general | solution.py:96
  23.1 2.9 collective-permute-start
  27.4 303.0 %collective-permute-done = bf16[1,12,4,384,384]{3,4,1,2,0:T(8,128)(2,1)} collective-permute-done((bf16[1,12,4,384,384]{3,4,1,2,0:T(8,128)(2,1)}, bf16[1,12,4,384,384]{3,4,1,2,0:T(8,128)(2,1)}, u32[]{:S(2)}, u32[]{:S(2)}) %collective-permute-start) | collective-permute-done | bytes 14155808 | tf_op jit(solution)/shard_map/ppermute | solution.py:13
  330.4 20.6 %fusion.59 = f32[4,384,384]{2,1,0:T(8,128)} fusion(bf16[1,12,4,384,384]{3,4,1,2,0:T(8,128)(2,1)} %collective-permute-done, bf16[1,4,384,384]{3,2,1,0:T(8,128)(2,1)S(1)} %copy-done.2, pred[4,384]{1,0:T(4,128)(4,1)S(1)} %iota_compare_fusion, bf16[1,12,4,384,384]{4,3,2,1,0:T(8,128)(2,1)} %param.10), kind=kOutput, calls=%fused_computation.61 | convolution fusion | flops 10881073152 | bytes 31852032 | tf_op jit(solution)/shard_map/ckqad,ckqed->cqae/dot_general | solution.py:110
  352.8 1.9 collective-permute-start.1
  368.8 3.0 collective-permute-done.15
  372.2 1.9 collective-permute-start.3
  374.1 4.0 collective-permute-done.16
  378.2 2.3 collective-permute-start.4
  380.5 3.9 collective-permute-done.17
  386.6 3.5 collective-permute-done.18
  392.3 3.0 collective-permute-done.19
  397.5 3.4 collective-permute-done.20
  401.6 1.9 collective-permute-start.8
  403.5 4.2 collective-permute-done.21
  409.9 3.5 collective-permute-done.22
  415.6 3.0 collective-permute-done.23
  420.7 3.8 collective-permute-done.24
  424.7 2.3 collective-permute-start.12
  427.0 4.1 collective-permute-done.25
  431.1 2.1 collective-permute-start.13
  433.2 3.0 collective-permute-done.26
  436.3 2.0 collective-permute-start.14
  438.3 3.0 collective-permute-done.27
  441.5 5.0 collective-permute-done.28
  451.6 2.0 fusion.47
  453.7 2.6 stack.193
  456.3 2.4 psum.21
  462.0 2.1 fusion.50
  464.0 19.3 %fusion.66 = f32[4,384,384]{2,1,0:T(8,128)S(1)} fusion(bf16[1,12,4,384,384]{3,4,1,2,0:T(8,128)(2,1)} %collective-permute-done, bf16[1,4,384,384]{3,2,1,0:T(8,128)(2,1)S(1)} %fusion.50, bf16[1,12,4,384,384]{4,3,2,1,0:T(8,128)(2,1)} %param.10), kind=kOutput, calls=%fused_computation.62 | convolution fusion | flops 10878713856 | bytes 31850496 | tf_op jit(solution)/shard_map/ckqad,ckqed->cqae/dot_general | solution.py:110
  485.7 3.8 collective-permute-done.29
  491.7 3.0 collective-permute-done.30
  496.9 3.3 collective-permute-done.31
  502.4 4.2 collective-permute-done.32
  508.8 4.2 collective-permute-done.33
  515.1 3.4 collective-permute-done.34
  520.7 3.0 collective-permute-done.35
  526.1 3.8 collective-permute-done.36
  532.0 4.5 collective-permute-done.37
  538.6 3.6 collective-permute-done.38
  544.4 3.0 collective-permute-done.39
  549.5 3.0 collective-permute-done.40
  554.7 3.0 collective-permute-done.41
  560.0 2.8 collective-permute-done.42
  562.8 1.9 collective-permute-done.56
  570.5 2.7 stack.216
  573.3 2.4 psum.22
  579.2 2.4 fusion.90
  581.6 20.2 %fusion.73 = f32[4,384,384]{2,1,0:T(8,128)} fusion(bf16[1,12,4,384,384]{3,4,1,2,0:T(8,128)(2,1)} %collective-permute-done, bf16[1,4,384,384]{3,2,1,0:T(8,128)(2,1)} %get-tuple-element.24, bf16[1,12,4,384,384]{4,3,2,1,0:T(8,128)(2,1)} %param.10), kind=kOutput, calls=%fused_computation.63 | convolution fusion | flops 10878713856 | bytes 31850496 | tf_op jit(solution)/shard_map/ckqad,ckqed->cqae/dot_general | solution.py:110
  605.8 3.8 collective-permute-done.57
  611.8 3.0 collective-permute-done.58
  617.0 3.3 collective-permute-done.59
  622.5 4.3 collective-permute-done.60
  629.1 3.9 collective-permute-done.61
  635.2 3.3 collective-permute-done.62
  640.7 3.0 collective-permute-done.63
  646.2 4.0 collective-permute-done.64
  652.4 4.2 collective-permute-done.65
  658.7 3.4 collective-permute-done.66
  664.2 3.0 collective-permute-done.67
  669.4 3.0 collective-permute-done.68
  674.5 3.0 collective-permute-done.69
  679.7 3.0 collective-permute-done.70
  688.6 2.4 psum.23
  (252 shorter events, 101.5 us)
Async XLA Ops:
  23.1 307.3 %collective-permute-start = (bf16[1,12,4,384,384]{3,4,1,2,0:T(8,128)(2,1)}, bf16[1,12,4,384,384]{3,4,1,2,0:T(8,128)(2,1)}, u32[]{:S(2)}, u32[]{:S(2)}) collective-permute-start(bf16[1,12,4,384,384]{3,4,1,2,0:T(8,128)(2,1)} %convert_bitcast_fusion), channel_id=1, source_target_pairs={{16,0},{0,16},{17,1},{1,17},{18,2},{2,18},{19,3},{3,19},{20,4},{4,... | collective-permute-start | bytes 42467336 | tf_op jit(solution)/shard_map/ppermute | solution.py:13
  352.8 14.1 %collective-permute-start.1 = (f32[96,384]{1,0:T(8,128)S(1)}, f32[96,384]{1,0:T(8,128)S(1)}, u32[]{:S(2)}, u32[]{:S(2)}) collective-permute-start(f32[96,384]{1,0:T(8,128)S(1)} %dynamic-slice_bitcast_fusion.5), channel_id=1, source_target_pairs={{0,4},{4,8},{8,12},{12,14},{14,10},{10,6},{6,2},{2,0},{1,5},{5,9},... | collective-permute-start | bytes 442376 | tf_op jit(solution)/shard_map/ppermute | solution.py:53
  366.7 5.2 collective-permute-start.15
  367.0 5.2 collective-permute-start.2
  371.9 6.2 collective-permute-start.16
  372.2 6.0 collective-permute-start.3
  378.1 6.3 collective-permute-start.17
  378.2 6.7 collective-permute-start.4
  384.5 5.7 collective-permute-start.18
  384.9 5.8 collective-permute-start.5
  390.1 5.2 collective-permute-start.19
  390.8 5.2 collective-permute-start.6
  395.4 5.5 collective-permute-start.20
  396.0 5.5 collective-permute-start.7
  400.9 6.8 collective-permute-start.21
  401.6 6.8 collective-permute-start.8
  407.8 5.6 collective-permute-start.22
  408.4 5.9 collective-permute-start.9
  418.6 6.0 collective-permute-start.24
  419.4 5.3 collective-permute-start.11
  424.5 6.5 collective-permute-start.25
  424.7 6.4 collective-permute-start.12
  431.1 5.2 collective-permute-start.13
  483.6 6.0 collective-permute-start.29
  485.4 6.0 collective-permute-start.43
  489.6 5.2 collective-permute-start.30
  491.4 5.2 collective-permute-start.44
  494.8 5.4 collective-permute-start.31
  496.6 5.5 collective-permute-start.45
  500.2 6.4 collective-permute-start.32
  502.1 6.6 collective-permute-start.46
  506.6 6.3 collective-permute-start.33
  508.7 6.1 collective-permute-start.47
  513.0 5.5 collective-permute-start.34
  514.8 5.5 collective-permute-start.48
  518.6 5.2 collective-permute-start.35
  520.3 5.3 collective-permute-start.49
  523.9 6.1 collective-permute-start.36
  525.8 5.9 collective-permute-start.50
  529.9 6.6 collective-permute-start.37
  531.7 6.5 collective-permute-start.51
  536.5 5.7 collective-permute-start.38
  538.3 5.7 collective-permute-start.52
  543.9 5.2 collective-permute-start.53
  559.4 5.4 collective-permute-start.56
  603.6 5.9 collective-permute-start.57
  605.3 6.0 collective-permute-start.71
  609.6 5.2 collective-permute-start.58
  611.3 5.2 collective-permute-start.72
  614.8 5.5 collective-permute-start.59
  616.5 5.4 collective-permute-start.73
  620.3 6.4 collective-permute-start.60
  622.0 6.6 collective-permute-start.74
  626.8 6.3 collective-permute-start.61
  628.6 6.2 collective-permute-start.75
  633.1 5.5 collective-permute-start.62
  634.7 5.5 collective-permute-start.76
  640.2 5.3 collective-permute-start.77
  643.9 6.2 collective-permute-start.64
  645.6 6.3 collective-permute-start.78
  650.1 6.4 collective-permute-start.65
  651.9 6.2 collective-permute-start.79
  656.5 5.6 collective-permute-start.66
  658.1 5.6 collective-permute-start.80
  (28 other events, 502.4 us)

commit v10 on v9

--- a/solution.py
+++ b/solution.py
@@ -68,8 +68,12 @@
 
 def gather_sector(values):
     count = lax.axis_size("sector")
+    column = jnp.arange(len(values))
+    row = jnp.zeros((len(values),), jnp.float32)
+    for index, value in enumerate(values):
+        row = jnp.where(column == index, value, row)
     mine = jnp.arange(count)[:, None] == lax.axis_index("sector")
-    return lax.psum(jnp.where(mine, values[None, :], 0.0), "sector")
+    return lax.psum(jnp.where(mine, row[None, :], 0.0), "sector")
 
 
 def quotient(vector_wide, sigma_full):
@@ -79,7 +83,7 @@
     local_rest = sigma_full - local_theta * vector_wide
     rest_part = jnp.sum(local_rest * local_rest)
     cross_part = jnp.sum(vector_wide * local_rest)
-    table = gather_sector(jnp.stack([norm_part, corr_part, rest_part, cross_part, local_theta]))
+    table = gather_sector([norm_part, corr_part, rest_part, cross_part, local_theta])
     norms, corrs, rests, crosses, thetas = (table[:, i] for i in range(5))
     rayleigh = jnp.sum(corrs) / jnp.sum(norms)
     shift = thetas - rayleigh
@@ -119,7 +123,7 @@
             vector = (residue * lax.rsqrt(spread / entry_count + 1e-06)).astype(jnp.bfloat16)
         else:
             table = gather_sector(
-                jnp.stack([jnp.sum(vector_wide * vector_wide), jnp.sum(vector_wide * sigma_full)])
+                [jnp.sum(vector_wide * vector_wide), jnp.sum(vector_wide * sigma_full)]
             )
             rayleigh = jnp.sum(table[:, 1]) / jnp.sum(table[:, 0])
             quotients.append(rayleigh)

time: 696 us -> 696 us (level)
  no operation moved by 1% of the time
where the time goes in v10:
time: 696 us; the launch traced here: 695 us
  waiting for transfers between devices  456 us (66%)
  starting transfers between devices  91.1 us (13%)
  matrix products  81.3 us (12%)
  other arithmetic  26.9 us (4%)
  between operations  23.4 us (3%)
  local copies, waits for them, and re-layouts  8.93 us (1%)
  blocking collectives  7.33 us (1%)
    ppermute x1, waiting for transfers between devices, from_behind(): return lax.ppermute(block, axis, route)  303 us
    ppermute x42, waiting for transfers between devices, ring_sum(): current = lax.ppermute(current, axis, routes[h])  77.9 us
    ppermute x42, waiting for transfers between devices, ring_sum(): arrived = lax.ppermute(moving[h], axis, routes[h])  75.2 us
    dot_general x3, matrix products, on_device(): jnp.einsum('ckqad,ckqed->cqae', products, right_ops, preferred_element_ty...  60.1 us
    ppermute x42, starting transfers between devices, ring_sum(): arrived = lax.ppermute(moving[h], axis, routes[h])  45.2 us
    ppermute x42, starting transfers between devices, ring_sum(): current = lax.ppermute(current, axis, routes[h])  43 us
    dot_general x1, matrix products, on_device(): jnp.einsum('cqba,ckqbd->ckqad', basis, half_env, preferred_element_type=j...  21.2 us
  transfers between devices with their start and end apart: 85, of which 59 were waited for; matrix products, arithmetic and copies ran while one was open for 0% of the time, Pallas kernels for 0%

profile of v10, /device:TPU:0, one launch (start us, length us, event | category | flops | bytes accessed | tf_op | source)
XLA Modules:
  0.0 695.2 jit_solution(6756396689960114390)
XLA Ops:
  1.9 21.2 %convert_bitcast_fusion = bf16[1,12,4,384,384]{3,4,1,2,0:T(8,128)(2,1)} fusion(bf16[1,4,384,384]{3,2,1,0:T(8,128)(2,1)S(1)} %copy-done, bf16[1,12,4,384,384]{4,3,2,1,0:T(8,128)(2,1)} %param.9), kind=kOutput, calls=%fused_computation.19 | convolution fusion | flops 10885791744 | bytes 29491200 | tf_op jit(solution)/shard_map/cqba,ckqbd->ckqad/dot_general | solution.py:100
  23.1 2.9 collective-permute-start
  27.4 303.0 %collective-permute-done = bf16[1,12,4,384,384]{3,4,1,2,0:T(8,128)(2,1)} collective-permute-done((bf16[1,12,4,384,384]{3,4,1,2,0:T(8,128)(2,1)}, bf16[1,12,4,384,384]{3,4,1,2,0:T(8,128)(2,1)}, u32[]{:S(2)}, u32[]{:S(2)}) %collective-permute-start) | collective-permute-done | bytes 14155808 | tf_op jit(solution)/shard_map/ppermute | solution.py:13
  330.4 20.6 %fusion.59 = f32[4,384,384]{2,1,0:T(8,128)} fusion(bf16[1,12,4,384,384]{3,4,1,2,0:T(8,128)(2,1)} %collective-permute-done, bf16[1,4,384,384]{3,2,1,0:T(8,128)(2,1)S(1)} %copy-done.2, pred[4,384]{1,0:T(4,128)(4,1)S(1)} %iota_compare_fusion, bf16[1,12,4,384,384]{4,3,2,1,0:T(8,128)(2,1)} %param.10), kind=kOutput, calls=%fused_computation.61 | convolution fusion | flops 10881073152 | bytes 31852032 | tf_op jit(solution)/shard_map/ckqad,ckqed->cqae/dot_general | solution.py:114
  352.8 1.9 collective-permute-start.1
  368.8 3.0 collective-permute-done.15
  372.2 1.9 collective-permute-start.3
  374.1 4.0 collective-permute-done.16
  378.2 2.3 collective-permute-start.4
  380.5 3.9 collective-permute-done.17
  386.6 3.5 collective-permute-done.18
  392.3 3.0 collective-permute-done.19
  397.5 3.4 collective-permute-done.20
  401.6 1.9 collective-permute-start.8
  403.5 4.2 collective-permute-done.21
  409.9 3.5 collective-permute-done.22
  415.6 3.0 collective-permute-done.23
  420.7 3.8 collective-permute-done.24
  424.7 2.3 collective-permute-start.12
  427.0 4.1 collective-permute-done.25
  431.1 2.1 collective-permute-start.13
  433.2 3.0 collective-permute-done.26
  436.3 2.0 collective-permute-start.14
  438.3 3.0 collective-permute-done.27
  441.5 5.0 collective-permute-done.28
  451.6 2.1 fusion.47
  453.7 2.5 compare_select_fusion.11
  456.3 2.4 psum.21
  462.0 2.1 fusion.50
  464.1 19.3 %fusion.66 = f32[4,384,384]{2,1,0:T(8,128)S(1)} fusion(bf16[1,12,4,384,384]{3,4,1,2,0:T(8,128)(2,1)} %collective-permute-done, bf16[1,4,384,384]{3,2,1,0:T(8,128)(2,1)S(1)} %fusion.50, bf16[1,12,4,384,384]{4,3,2,1,0:T(8,128)(2,1)} %param.10), kind=kOutput, calls=%fused_computation.62 | convolution fusion | flops 10878713856 | bytes 31850496 | tf_op jit(solution)/shard_map/ckqad,ckqed->cqae/dot_general | solution.py:114
  485.7 3.8 collective-permute-done.29
  491.7 3.0 collective-permute-done.30
  496.9 3.3 collective-permute-done.31
  502.4 4.2 collective-permute-done.32
  508.8 4.2 collective-permute-done.33
  515.2 3.4 collective-permute-done.34
  520.7 3.0 collective-permute-done.35
  526.1 3.8 collective-permute-done.36
  532.1 4.5 collective-permute-done.37
  538.6 3.6 collective-permute-done.38
  544.4 3.0 collective-permute-done.39
  549.5 3.0 collective-permute-done.40
  554.7 3.0 collective-permute-done.41
  560.0 2.8 collective-permute-done.42
  562.9 1.9 collective-permute-done.56
  570.5 2.5 compare_select_fusion.10
  573.1 2.4 psum.22
  578.9 2.4 fusion.90
  581.4 20.2 %fusion.73 = f32[4,384,384]{2,1,0:T(8,128)} fusion(bf16[1,12,4,384,384]{3,4,1,2,0:T(8,128)(2,1)} %collective-permute-done, bf16[1,4,384,384]{3,2,1,0:T(8,128)(2,1)} %get-tuple-element.24, bf16[1,12,4,384,384]{4,3,2,1,0:T(8,128)(2,1)} %param.10), kind=kOutput, calls=%fused_computation.63 | convolution fusion | flops 10878713856 | bytes 31850496 | tf_op jit(solution)/shard_map/ckqad,ckqed->cqae/dot_general | solution.py:114
  605.6 3.8 collective-permute-done.57
  611.6 3.0 collective-permute-done.58
  616.8 3.3 collective-permute-done.59
  622.3 4.2 collective-permute-done.60
  628.9 4.0 collective-permute-done.61
  635.0 3.4 collective-permute-done.62
  640.6 3.0 collective-permute-done.63
  646.0 3.9 collective-permute-done.64
  652.0 4.3 collective-permute-done.65
  658.5 3.5 collective-permute-done.66
  664.1 3.0 collective-permute-done.67
  669.3 3.0 collective-permute-done.68
  674.4 3.0 collective-permute-done.69
  679.5 3.0 collective-permute-done.70
  688.4 2.4 psum.23
  (252 shorter events, 101.2 us)
Async XLA Ops:
  23.1 307.3 %collective-permute-start = (bf16[1,12,4,384,384]{3,4,1,2,0:T(8,128)(2,1)}, bf16[1,12,4,384,384]{3,4,1,2,0:T(8,128)(2,1)}, u32[]{:S(2)}, u32[]{:S(2)}) collective-permute-start(bf16[1,12,4,384,384]{3,4,1,2,0:T(8,128)(2,1)} %convert_bitcast_fusion), channel_id=1, source_target_pairs={{16,0},{0,16},{17,1},{1,17},{18,2},{2,18},{19,3},{3,19},{20,4},{4,... | collective-permute-start | bytes 42467336 | tf_op jit(solution)/shard_map/ppermute | solution.py:13
  352.8 14.1 %collective-permute-start.1 = (f32[96,384]{1,0:T(8,128)S(1)}, f32[96,384]{1,0:T(8,128)S(1)}, u32[]{:S(2)}, u32[]{:S(2)}) collective-permute-start(f32[96,384]{1,0:T(8,128)S(1)} %dynamic-slice_bitcast_fusion.5), channel_id=1, source_target_pairs={{0,4},{4,8},{8,12},{12,14},{14,10},{10,6},{6,2},{2,0},{1,5},{5,9},... | collective-permute-start | bytes 442376 | tf_op jit(solution)/shard_map/ppermute | solution.py:53
  366.7 5.2 collective-permute-start.15
  367.0 5.2 collective-permute-start.2
  371.9 6.2 collective-permute-start.16
  372.2 6.0 collective-permute-start.3
  378.1 6.3 collective-permute-start.17
  378.2 6.7 collective-permute-start.4
  384.5 5.7 collective-permute-start.18
  384.9 5.8 collective-permute-start.5
  390.1 5.2 collective-permute-start.19
  390.8 5.2 collective-permute-start.6
  395.4 5.5 collective-permute-start.20
  396.0 5.5 collective-permute-start.7
  400.9 6.8 collective-permute-start.21
  401.6 6.8 collective-permute-start.8
  407.8 5.6 collective-permute-start.22
  408.4 5.9 collective-permute-start.9
  418.6 6.0 collective-permute-start.24
  419.4 5.3 collective-permute-start.11
  424.5 6.5 collective-permute-start.25
  424.7 6.4 collective-permute-start.12
  431.1 5.2 collective-permute-start.13
  483.6 6.0 collective-permute-start.29
  485.4 6.0 collective-permute-start.43
  489.6 5.2 collective-permute-start.30
  491.4 5.2 collective-permute-start.44
  494.8 5.4 collective-permute-start.31
  496.6 5.5 collective-permute-start.45
  500.3 6.4 collective-permute-start.32
  502.1 6.6 collective-permute-start.46
  506.7 6.3 collective-permute-start.33
  508.7 6.1 collective-permute-start.47
  513.0 5.5 collective-permute-start.34
  514.8 5.5 collective-permute-start.48
  518.6 5.2 collective-permute-start.35
  520.4 5.3 collective-permute-start.49
  523.9 6.1 collective-permute-start.36
  525.8 5.9 collective-permute-start.50
  529.9 6.6 collective-permute-start.37
  531.7 6.5 collective-permute-start.51
  536.5 5.7 collective-permute-start.38
  538.3 5.7 collective-permute-start.52
  544.0 5.2 collective-permute-start.53
  559.4 5.4 collective-permute-start.56
  603.4 6.0 collective-permute-start.57
  605.1 6.0 collective-permute-start.71
  609.4 5.2 collective-permute-start.58
  614.6 5.4 collective-permute-start.59
  616.3 5.4 collective-permute-start.73
  620.1 6.4 collective-permute-start.60
  621.8 6.6 collective-permute-start.74
  626.5 6.3 collective-permute-start.61
  628.4 6.1 collective-permute-start.75
  632.8 5.5 collective-permute-start.62
  634.5 5.5 collective-permute-start.76
  638.4 5.2 collective-permute-start.63
  640.0 5.3 collective-permute-start.77
  643.7 6.2 collective-permute-start.64
  645.4 6.3 collective-permute-start.78
  649.9 6.5 collective-permute-start.65
  651.7 6.2 collective-permute-start.79
  656.4 5.6 collective-permute-start.66
  657.9 5.6 collective-permute-start.80
  (28 other events, 502.3 us)

commit v11 on v10

--- a/solution.py
+++ b/solution.py
@@ -64,6 +64,61 @@
             )
         gathered.append(table)
     return jnp.stack(gathered).reshape(shape)
+
+
+def ring_update(partial, vector, live, entry_count, axis):
+    cycle = ring_order(axis)
+    count = len(cycle)
+    place = jnp.asarray([cycle.index(i) for i in range(count)], jnp.int32)[lax.axis_index(axis)]
+    shape = partial.shape
+    chunks = partial.reshape(2, count, -1, shape[-1])
+    forward = [(cycle[p], cycle[(p + 1) % count]) for p in range(count)]
+    backward = [(cycle[p], cycle[(p - 1) % count]) for p in range(count)]
+    routes = (forward, backward)
+    signs = (1, -1)
+
+    def pick(array, half, index):
+        return lax.dynamic_index_in_dim(array.reshape(chunks.shape)[half], index % count, 0, keepdims=False)
+
+    moving = [pick(partial, h, place - signs[h]) for h in range(2)]
+    for step in range(count - 1):
+        for h in range(2):
+            arrived = lax.ppermute(moving[h], axis, routes[h])
+            moving[h] = arrived + pick(partial, h, place - signs[h] * (step + 2))
+    sigma = jnp.stack(moving) * jnp.stack([pick(live, h, place) for h in range(2)])
+    vec = jnp.stack([pick(vector, h, place) for h in range(2)]).astype(jnp.float32)
+    norm_part = jnp.sum(vec * vec)
+    corr_part = jnp.sum(vec * sigma)
+    local_theta = jnp.where(norm_part > 0, corr_part / jnp.where(norm_part > 0, norm_part, 1.0), 0.0)
+    local_rest = sigma - local_theta * vec
+    values = [norm_part, corr_part, jnp.sum(local_rest * local_rest), jnp.sum(vec * local_rest), local_theta]
+    column = jnp.arange(len(values))
+    row = jnp.zeros((len(values),), jnp.float32)
+    for index, value in enumerate(values):
+        row = jnp.where(column == index, value, row)
+    here = lax.axis_index(axis)
+    table = jnp.where(jnp.arange(count)[:, None] == here, row[None, :], 0.0)
+    for shift in range(1, count):
+        sent = lax.ppermute(row, axis, [(i, (i + shift) % count) for i in range(count)])
+        table = jnp.where(jnp.arange(count)[:, None] == (here - shift) % count, sent[None, :], table)
+    table = gather_sector(list(table.reshape(-1))).reshape(-1, len(values))
+    norms, corrs, rests, crosses, thetas = (table[:, i] for i in range(len(values)))
+    rayleigh = jnp.sum(corrs) / jnp.sum(norms)
+    shift = thetas - rayleigh
+    spread = jnp.sum(rests + 2.0 * shift * crosses + shift * shift * norms)
+    ahead = ((sigma - rayleigh * vec) * lax.rsqrt(spread / entry_count + 1e-06)).astype(jnp.bfloat16)
+    gathered = []
+    for h in range(2):
+        table = jnp.zeros(chunks.shape[1:], jnp.bfloat16)
+        table = lax.dynamic_update_index_in_dim(table, ahead[h], place % count, 0)
+        current = ahead[h]
+        for step in range(count - 1):
+            current = lax.ppermute(current, axis, routes[h])
+            table = lax.dynamic_update_index_in_dim(
+                table, current, (place - signs[h] * (step + 1)) % count, 0
+            )
+        gathered.append(table)
+    return rayleigh, jnp.stack(gathered).reshape(shape)
 
 
 def gather_sector(values):
@@ -114,14 +169,12 @@
         partial_sigma = jnp.einsum(
             "ckqad,ckqed->cqae", products, right_ops, preferred_element_type=jnp.float32
         )
-        sigma_full = ring_sum(partial_sigma, "ops") * live
-        vector_wide = vector.astype(jnp.float32)
         if iteration + 1 < ITERS:
-            rayleigh, spread = quotient(vector_wide, sigma_full)
+            rayleigh, vector = ring_update(partial_sigma, vector, live, entry_count, "ops")
             quotients.append(rayleigh)
-            residue = sigma_full - rayleigh * vector_wide
-            vector = (residue * lax.rsqrt(spread / entry_count + 1e-06)).astype(jnp.bfloat16)
         else:
+            sigma_full = ring_sum(partial_sigma, "ops") * live
+            vector_wide = vector.astype(jnp.float32)
             table = gather_sector(
                 [jnp.sum(vector_wide * vector_wide), jnp.sum(vector_wide * sigma_full)]
             )

time: 696 us -> 756 us (1.086)
  other arithmetic: 26.9 us -> 75.6 us
  starting transfers between devices: 91.1 us -> 110 us
  waiting for transfers between devices: 456 us -> 444 us
    ppermute x0 -> x70, waiting for transfers between devices: none -> 94.7 us  [the longest x28 50.6 us: ring_update(): arrived = lax.ppermute(moving[h], axis, routes[h])]
    ppermute x0 -> x70, starting transfers between devices: none -> 78 us  [the longest x28 30.6 us: ring_update(): arrived = lax.ppermute(moving[h], axis, routes[h])]
    ppermute x42 -> x14, waiting for transfers between devices: 77.9 us -> 25.7 us  [ring_sum(): current = lax.ppermute(current, axis, routes[h])]
    ppermute x42 -> x14, waiting for transfers between devices: 75.2 us -> 25.1 us  [ring_sum(): arrived = lax.ppermute(moving[h], axis, routes[h])]
    select_n x3, other arithmetic: 6.28 us -> 51 us  [gather_sector(): row = jnp.where(column == index, value, row)]
    ppermute x42 -> x14, starting transfers between devices: 45.2 us -> 14.9 us  [ring_sum(): arrived = lax.ppermute(moving[h], axis, routes[h])]
    ppermute x42 -> x14, starting transfers between devices: 43 us -> 14 us  [ring_sum(): current = lax.ppermute(current, axis, routes[h])]
  transfers between devices with their start and end apart: 85 -> 99, of which waited for: 59 -> 70; matrix products, arithmetic and copies ran while one was open for 0% -> 1% of each run, Pallas kernels for 0% -> 0%
where the time goes in v11:
time: 756 us; the launch traced here: 755 us
  waiting for transfers between devices  444 us (59%)
  starting transfers between devices  110 us (15%)
  matrix products  80.8 us (11%)
  other arithmetic  75.6 us (10%)
  between operations  23.4 us (3%)
  local copies, waits for them, and re-layouts  13.6 us (2%)
    ppermute x1, waiting for transfers between devices, from_behind(): return lax.ppermute(block, axis, route)  299 us
    dot_general x3, matrix products, on_device(): jnp.einsum('ckqad,ckqed->cqae', products, right_ops, preferred_element_ty...  59.6 us
    select_n x3, other arithmetic, gather_sector(): row = jnp.where(column == index, value, row)  51 us
    ppermute x28, waiting for transfers between devices, ring_update(): arrived = lax.ppermute(moving[h], axis, routes[h])  50.6 us
    ppermute x28, waiting for transfers between devices, ring_update(): current = lax.ppermute(current, axis, routes[h])  34 us
    ppermute x28, starting transfers between devices, ring_update(): arrived = lax.ppermute(moving[h], axis, routes[h])  30.6 us
    ppermute x28, starting transfers between devices, ring_update(): current = lax.ppermute(current, axis, routes[h])  28.6 us
    ppermute x14, waiting for transfers between devices, ring_sum(): current = lax.ppermute(current, axis, routes[h])  25.7 us
  transfers between devices with their start and end apart: 99, of which 70 were waited for; matrix products, arithmetic and copies ran while one was open for 1% of the time, Pallas kernels for 0%

profile of v11, /device:TPU:0, one launch (start us, length us, event | category | flops | bytes accessed | tf_op | source)
XLA Modules:
  0.0 754.8 jit_solution(1919278878300387549)
XLA Ops:
  1.9 21.2 %convert_bitcast_fusion = bf16[1,12,4,384,384]{3,4,1,2,0:T(8,128)(2,1)} fusion(bf16[1,4,384,384]{3,2,1,0:T(8,128)(2,1)S(1)} %copy-done, bf16[1,12,4,384,384]{4,3,2,1,0:T(8,128)(2,1)} %param.9), kind=kOutput, calls=%fused_computation.19 | convolution fusion | flops 10885791744 | bytes 29491200 | tf_op jit(solution)/shard_map/cqba,ckqbd->ckqad/dot_general | solution.py:155
  23.1 2.9 collective-permute-start
  31.7 298.7 %collective-permute-done = bf16[1,12,4,384,384]{3,4,1,2,0:T(8,128)(2,1)} collective-permute-done((bf16[1,12,4,384,384]{3,4,1,2,0:T(8,128)(2,1)}, bf16[1,12,4,384,384]{3,4,1,2,0:T(8,128)(2,1)}, u32[]{:S(2)}, u32[]{:S(2)}) %collective-permute-start) | collective-permute-done | bytes 14155808 | tf_op jit(solution)/shard_map/ppermute | solution.py:13
  330.4 20.1 %fusion.43 = f32[4,384,384]{2,1,0:T(8,128)} fusion(bf16[1,12,4,384,384]{3,4,1,2,0:T(8,128)(2,1)} %collective-permute-done, bf16[1,4,384,384]{3,2,1,0:T(8,128)(2,1)S(1)} %compare_select_fusion, bf16[1,12,4,384,384]{4,3,2,1,0:T(8,128)(2,1)} %param.10), kind=kOutput, calls=%fused_computation.28 | convolution fusion | flops 10878713856 | bytes 31850496 | tf_op jit(solution)/shard_map/ckqad,ckqed->cqae/dot_general | solution.py:169
  368.4 3.0 collective-permute-done.8
  373.7 4.0 collective-permute-done.9
  377.8 2.3 collective-permute-start.4
  380.1 3.9 collective-permute-done.10
  386.2 3.5 collective-permute-done.11
  391.9 3.0 collective-permute-done.12
  397.1 3.0 collective-permute-done.13
  400.8 4.5 collective-permute-done.14
  408.6 2.4 compare_select_fusion.90
  411.0 3.9 collective-permute-start.15
  415.7 3.4 collective-permute-start.18
  421.7 2.8 collective-permute-done.19
  428.7 24.8 %compare_select_fusion.92 = f32[40]{0:T(128)S(1)} fusion(f32[]{:T(128)} %bitcast.84, f32[]{:T(128)} %bitcast.83, f32[]{:T(128)} %bitcast.82, f32[]{:T(128)} %bitcast.81, f32[]{:T(128)} %bitcast.80, f32[]{:T(128)} %bitcast.79, f32[]{:T(128)} %bitcast.78, f32[]{:T(128)} %bitcast.77, f32[]{:T(128)} %bitcast.76, f32[]{:T(128)} %bitcast.75, f32[]{:T(128)} %bitcast.74, ...), kind=kLoop, calls=%fused_computation.290 | loop fusion | flops 3200 | bytes 320 | tf_op jit(solution)/shard_map/jit(_where)/select_n | solution.py:129
  453.7 2.5 psum.21
  459.7 2.1 collective-permute-start.29
  461.8 2.2 collective-permute-done.22
  466.1 2.2 collective-permute-done.23
  470.5 2.9 collective-permute-done.24
  473.4 2.1 collective-permute-start.32
  475.5 2.2 collective-permute-done.25
  479.8 2.2 collective-permute-done.26
  484.2 2.2 collective-permute-done.27
  488.5 2.2 collective-permute-done.28
  492.5 19.4 %fusion.50 = f32[4,384,384]{2,1,0:T(8,128)S(1)} fusion(bf16[4,384,384,1]{2,1,3,0:T(8,128)(2,1)} %bitcast.490, bf16[1,12,4,384,384]{3,4,1,2,0:T(8,128)(2,1)} %collective-permute-done, bf16[1,12,4,384,384]{4,3,2,1,0:T(8,128)(2,1)} %param.10), kind=kOutput, calls=%fused_computation.29 | convolution fusion | flops 10878713856 | bytes 31850496 | tf_op jit(solution)/shard_map/ckqad,ckqed->cqae/dot_general | solution.py:169
  514.3 4.5 collective-permute-done.36
  520.9 3.9 collective-permute-done.37
  527.0 3.1 collective-permute-done.38
  532.2 3.2 collective-permute-done.39
  537.6 3.0 collective-permute-done.40
  542.9 3.0 collective-permute-done.41
  548.1 3.0 collective-permute-done.42
  556.4 2.6 compare_select_fusion.89
  574.7 24.9 %compare_select_fusion.91 = f32[40]{0:T(128)S(1)} fusion(f32[]{:T(128)} %bitcast.169, f32[]{:T(128)} %bitcast.168, f32[]{:T(128)} %bitcast.167, f32[]{:T(128)} %bitcast.166, f32[]{:T(128)} %bitcast.165, f32[]{:T(128)} %bitcast.164, f32[]{:T(128)} %bitcast.163, f32[]{:T(128)} %bitcast.162, f32[]{:T(128)} %bitcast.161, f32[]{:T(128)} %bitcast.160, ...), kind=kLoop, calls=%fused_computation.289 | loop fusion | flops 3200 | bytes 320 | tf_op jit(solution)/shard_map/jit(_where)/select_n | solution.py:129
  599.8 2.5 psum.22
  606.0 2.1 collective-permute-start.64
  608.0 2.2 collective-permute-done.57
  612.4 2.2 collective-permute-done.58
  616.8 2.9 collective-permute-done.59
  619.7 2.1 collective-permute-start.67
  621.8 2.2 collective-permute-done.60
  626.2 2.2 collective-permute-done.61
  630.5 2.2 collective-permute-done.62
  634.9 2.2 collective-permute-done.63
  639.0 20.1 %fusion.57 = f32[4,384,384]{2,1,0:T(8,128)} fusion(bf16[4,384,384,1]{2,1,3,0:T(8,128)(2,1)S(1)} %bitcast.491, bf16[1,12,4,384,384]{3,4,1,2,0:T(8,128)(2,1)} %collective-permute-done, bf16[1,12,4,384,384]{4,3,2,1,0:T(8,128)(2,1)} %param.10), kind=kOutput, calls=%fused_computation.30 | convolution fusion | flops 10878713856 | bytes 31850496 | tf_op jit(solution)/shard_map/ckqad,ckqed->cqae/dot_general | solution.py:169
  664.4 3.3 collective-permute-done.71
  671.0 3.6 collective-permute-done.72
  677.0 2.9 collective-permute-done.73
  682.2 3.3 collective-permute-done.74
  687.8 4.3 collective-permute-done.75
  694.4 3.8 collective-permute-done.76
  700.4 3.1 collective-permute-done.77
  705.9 3.4 collective-permute-done.78
  711.6 4.2 collective-permute-done.79
  718.2 3.7 collective-permute-done.80
  724.1 3.0 collective-permute-done.81
  729.2 3.0 collective-permute-done.82
  734.4 3.0 collective-permute-done.83
  739.5 3.0 collective-permute-done.84
  743.8 2.8 multiply_reduce_fusion.1
  748.0 2.4 psum.23
  (358 shorter events, 135.1 us)
Async XLA Ops:
  23.1 307.3 %collective-permute-start = (bf16[1,12,4,384,384]{3,4,1,2,0:T(8,128)(2,1)}, bf16[1,12,4,384,384]{3,4,1,2,0:T(8,128)(2,1)}, u32[]{:S(2)}, u32[]{:S(2)}) collective-permute-start(bf16[1,12,4,384,384]{3,4,1,2,0:T(8,128)(2,1)} %convert_bitcast_fusion), channel_id=1, source_target_pairs={{16,0},{0,16},{17,1},{1,17},{18,2},{2,18},{19,3},{3,19},{20,4},{4,... | collective-permute-start | bytes 42467336 | tf_op jit(solution)/shard_map/ppermute | solution.py:13
  352.3 14.2 %collective-permute-start.1 = (f32[96,384]{1,0:T(8,128)S(1)}, f32[96,384]{1,0:T(8,128)S(1)}, u32[]{:S(2)}, u32[]{:S(2)}) collective-permute-start(f32[96,384]{1,0:T(8,128)S(1)} %dynamic-slice_bitcast_fusion.5), channel_id=1, source_target_pairs={{0,4},{4,8},{8,12},{12,14},{14,10},{10,6},{6,2},{2,0},{1,5},{5,9},... | collective-permute-start | bytes 442376 | tf_op jit(solution)/shard_map/ppermute | solution.py:86
  366.1 5.4 collective-permute-start.8
  366.6 5.2 collective-permute-start.2
  371.5 6.2 collective-permute-start.9
  371.8 6.0 collective-permute-start.3
  377.7 6.3 collective-permute-start.10
  377.8 6.7 collective-permute-start.4
  384.1 5.6 collective-permute-start.11
  384.5 5.9 collective-permute-start.5
  389.7 5.2 collective-permute-start.12
  390.4 5.2 collective-permute-start.6
  395.0 5.2 collective-permute-start.13
  395.6 5.2 collective-permute-start.7
  400.2 5.2 collective-permute-start.14
  411.0 8.2 %collective-permute-start.15 = (f32[5]{0:T(128)S(1)}, f32[5]{0:T(128)S(1)}, u32[]{:S(2)}, u32[]{:S(2)}) collective-permute-start(f32[5]{0:T(128)S(1)} %compare_select_fusion.90), channel_id=1, source_target_pairs={{0,14},{2,0},{4,2},{6,4},{8,6},{10,8},{12,10},{14,12},{1,15},{3,1}... | collective-permute-start | bytes 68 | tf_op jit(solution)/shard_map/ppermute | solution.py:102
  414.9 5.3 collective-permute-start.16
  415.3 6.4 collective-permute-start.17
  415.7 6.0 collective-permute-start.18
  419.2 5.3 collective-permute-start.19
  419.2 5.4 collective-permute-start.20
  420.2 6.2 collective-permute-start.21
  512.1 6.7 collective-permute-start.36
  514.0 6.4 collective-permute-start.43
  518.8 6.0 collective-permute-start.37
  520.5 5.6 collective-permute-start.44
  524.8 5.2 collective-permute-start.38
  526.1 5.2 collective-permute-start.45
  530.1 5.4 collective-permute-start.39
  531.3 5.9 collective-permute-start.46
  535.5 5.2 collective-permute-start.40
  537.2 5.2 collective-permute-start.47
  540.7 5.2 collective-permute-start.41
  542.5 5.2 collective-permute-start.48
  545.9 5.2 collective-permute-start.42
  547.7 5.2 collective-permute-start.49
  559.0 6.3 collective-permute-start.50
  560.6 5.6 collective-permute-start.51
  561.3 5.8 collective-permute-start.52
  563.8 5.3 collective-permute-start.54
  565.2 5.3 collective-permute-start.55
  566.2 6.2 collective-permute-start.56
  661.6 6.0 collective-permute-start.71
  664.1 6.6 collective-permute-start.85
  668.6 6.0 collective-permute-start.72
  670.7 5.9 collective-permute-start.86
  674.6 5.2 collective-permute-start.73
  676.6 5.2 collective-permute-start.87
  679.9 5.6 collective-permute-start.74
  681.8 5.3 collective-permute-start.88
  685.5 6.6 collective-permute-start.75
  687.2 6.7 collective-permute-start.89
  692.1 6.1 collective-permute-start.76
  693.9 5.9 collective-permute-start.90
  698.3 5.3 collective-permute-start.77
  699.8 5.3 collective-permute-start.91
  703.7 5.7 collective-permute-start.78
  705.2 6.0 collective-permute-start.92
  709.3 6.6 collective-permute-start.79
  711.2 6.4 collective-permute-start.93
  715.9 6.1 collective-permute-start.80
  717.6 5.6 collective-permute-start.94
  722.0 5.1 collective-permute-start.81
  723.2 5.1 collective-permute-start.95
  (61 other events, 3734.9 us)

commit v12 on v10

--- a/solution.py
+++ b/solution.py
@@ -94,13 +94,18 @@
 def on_device(psi, left_ops, right_ops, basis, block_dims):
     block_size = psi.shape[2]
     live = live_mask(block_dims, block_size)
-    half_env = jnp.einsum(
-        "ckqab,cqbd->ckqad", left_ops, basis, preferred_element_type=jnp.float32
-    ).astype(jnp.bfloat16)
-    boundary_ops = jnp.einsum(
-        "cqba,ckqbd->ckqad", basis, half_env, preferred_element_type=jnp.float32
-    ).astype(jnp.bfloat16)
-    shifted = from_behind(boundary_ops, "chain", 1)
+    sectors = psi.shape[1]
+    cut = sectors // 2 if sectors % 2 == 0 else sectors
+    spans = [slice(0, cut)] + ([slice(cut, sectors)] if cut < sectors else [])
+    shifted = []
+    for span in spans:
+        half_env = jnp.einsum(
+            "ckqab,cqbd->ckqad", left_ops[:, :, span], basis[:, span], preferred_element_type=jnp.float32
+        ).astype(jnp.bfloat16)
+        boundary_ops = jnp.einsum(
+            "cqba,ckqbd->ckqad", basis[:, span], half_env, preferred_element_type=jnp.float32
+        ).astype(jnp.bfloat16)
+        shifted.append(from_behind(boundary_ops, "chain", 1))
     vector = jnp.where(live > 0, psi, jnp.zeros_like(psi))
     entry_count = float(SECTORS * block_size * block_size)
     share_rows = block_size // lax.axis_size("ops")
@@ -108,12 +113,15 @@
     residual = None
     quotients = []
     for iteration in range(ITERS):
-        products = jnp.einsum(
-            "ckqab,cqbd->ckqad", shifted, vector, preferred_element_type=jnp.float32
-        ).astype(jnp.bfloat16)
-        partial_sigma = jnp.einsum(
-            "ckqad,ckqed->cqae", products, right_ops, preferred_element_type=jnp.float32
-        )
+        pieces = []
+        for span, moved in zip(spans, shifted):
+            products = jnp.einsum(
+                "ckqab,cqbd->ckqad", moved, vector[:, span], preferred_element_type=jnp.float32
+            ).astype(jnp.bfloat16)
+            pieces.append(jnp.einsum(
+                "ckqad,ckqed->cqae", products, right_ops[:, :, span], preferred_element_type=jnp.float32
+            ))
+        partial_sigma = jnp.concatenate(pieces, axis=1)
         sigma_full = ring_sum(partial_sigma, "ops") * live
         vector_wide = vector.astype(jnp.float32)
         if iteration + 1 < ITERS:

time: 696 us -> 693 us (level); the launches traced: 695 us -> 685 us
  waiting for transfers between devices: 456 us -> 398 us
  local copies, waits for them, and re-layouts: 8.93 us -> 32.6 us
  matrix products: 81.3 us -> 91.1 us
  other arithmetic: 26.9 us -> 35.8 us
    ppermute x1 -> x2, waiting for transfers between devices: 303 us -> 253 us  [from_behind(): return lax.ppermute(block, axis, route)]
    slice x3 -> x2, local copies, waits for them, and re-layouts: 3.75 us -> 20.7 us  [the longest x1 10.4 us: on_device(): right_ops[:, :, span]]
    dot_general x4 -> x8, matrix products: 81.3 us -> 91.1 us  [the longest x6 66.7 us: on_device(): jnp.einsum('ckqad,ckqed->cqae', products, right_ops[:, :, span], preferre...]
  transfers between devices with their start and end apart: 85 -> 86, of which waited for: 59 -> 76; matrix products, arithmetic and copies ran while one was open for 0% -> 11% of each run, Pallas kernels for 0% -> 0%
where the time goes in v12:
time: 693 us; the launch traced here: 685 us
  waiting for transfers between devices  398 us (57%)
  starting transfers between devices  95.8 us (14%)
  matrix products  91.1 us (13%)
  other arithmetic  35.8 us (5%)
  local copies, waits for them, and re-layouts  32.6 us (5%)
  between operations  23.8 us (3%)
  blocking collectives  7.33 us (1%)
    ppermute x2, waiting for transfers between devices, from_behind(): return lax.ppermute(block, axis, route)  253 us
    ppermute x42, waiting for transfers between devices, ring_sum(): current = lax.ppermute(current, axis, routes[h])  75.7 us
    ppermute x42, waiting for transfers between devices, ring_sum(): arrived = lax.ppermute(moving[h], axis, routes[h])  69.7 us
    dot_general x6, matrix products, on_device(): jnp.einsum('ckqad,ckqed->cqae', products, right_ops[:, :, span], preferre...  66.7 us
    ppermute x42, starting transfers between devices, ring_sum(): arrived = lax.ppermute(moving[h], axis, routes[h])  48.9 us
    ppermute x42, starting transfers between devices, ring_sum(): current = lax.ppermute(current, axis, routes[h])  44 us
    dot_general x2, matrix products, on_device(): jnp.einsum('cqba,ckqbd->ckqad', basis[:, span], half_env, preferred_eleme...  24.5 us
  transfers between devices with their start and end apart: 86, of which 76 were waited for; matrix products, arithmetic and copies ran while one was open for 11% of the time, Pallas kernels for 0%

profile of v12, /device:TPU:0, one launch (start us, length us, event | category | flops | bytes accessed | tf_op | source)
XLA Modules:
  0.0 684.5 jit_solution(4756697491889670697)
XLA Ops:
  0.6 10.4 %fusion.92 = (bf16[1,12,2,384,384]{4,3,2,1,0:T(8,128)(2,1)}, bf16[1,12,2,384,384]{4,3,2,1,0:T(8,128)(2,1)}) fusion(bf16[1,12,4,384,384]{4,3,2,1,0:T(8,128)(2,1)} %param.9), kind=kLoop, calls=%fused_computation.215 | loop fusion | bytes 28311552 | tf_op jit(solution)/shard_map/slice | solution.py:103
  11.0 12.2 %convert_bitcast_fusion.1 = bf16[1,12,2,384,384]{3,4,1,2,0:T(8,128)(2,1)} fusion(bf16[1,12,2,384,384]{4,3,2,1,0:T(8,128)(2,1)} %get-tuple-element.39, bf16[1,4,384,384]{3,2,1,0:T(8,128)(2,1)S(1)} %copy-done.6), kind=kOutput, calls=%fused_computation.42 | convolution fusion | flops 5442895872 | bytes 15335424 | tf_op jit(solution)/shard_map/cqba,ckqbd->ckqad/dot_general | solution.py:105
  23.2 2.9 collective-permute-start
  26.2 12.2 %convert_bitcast_fusion = bf16[1,12,2,384,384]{3,4,1,2,0:T(8,128)(2,1)} fusion(bf16[1,12,2,384,384]{4,3,2,1,0:T(8,128)(2,1)} %get-tuple-element.40, bf16[1,4,384,384]{3,2,1,0:T(8,128)(2,1)S(1)} %copy-done.6), kind=kOutput, calls=%fused_computation.39 | convolution fusion | flops 5442895872 | bytes 15335424 | tf_op jit(solution)/shard_map/cqba,ckqbd->ckqad/dot_general | solution.py:105
  53.1 10.4 %fusion.93 = (bf16[1,12,2,384,384]{4,3,2,1,0:T(8,128)(2,1)}, bf16[1,12,2,384,384]{4,3,2,1,0:T(8,128)(2,1)}) fusion(bf16[1,12,4,384,384]{4,3,2,1,0:T(8,128)(2,1)} %param.10), kind=kLoop, calls=%fused_computation.216 | loop fusion | bytes 28311552 | tf_op jit(solution)/shard_map/slice | solution.py:122
  63.5 116.2 %collective-permute-done = bf16[1,12,2,384,384]{3,4,1,2,0:T(8,128)(2,1)} collective-permute-done((bf16[1,12,2,384,384]{3,4,1,2,0:T(8,128)(2,1)}, bf16[1,12,2,384,384]{3,4,1,2,0:T(8,128)(2,1)}, u32[]{:S(2)}, u32[]{:S(2)}) %collective-permute-start) | collective-permute-done | bytes 7077920 | tf_op jit(solution)/shard_map/ppermute | solution.py:13
  179.7 11.4 %fusion.14 = f32[2,384,384,1]{2,1,3,0:T(8,128)S(1)} fusion(bf16[1,12,2,384,384]{4,3,2,1,0:T(8,128)(2,1)} %get-tuple-element.41, bf16[1,12,2,384,384]{3,4,1,2,0:T(8,128)(2,1)} %collective-permute-done, bf16[1,4,384,384]{2,3,1,0:T(8,128)(2,1)S(1)} %fusion.81), kind=kOutput, calls=%fused_computation.18 | convolution fusion | flops 5439356928 | bytes 15925248 | tf_op jit(solution)/shard_map/ckqad,ckqed->cqae/dot_general | solution.py:121
  191.9 2.1 collective-permute-start.1
  194.0 136.5 %collective-permute-done.15 = bf16[1,12,2,384,384]{3,4,1,2,0:T(8,128)(2,1)} collective-permute-done((bf16[1,12,2,384,384]{3,4,1,2,0:T(8,128)(2,1)}, bf16[1,12,2,384,384]{3,4,1,2,0:T(8,128)(2,1)}, u32[]{:S(2)}, u32[]{:S(2)}) %collective-permute-start.15) | collective-permute-done | bytes 7077920 | tf_op jit(solution)/shard_map/ppermute | solution.py:13
  330.5 11.0 %fusion.10 = f32[2,384,384,1]{2,1,3,0:T(8,128)S(1)} fusion(bf16[1,12,2,384,384]{4,3,2,1,0:T(8,128)(2,1)} %get-tuple-element.42, bf16[1,12,2,384,384]{3,4,1,2,0:T(8,128)(2,1)} %collective-permute-done.15, bf16[1,4,384,384]{2,3,1,0:T(8,128)(2,1)S(1)} %fusion.81), kind=kOutput, calls=%fused_computation.14 | convolution fusion | flops 5439356928 | bytes 15925248 | tf_op jit(solution)/shard_map/ckqad,ckqed->cqae/dot_general | solution.py:121
  352.0 2.2 collective-permute-start.18
  355.6 3.4 collective-permute-done.18
  362.3 2.9 collective-permute-done.19
  379.3 2.1 collective-permute-done.22
  385.2 3.3 collective-permute-done.23
  391.6 2.5 collective-permute-done.24
  402.3 2.5 collective-permute-done.26
  407.4 2.5 collective-permute-done.27
  412.6 3.0 collective-permute-done.28
  417.3 3.4 collective-permute-done.29
  422.4 2.2 copy.70
  430.4 2.5 compare_select_fusion.11
  433.1 2.4 psum.21
  440.6 11.2 %fusion.8 = f32[2,384,384,1]{2,1,3,0:T(8,128)S(1)} fusion(bf16[1,12,2,384,384]{4,3,2,1,0:T(8,128)(2,1)} %get-tuple-element.41, bf16[1,12,2,384,384]{3,4,1,2,0:T(8,128)(2,1)} %collective-permute-done, bf16[1,4,384,384]{2,3,1,0:T(8,128)(2,1)} %fusion.73), kind=kOutput, calls=%fused_computation.12 | convolution fusion | flops 5439356928 | bytes 15925248 | tf_op jit(solution)/shard_map/ckqad,ckqed->cqae/dot_general | solution.py:121
  454.5 11.0 %fusion.6 = f32[2,384,384,1]{2,1,3,0:T(8,128)S(1)} fusion(bf16[1,12,2,384,384]{4,3,2,1,0:T(8,128)(2,1)} %get-tuple-element.42, bf16[1,12,2,384,384]{3,4,1,2,0:T(8,128)(2,1)} %collective-permute-done.15, bf16[1,4,384,384]{2,3,1,0:T(8,128)(2,1)S(1)} %copy-done), kind=kOutput, calls=%fused_computation.10 | convolution fusion | flops 5439356928 | bytes 15925248 | tf_op jit(solution)/shard_map/ckqad,ckqed->cqae/dot_general | solution.py:121
  468.6 2.9 collective-permute-done.44
  474.3 2.4 collective-permute-done.45
  479.5 2.6 collective-permute-done.46
  482.7 2.4 collective-permute-start.34
  485.0 3.9 collective-permute-done.47
  489.1 2.5 collective-permute-start.35
  491.7 3.3 collective-permute-done.48
  495.3 2.3 collective-permute-start.36
  497.6 2.7 collective-permute-done.49
  502.9 2.8 collective-permute-done.50
  508.1 4.2 collective-permute-done.51
  514.5 4.1 collective-permute-done.52
  520.7 3.4 collective-permute-done.53
  526.3 3.0 collective-permute-done.54
  531.4 3.0 collective-permute-done.55
  536.5 3.0 collective-permute-done.56
  540.4 4.4 collective-permute-done.57
  553.8 2.5 compare_select_fusion.10
  556.4 2.4 psum.22
  562.1 2.4 fusion.90
  564.5 11.2 %fusion.4 = f32[2,384,384,1]{2,1,3,0:T(8,128)S(1)} fusion(bf16[1,12,2,384,384]{4,3,2,1,0:T(8,128)(2,1)} %get-tuple-element.41, bf16[1,12,2,384,384]{3,4,1,2,0:T(8,128)(2,1)} %collective-permute-done, bf16[1,4,384,384]{2,3,1,0:T(8,128)(2,1)} %get-tuple-element.30), kind=kOutput, calls=%fused_computation.8 | convolution fusion | flops 5439356928 | bytes 15925248 | tf_op jit(solution)/shard_map/ckqad,ckqed->cqae/dot_general | solution.py:121
  578.3 11.0 %fusion.2 = f32[2,384,384,1]{2,1,3,0:T(8,128)S(1)} fusion(bf16[1,12,2,384,384]{4,3,2,1,0:T(8,128)(2,1)} %get-tuple-element.42, bf16[1,12,2,384,384]{3,4,1,2,0:T(8,128)(2,1)} %collective-permute-done.15, bf16[1,4,384,384]{2,3,1,0:T(8,128)(2,1)S(1)} %copy-done.1), kind=kOutput, calls=%fused_computation.6 | convolution fusion | flops 5439356928 | bytes 15925248 | tf_op jit(solution)/shard_map/ckqad,ckqed->cqae/dot_general | solution.py:121
  592.3 2.6 collective-permute-done.72
  597.8 2.4 collective-permute-done.73
  603.0 3.0 collective-permute-done.74
  608.9 3.8 collective-permute-done.75
  615.5 3.3 collective-permute-done.76
  621.2 2.8 collective-permute-done.77
  626.5 2.9 collective-permute-done.78
  632.1 4.1 collective-permute-done.79
  638.8 3.4 collective-permute-done.80
  644.6 2.7 collective-permute-done.81
  649.8 3.0 collective-permute-done.82
  654.9 3.0 collective-permute-done.83
  660.1 3.0 collective-permute-done.84
  663.4 4.7 collective-permute-done.85
  671.8 2.5 multiply_reduce_fusion.1
  675.7 2.4 psum.23
  680.0 2.5 multiply_subtract_fusion
  (265 shorter events, 143.6 us)
Async XLA Ops:
  23.2 156.4 %collective-permute-start = (bf16[1,12,2,384,384]{3,4,1,2,0:T(8,128)(2,1)}, bf16[1,12,2,384,384]{3,4,1,2,0:T(8,128)(2,1)}, u32[]{:S(2)}, u32[]{:S(2)}) collective-permute-start(bf16[1,12,2,384,384]{3,4,1,2,0:T(8,128)(2,1)} %convert_bitcast_fusion.1), channel_id=1, source_target_pairs={{16,0},{0,16},{17,1},{1,17},{18,2},{2,18},{19,3},{3,19},{20,4},{4,... | collective-permute-start | bytes 21233672 | tf_op jit(solution)/shard_map/ppermute | solution.py:13
  38.4 292.1 %collective-permute-start.15 = (bf16[1,12,2,384,384]{3,4,1,2,0:T(8,128)(2,1)}, bf16[1,12,2,384,384]{3,4,1,2,0:T(8,128)(2,1)}, u32[]{:S(2)}, u32[]{:S(2)}) collective-permute-start(bf16[1,12,2,384,384]{3,4,1,2,0:T(8,128)(2,1)} %convert_bitcast_fusion), channel_id=1, source_target_pairs={{16,0},{0,16},{17,1},{1,17},{18,2},{2,18},{19,3},{3,19},{20,4},{4,... | collective-permute-start | bytes 21233672 | tf_op jit(solution)/shard_map/ppermute | solution.py:13
  191.9 151.5 %collective-permute-start.1 = (f32[96,384]{1,0:T(8,128)}, f32[96,384]{1,0:T(8,128)}, u32[]{:S(2)}, u32[]{:S(2)}) collective-permute-start(f32[96,384]{1,0:T(8,128)} %dynamic-slice_bitcast_fusion.5), channel_id=1, source_target_pairs={{0,4},{4,8},{8,12},{12,14},{14,10},{10,6},{6,2},{2,0},{1,5},{5,9},... | collective-permute-start | bytes 442376 | tf_op jit(solution)/shard_map/ppermute | solution.py:53
  341.5 5.2 collective-permute-start.16
  344.4 5.2 collective-permute-start.2
  346.8 5.2 collective-permute-start.17
  349.6 5.9 collective-permute-start.3
  352.0 7.0 %collective-permute-start.18 = (f32[96,384]{1,0:T(8,128)S(1)}, f32[96,384]{1,0:T(8,128)S(1)}, u32[]{:S(2)}, u32[]{:S(2)}) collective-permute-start(f32[96,384]{1,0:T(8,128)S(1)} %bitcast_add_fusion.33), channel_id=1, source_target_pairs={{0,2},{4,0},{8,4},{12,8},{14,12},{10,14},{6,10},{2,6},{1,3},{5,1},... | collective-permute-start | bytes 442376 | tf_op jit(solution)/shard_map/ppermute | solution.py:53
  355.5 6.7 collective-permute-start.4
  359.0 6.2 collective-permute-start.19
  362.2 5.9 collective-permute-start.5
  365.2 5.3 collective-permute-start.20
  368.2 5.2 collective-permute-start.6
  370.5 5.2 collective-permute-start.21
  373.4 5.3 collective-permute-start.7
  375.8 5.7 collective-permute-start.22
  378.8 6.4 collective-permute-start.8
  381.5 7.0 %collective-permute-start.23 = (f32[96,384]{1,0:T(8,128)S(1)}, f32[96,384]{1,0:T(8,128)S(1)}, u32[]{:S(2)}, u32[]{:S(2)}) collective-permute-start(f32[96,384]{1,0:T(8,128)S(1)} %get-tuple-element.38), channel_id=1, source_target_pairs={{0,2},{4,0},{8,4},{12,8},{14,12},{10,14},{6,10},{2,6},{1,3},{5,1},... | collective-permute-start | bytes 442376 | tf_op jit(solution)/shard_map/ppermute | solution.py:61
  385.2 6.0 collective-permute-start.9
  388.6 5.5 collective-permute-start.24
  391.2 5.6 collective-permute-start.10
  399.2 5.6 collective-permute-start.26
  410.0 5.6 collective-permute-start.28
  452.5 13.1 %collective-permute-start.30 = (f32[96,384]{1,0:T(8,128)}, f32[96,384]{1,0:T(8,128)}, u32[]{:S(2)}, u32[]{:S(2)}) collective-permute-start(f32[96,384]{1,0:T(8,128)} %dynamic-slice_bitcast_fusion.3), channel_id=1, source_target_pairs={{0,4},{4,8},{8,12},{12,14},{14,10},{10,6},{6,2},{2,0},{1,5},{5,9},... | collective-permute-start | bytes 442376 | tf_op jit(solution)/shard_map/ppermute | solution.py:53
  465.5 6.0 collective-permute-start.44
  466.5 5.7 collective-permute-start.31
  471.5 5.2 collective-permute-start.45
  472.2 5.2 collective-permute-start.32
  476.7 5.4 collective-permute-start.46
  477.5 5.2 collective-permute-start.33
  482.2 6.7 collective-permute-start.47
  482.7 6.5 collective-permute-start.34
  489.0 6.0 collective-permute-start.48
  489.1 6.1 collective-permute-start.35
  495.0 5.4 collective-permute-start.49
  495.3 6.1 collective-permute-start.36
  500.3 5.4 collective-permute-start.50
  501.5 5.2 collective-permute-start.37
  505.9 6.4 collective-permute-start.51
  506.7 5.7 collective-permute-start.38
  512.3 6.3 collective-permute-start.52
  512.4 6.7 collective-permute-start.39
  518.6 5.6 collective-permute-start.53
  519.0 5.8 collective-permute-start.40
  524.8 5.2 collective-permute-start.41
  576.4 13.3 %collective-permute-start.58 = (f32[96,384]{1,0:T(8,128)}, f32[96,384]{1,0:T(8,128)}, u32[]{:S(2)}, u32[]{:S(2)}) collective-permute-start(f32[96,384]{1,0:T(8,128)} %dynamic-slice_bitcast_fusion.1), channel_id=1, source_target_pairs={{0,4},{4,8},{8,12},{12,14},{14,10},{10,6},{6,2},{2,0},{1,5},{5,9},... | collective-permute-start | bytes 442376 | tf_op jit(solution)/shard_map/ppermute | solution.py:53
  589.3 5.7 collective-permute-start.72
  590.6 5.4 collective-permute-start.59
  600.2 5.8 collective-permute-start.74
  601.3 5.9 collective-permute-start.61
  606.0 6.7 collective-permute-start.75
  607.2 6.5 collective-permute-start.62
  612.7 6.1 collective-permute-start.76
  613.7 5.7 collective-permute-start.63
  618.8 5.2 collective-permute-start.77
  624.0 5.4 collective-permute-start.78
  624.8 5.3 collective-permute-start.65
  629.5 6.7 collective-permute-start.79
  630.1 6.6 collective-permute-start.66
  636.2 6.0 collective-permute-start.80
  636.6 5.9 collective-permute-start.67
  647.3 5.4 collective-permute-start.82
  647.7 5.4 collective-permute-start.69
  653.1 5.2 collective-permute-start.70
  (30 other events, 337.5 us)
